TPU v7x, 512 devices: a whole 4x4x16 slice. The times are simulated.
512 devices in a mesh: seq: 64 (over z, x), tp: 8 (over y, core).
Axes of the slice: x: 4, y: 4, z: 16, core: 2. Of those that a mesh axis runs over, the one named last changes fastest.
Arguments:
- mamba_x: bfloat16 [4096, 8192], P('seq', 'tp'), may hold values from -6 to 6
- gate_z: bfloat16 [4096, 8192], P('seq', 'tp'), may hold values from -6 to 6
- b_in: bfloat16 [4096, 1024], P('seq', 'tp'), may hold values from -1.25 to 1.25
- c_in: bfloat16 [4096, 1024], P('seq', 'tp'), may hold values from -1.25 to 1.25
- dt_raw: float32 [128, 4096], P('tp', 'seq'), may hold values from -2 to 24576
- a_log: float32 [128], P('tp'), may hold values from -14 to -3
- skip_d: float32 [128], P('tp'), may hold values from 0.5 to 1.5
- norm_gain: float32 [8192], P('tp'), may hold values from 0.5 to 1.5
- value_weight: bfloat16 [8192, 1024], P('tp'), may hold values from -0.09375 to 0.09375
- queries: bfloat16 [4096, 4096], P('seq', 'tp'), may hold values from -18 to 18
- keys: bfloat16 [4096, 1024], P('seq', 'tp'), may hold values from -4.5 to 4.5
Outputs:
- mamba_out: bfloat16 [4096, 8192], P('seq', 'tp')
- attention: bfloat16 [4096, 4096], P('seq', 'tp')
All inputs are finite; a program needn't handle non-finite values.
Results may differ from a plain program's by a relative error of at most 0.02.
Values may be sent and summed in bfloat16 or wider, within the bound.
No kernel may reach another device: no remote copies, remote signals or barrier semaphores. Data moves between devices by JAX's collectives and lax.ppermute only.
A program may use at most 128 MiB of HBM per device.

v0:
```python
import math

import jax
import jax.numpy as jnp
from jax import lax
from jax.sharding import PartitionSpec as P

MHEAD_DIM = 64
STATE = 128
QHEADS = 32
KVHEADS = 8
HEAD_DIM = 128


highest = lax.Precision.HIGHEST
norm_eps = 1e-05


def carried_in(part, axis, combine, identity):
    place = lax.axis_index(axis)
    gathered = jax.tree.map(lambda a: lax.all_gather(a, axis), part)
    state = jax.tree.map(lambda a, e: jnp.zeros_like(a) + jnp.asarray(e, a.dtype), part, identity)

    def one(lap, state):
        return combine(
            state, jax.tree.map(lambda a: lax.dynamic_index_in_dim(a, lap, 0, False), gathered)
        )

    return lax.fori_loop(0, place, one, state)


def block_scan(inputs, b_group, c_group, time_step, decay_rate):
    token_count = inputs.shape[0]
    log_decay = jnp.cumsum(-time_step * decay_rate[..., None], axis=2)
    log_gaps = log_decay[..., :, None] - log_decay[..., None, :]
    causal = jnp.arange(token_count)[:, None] >= jnp.arange(token_count)[None, :]
    decay_mat = jnp.exp(jnp.where(causal, log_gaps, -jnp.inf))
    cross_terms = jnp.einsum("tgn,sgn->gts", c_group, b_group, precision=highest)
    mixing = cross_terms[:, None] * decay_mat * time_step[:, :, None, :]
    local_out = jnp.einsum("gkts,sgkp->tgkp", mixing, inputs, precision=highest)
    tail_weight = jnp.exp(log_decay[..., -1:] - log_decay) * time_step
    summary = jnp.einsum("gks,sgkp,sgn->gkpn", tail_weight, inputs, b_group, precision=highest)
    return (log_decay, local_out, summary, jnp.exp(log_decay[..., -1]))


def carried_out(c_group, state_in, log_decay):
    carried_term = jnp.einsum("tgn,gkpn->tgkp", c_group, state_in, precision=highest)
    return carried_term * jnp.transpose(jnp.exp(log_decay), (2, 0, 1))[..., None]


def gated_norm(ssm_out, gate_z, norm_gain, group_count):
    token_count = ssm_out.shape[0]
    gated = ssm_out * jax.nn.silu(gate_z.astype(jnp.float32))
    grouped = gated.reshape(token_count, group_count, -1)
    inverse = lax.rsqrt(jnp.mean(grouped * grouped, axis=2, keepdims=True) + norm_eps)
    return ((grouped * inverse).reshape(token_count, -1) * norm_gain).astype(jnp.bfloat16)


def chain_combine(earlier, latter):
    return (earlier[0] * latter[0], latter[0][..., None, None] * earlier[1] + latter[1])


def query_layout(payload, kv_here, per_kv):
    count_rows = payload.shape[0]
    shaped = payload.reshape(count_rows, kv_here, per_kv, HEAD_DIM)
    return jnp.transpose(shaped, (1, 2, 0, 3)).reshape(kv_here, per_kv * count_rows, HEAD_DIM)


def row_positions(first_pos, count_rows, per_kv):
    return jnp.tile(first_pos + jnp.arange(count_rows, dtype=jnp.int32), per_kv)


def set_output(finished_set, kv_here, per_kv):
    running_max, running_sum, running_out = finished_set
    count_rows = running_sum.shape[1] // per_kv
    result = (running_out / running_sum[..., None]).astype(jnp.bfloat16)
    result = result.reshape(kv_here, per_kv, count_rows, HEAD_DIM)
    return jnp.transpose(result, (2, 0, 1, 3)).reshape(count_rows, kv_here * per_kv * HEAD_DIM)


def attend(running, query_set, key_slab, value_slab, key_first):
    query_block, query_pos = query_set
    score_scale = 1.0 / math.sqrt(HEAD_DIM)
    key_pos = key_first + jnp.arange(key_slab.shape[1], dtype=jnp.int32)

    def update(current):
        running_max, running_sum, running_out = current
        scores = (
            jnp.einsum("hrd,hcd->hrc", query_block, key_slab, preferred_element_type=jnp.float32)
            * score_scale
        )
        allowed = key_pos[None, :] <= query_pos[:, None]
        scores = jnp.where(allowed[None], scores, -jnp.inf)
        new_max = jnp.maximum(running_max, jnp.max(scores, axis=2))
        weights = jnp.exp(scores - new_max[..., None])
        shrink = jnp.exp(running_max - new_max)
        new_sum = running_sum * shrink + jnp.sum(weights, axis=2)
        new_out = running_out * shrink[..., None] + jnp.einsum(
            "hrc,hcd->hrd",
            weights.astype(jnp.bfloat16),
            value_slab,
            preferred_element_type=jnp.float32,
        )
        return (new_max, new_sum, new_out)

    def unchanged(current):
        return current

    return lax.cond(key_first <= jnp.max(query_pos), update, unchanged, running)


def per_device(
    mamba_x, gate_z, b_in, c_in, dt_raw, a_log, skip_d, norm_gain, value_weight, queries, keys
):
    tokens_here = mamba_x.shape[0]
    group_count = b_in.shape[1] // STATE
    head_count = dt_raw.shape[0]
    per_group = head_count // group_count
    inputs = mamba_x.astype(jnp.float32).reshape(tokens_here, group_count, per_group, MHEAD_DIM)
    b_group = b_in.astype(jnp.float32).reshape(tokens_here, group_count, STATE)
    c_group = c_in.astype(jnp.float32).reshape(tokens_here, group_count, STATE)
    time_step = jax.nn.softplus(dt_raw).reshape(group_count, per_group, tokens_here)
    decay_rate = jnp.exp(a_log).reshape(group_count, per_group)
    log_decay, local_out, summary, totals = block_scan(
        inputs, b_group, c_group, time_step, decay_rate
    )
    _, state_in = carried_in(
        (totals, summary), "seq", chain_combine, (jnp.ones_like(totals), jnp.zeros_like(summary))
    )
    skip_heads = skip_d.reshape(group_count, per_group)[None, :, :, None]
    ssm_out = local_out + carried_out(c_group, state_in, log_decay) + skip_heads * inputs
    mamba_out = gated_norm(ssm_out.reshape(tokens_here, -1), gate_z, norm_gain, group_count)
    kv_here = keys.shape[1] // HEAD_DIM
    per_kv = QHEADS // KVHEADS
    product = jnp.dot(mamba_out, value_weight, preferred_element_type=jnp.float32)
    values = lax.psum_scatter(
        jnp.transpose(
            product.reshape(tokens_here, lax.axis_size("tp") * kv_here, HEAD_DIM), (1, 0, 2)
        ).astype(jnp.bfloat16),
        "tp",
        scatter_dimension=0,
        tiled=True,
    )
    key_heads = jnp.transpose(keys.reshape(tokens_here, kv_here, HEAD_DIM), (1, 0, 2))
    my_index = lax.axis_index("seq")
    query_sets = [
        (
            query_layout(queries, kv_here, per_kv),
            row_positions(my_index * tokens_here, tokens_here, per_kv),
        )
    ]
    initial = tuple(
        (
            (
                jnp.full((kv_here, query_set[0].shape[1]), -jnp.inf, jnp.float32),
                jnp.zeros((kv_here, query_set[0].shape[1]), jnp.float32),
                jnp.zeros((kv_here, query_set[0].shape[1], HEAD_DIM), jnp.float32),
            )
            for query_set in query_sets
        )
    )
    key_portion = lax.all_gather(key_heads, "seq", axis=1, tiled=True)
    value_portion = lax.all_gather(values, "seq", axis=1, tiled=True)
    length = key_portion.shape[1]
    block_len = length
    for multiple in (1, 2, 4):
        block_len = multiple * tokens_here

    def one_block(block_index, current):
        offset = block_index * block_len
        key_slab = lax.dynamic_slice_in_dim(key_portion, offset, block_len, 1)
        value_slab = lax.dynamic_slice_in_dim(value_portion, offset, block_len, 1)
        return tuple(
            (
                attend(current[set_index], query_sets[set_index], key_slab, value_slab, offset)
                for set_index in range(len(query_sets))
            )
        )

    finished = lax.fori_loop(0, length // block_len, one_block, initial)
    outputs = [set_output(finished_set, kv_here, per_kv) for finished_set in finished]
    attention = outputs[0]
    return (mamba_out, attention)


def solution(mesh):
    placed = (
        P("seq", "tp"),
        P("seq", "tp"),
        P("seq", "tp"),
        P("seq", "tp"),
        P("tp", "seq"),
        P("tp"),
        P("tp"),
        P("tp"),
        P("tp", None),
        P("seq", "tp"),
        P("seq", "tp"),
    )
    return jax.shard_map(
        per_device,
        mesh=mesh,
        in_specs=placed,
        out_specs=(P("seq", "tp"), P("seq", "tp")),
        check_vma=False,
    )
```

profile of v0, /device:TPU:480, one launch (start us, length us, event | category | flops | bytes accessed | tf_op | source)
XLA Modules:
  0.0 750.5 jit_solution(6143692668134072282)
XLA Ops:
  13.3 2.9 copy.71
  16.2 72.4 %all-gather = f32[64,16,1]{1,2,0:T(1,128)S(1)} all-gather(f32[1,16,1]{1,2,0:T(1,128)S(1)} %exp.63), channel_id=2, replica_groups=mesh['seq'=64,'tp'=8] {'seq'}, dimensions={0}, use_global_device_ids=true | all-gather | bytes 4160 | tf_op jit(solution)/shard_map/all_gather | solution.py:21
  90.2 212.9 %all-gather.9.cloned.1.call-done = f32[1024,64,128]{2,1,0:T(8,128)} async-done(((f32[16,64,128]{2,1,0:T(8,128)}), f32[1024,64,128]{2,1,0:T(8,128)}) %all-gather.9.cloned.1.call-update) | async-done | bytes 33554448 | tf_op jit(solution)/shard_map/all_gather | solution.py:21
  303.2 74.1 %while.32 = (s32[]{:T(128)}, f32[1,16,64,128]{3,2,1,0:T(8,128)S(1)}, s32[]{:T(128)}, f32[64,1,16]{2,1,0:T(1,128)S(1)}, f32[64,1,16,64,128]{4,3,2,1,0:T(8,128)}, /*index=5*/s32[]{:T(128)}, s32[]{:T(128)}, s32[]{:T(128)}) while((s32[]{:T(128)}, f32[1,16,64,128]{3,2,1,0:T(8,128)S(1)}, s32[]{:T(128)}, f32[64,1,16]{2,1,0:T(1,128)S(1)}, ...), condition=%wide.region_2.3_spmd, body=%wide.region_1.2_spmd.sunk | while | flops 262149 | bytes 1573183 | solution.py:29
  382.4 33.4 %reduce-scatter.2.cloned.1.call-done = bf16[1,64,128]{2,1,0:T(8,128)(2,1)} async-done(((bf16[8,64,128]{2,1,0:T(8,128)(2,1)}), bf16[1,64,128]{2,1,0:T(8,128)(2,1)}) %reduce-scatter.2.cloned.1.call-update) | async-done | bytes 16400 | tf_op jit(solution)/shard_map/reduce_scatter | solution.py:136
  416.7 138.2 %all-gather.11.cloned.1.call-done = bf16[4096,128]{1,0:T(8,128)(2,1)} async-done(((bf16[64,128]{1,0:T(8,128)(2,1)}), bf16[4096,128]{1,0:T(8,128)(2,1)}) %all-gather.11.cloned.1.call-update) | async-done | bytes 1048592 | tf_op jit(solution)/shard_map/all_gather | solution.py:162
  554.8 138.3 %all-gather.7.cloned.1.call-done = bf16[1,4096,128]{2,1,0:T(8,128)(2,1)} async-done(((bf16[1,64,128]{2,1,0:T(8,128)(2,1)}), bf16[1,4096,128]{2,1,0:T(8,128)(2,1)}) %all-gather.7.cloned.1.call-update) | async-done | bytes 1048592 | tf_op jit(solution)/shard_map/all_gather | solution.py:163
  693.1 50.0 %while.33 = (s32[]{:T(128)}, f32[1,256]{1,0:T(1,128)S(1)}, f32[1,256]{1,0:T(1,128)S(1)}, f32[1,256,128]{2,1,0:T(8,128)S(1)}, s32[]{:T(128)}, /*index=5*/bf16[1,4...) while((s32[]{:T(128)}, f32[1,256]{1,0:T(1,128)S(1)}, ...), condition=%wide.region_11.12_spmd.clone, body=%wide.region_6.11_spmd.clone.sunk | while | flops 34145032 | bytes 1270325 | solution.py:180
  693.8 2.4 conditional.3
  697.0 2.4 conditional.3
  700.1 2.4 conditional.3
  703.2 2.4 conditional.3
  706.3 2.4 conditional.3
  709.5 2.4 conditional.3
  712.6 2.4 conditional.3
  715.7 2.4 conditional.3
  718.8 2.4 conditional.3
  721.9 2.4 conditional.3
  725.1 2.4 conditional.3
  728.2 2.4 conditional.3
  731.3 2.4 conditional.3
  734.4 2.4 conditional.3
  737.6 2.4 conditional.3
  740.7 2.4 conditional.3
  (334 shorter events, 123.7 us)
Async XLA Ops:
  7.2 3.7 copy-start
  7.2 295.9 %all-gather.9.cloned.1.call-start = ((), (), s32[]{:S(2)}) async-start(), calls=%async_computation.3 | async-start | bytes 34078720 | tf_op jit(solution)/shard_map/all_gather | solution.py:21
  12.2 403.7 %reduce-scatter.2.cloned.1.call-start = ((), (), s32[]{:S(2)}) async-start(), calls=%async_computation.1 | async-start | bytes 147456 | tf_op jit(solution)/shard_map/reduce_scatter | solution.py:136
  13.3 75.3 %copy-start.3 = (bf16[64,128]{1,0:T(8,128)(2,1)S(1)}, bf16[64,128]{1,0:T(8,128)(2,1)}, u32[]{:S(2)}) copy-start(bf16[64,128]{1,0:T(8,128)(2,1)} %param.20) | copy-start | bytes 49156
  303.2 74.1 %copy-start.6 = (f32[16]{0:T(128)S(1)}, f32[16]{0:T(128)}, u32[]{:S(2)}) copy-start(f32[16]{0:T(128)} %param.23) | copy-start | bytes 196
  377.3 2.6 copy-start.2
  377.3 2.8 copy-start.5
  379.7 36.2 %copy-start.4 = (bf16[64,512]{1,0:T(8,128)(2,1)S(1)}, bf16[64,512]{1,0:T(8,128)(2,1)}, u32[]{:S(2)}) copy-start(bf16[64,512]{1,0:T(8,128)(2,1)} %param.26) | copy-start | bytes 196612
  380.2 312.9 %copy-start.1 = (bf16[64,1024]{1,0:T(8,128)(2,1)}, bf16[64,1024]{1,0:T(8,128)(2,1)S(1)}, u32[]{:S(2)}) copy-start(bf16[64,1024]{1,0:T(8,128)(2,1)S(1)} %multiply_convert_fusion) | copy-start | bytes 393220
  381.6 173.2 %all-gather.11.cloned.1.call-start = ((), (), s32[]{:S(2)}) async-start(), calls=%async_computation.4 | async-start | bytes 1064960 | tf_op jit(solution)/shard_map/all_gather | solution.py:162
  382.4 310.7 %all-gather.7.cloned.1.call-start = ((), (), s32[]{:S(2)}) async-start(), calls=%async_computation.2 | async-start | bytes 1064960 | tf_op jit(solution)/shard_map/all_gather | solution.py:163
Sparse Core Ops, SparseCore 0:
  12.3 290.7 all-gather.8
  381.8 34.0 reduce-scatter.1
  419.2 135.5 all-gather.10
  558.0 134.9 all-gather.6
where the time goes:
time: 755 us; the launch traced here: 750 us
  waiting for transfers between devices  523 us (69%)
  other arithmetic  75.7 us (10%)
  blocking collectives  72.4 us (10%)
  matrix products  41 us (5%)
  loops' own time  14.7 us (2%)
  between operations  14 us (2%)
  local copies, waits for them, and re-layouts  9.01 us (1%)
    all_gather x1, waiting for transfers between devices, carried_in(): gathered = jax.tree.map(lambda a: lax.all_gather(a, axis), part)  213 us
    all_gather x1, waiting for transfers between devices, per_device(): value_portion = lax.all_gather(values, 'seq', axis=1, tiled=True)  138 us
    all_gather x1, waiting for transfers between devices, per_device(): key_portion = lax.all_gather(key_heads, 'seq', axis=1, tiled=True)  138 us
    all_gather x1, blocking collectives, carried_in(): gathered = jax.tree.map(lambda a: lax.all_gather(a, axis), part)  72.4 us
    add x60, other arithmetic, chain_combine(): latter[0][..., None, None] * earlier[1] + latter[1]  71.2 us
    reduce_scatter x1, waiting for transfers between devices, per_device(): lax.psum_scatter(jnp.transpose(product.reshape(tokens_here, lax.axis_size...  33.4 us
    dot_general x16, matrix products, update(): jnp.einsum('hrc,hcd->hrd', weights.astype(jnp.bfloat16), value_slab, pref...  17.8 us
    dot_general x16, matrix products, update(): jnp.einsum('hrd,hcd->hrc', query_block, key_slab, preferred_element_type=...  17 us
  transfers between devices with their start and end apart: 4, of which 4 were waited for; matrix products, arithmetic and copies ran while one was open for 1% of the time, Pallas kernels for 0%

commit v1 on v0

--- a/solution.py
+++ b/solution.py
@@ -3,7 +3,7 @@
 import jax
 import jax.numpy as jnp
 from jax import lax
-from jax.sharding import PartitionSpec as P
+from jax.sharding import Mesh, PartitionSpec as P
 
 MHEAD_DIM = 64
 STATE = 128
@@ -14,19 +14,6 @@
 
 highest = lax.Precision.HIGHEST
 norm_eps = 1e-05
-
-
-def carried_in(part, axis, combine, identity):
-    place = lax.axis_index(axis)
-    gathered = jax.tree.map(lambda a: lax.all_gather(a, axis), part)
-    state = jax.tree.map(lambda a, e: jnp.zeros_like(a) + jnp.asarray(e, a.dtype), part, identity)
-
-    def one(lap, state):
-        return combine(
-            state, jax.tree.map(lambda a: lax.dynamic_index_in_dim(a, lap, 0, False), gathered)
-        )
-
-    return lax.fori_loop(0, place, one, state)
 
 
 def block_scan(inputs, b_group, c_group, time_step, decay_rate):
@@ -56,10 +43,6 @@
     return ((grouped * inverse).reshape(token_count, -1) * norm_gain).astype(jnp.bfloat16)
 
 
-def chain_combine(earlier, latter):
-    return (earlier[0] * latter[0], latter[0][..., None, None] * earlier[1] + latter[1])
-
-
 def query_layout(payload, kv_here, per_kv):
     count_rows = payload.shape[0]
     shaped = payload.reshape(count_rows, kv_here, per_kv, HEAD_DIM)
@@ -107,6 +90,50 @@
         return current
 
     return lax.cond(key_first <= jnp.max(query_pos), update, unchanged, running)
+
+
+def masked_weights(decays, upto):
+    count = decays.shape[0]
+    earlier = jnp.arange(count)[:, None]
+    later = jnp.arange(count)[None, :]
+    between = (later > earlier) & (later < upto)
+    spans = jnp.prod(jnp.where(between[:, :, None], decays[None, :, :], 1.0), axis=1)
+    return jnp.where((jnp.arange(count) < upto)[:, None], spans, 0.0)
+
+
+def carried_state(totals, summary):
+    head_total = totals.size
+    flat = summary.reshape(head_total, -1)
+    width = flat.shape[1]
+    lanes = 128
+    packed = jnp.concatenate(
+        [flat, jnp.broadcast_to(totals.reshape(head_total, 1), (head_total, lanes))], axis=1
+    )
+    near = lax.all_gather(packed, "sx")
+    near_count = near.shape[0]
+    here = lax.axis_index("sx")
+    near_decay = near[:, :, width]
+    near_state = near[:, :, :width]
+    own_weights = masked_weights(near_decay, here)
+    prefix = jnp.sum(own_weights[:, :, None] * near_state, axis=0)
+    group_weights = masked_weights(near_decay, near_count)
+    group_state = jnp.sum(group_weights[:, :, None] * near_state, axis=0)
+    group_decay = jnp.prod(near_decay, axis=0)
+    own_decay = jnp.prod(
+        jnp.where((jnp.arange(near_count) < here)[:, None], near_decay, 1.0), axis=0
+    )
+    chunk = width // near_count
+    piece = lax.dynamic_slice_in_dim(group_state, here * chunk, chunk, 1)
+    far_packed = jnp.concatenate(
+        [piece, jnp.broadcast_to(group_decay.reshape(head_total, 1), (head_total, lanes))], axis=1
+    )
+    far = lax.all_gather(far_packed, "sz")
+    far_weights = masked_weights(far[:, :, chunk], lax.axis_index("sz"))
+    entering = jnp.sum(far_weights[:, :, None] * far[:, :, :chunk], axis=0)
+    assembled = lax.all_gather(entering, "sx")
+    before = jnp.transpose(assembled, (1, 0, 2)).reshape(head_total, width)
+    state_in = own_decay[:, None] * before + prefix
+    return state_in.reshape(summary.shape)
 
 
 def per_device(
@@ -124,25 +151,30 @@
     log_decay, local_out, summary, totals = block_scan(
         inputs, b_group, c_group, time_step, decay_rate
     )
-    _, state_in = carried_in(
-        (totals, summary), "seq", chain_combine, (jnp.ones_like(totals), jnp.zeros_like(summary))
-    )
+    state_in = carried_state(totals, summary)
     skip_heads = skip_d.reshape(group_count, per_group)[None, :, :, None]
     ssm_out = local_out + carried_out(c_group, state_in, log_decay) + skip_heads * inputs
     mamba_out = gated_norm(ssm_out.reshape(tokens_here, -1), gate_z, norm_gain, group_count)
     kv_here = keys.shape[1] // HEAD_DIM
     per_kv = QHEADS // KVHEADS
+    tp_count = lax.axis_size("tp")
     product = jnp.dot(mamba_out, value_weight, preferred_element_type=jnp.float32)
-    values = lax.psum_scatter(
-        jnp.transpose(
-            product.reshape(tokens_here, lax.axis_size("tp") * kv_here, HEAD_DIM), (1, 0, 2)
-        ).astype(jnp.bfloat16),
-        "tp",
-        scatter_dimension=0,
-        tiled=True,
-    )
+    partials = jnp.transpose(
+        product.reshape(tokens_here, tp_count, kv_here * HEAD_DIM), (1, 0, 2)
+    )
+    exchanged = lax.all_to_all(partials, "tp", 0, 0, tiled=True)
+    values = jnp.sum(exchanged, axis=0).astype(jnp.bfloat16)
+    values = jnp.transpose(values.reshape(tokens_here, kv_here, HEAD_DIM), (1, 0, 2))
     key_heads = jnp.transpose(keys.reshape(tokens_here, kv_here, HEAD_DIM), (1, 0, 2))
-    my_index = lax.axis_index("seq")
+    pair = jnp.stack([key_heads, values])
+    far_pairs = lax.all_gather(pair, "sz")
+    all_pairs = lax.all_gather(far_pairs, "sx", axis=1)
+    all_pairs = jnp.transpose(all_pairs, (2, 3, 0, 1, 4, 5)).reshape(
+        2, kv_here, -1, HEAD_DIM
+    )
+    key_portion = all_pairs[0]
+    value_portion = all_pairs[1]
+    my_index = lax.axis_index("sz") * lax.axis_size("sx") + lax.axis_index("sx")
     query_sets = [
         (
             query_layout(queries, kv_here, per_kv),
@@ -159,8 +191,6 @@
             for query_set in query_sets
         )
     )
-    key_portion = lax.all_gather(key_heads, "seq", axis=1, tiled=True)
-    value_portion = lax.all_gather(values, "seq", axis=1, tiled=True)
     length = key_portion.shape[1]
     block_len = length
     for multiple in (1, 2, 4):
@@ -184,23 +214,30 @@
 
 
 def solution(mesh):
+    seq_count = mesh.shape["seq"]
+    near_count = 4 if seq_count % 4 == 0 else 1
+    split = Mesh(
+        mesh.devices.reshape(seq_count // near_count, near_count, mesh.shape["tp"]),
+        ("sz", "sx", "tp"),
+    )
+    rows = ("sz", "sx")
     placed = (
-        P("seq", "tp"),
-        P("seq", "tp"),
-        P("seq", "tp"),
-        P("seq", "tp"),
-        P("tp", "seq"),
+        P(rows, "tp"),
+        P(rows, "tp"),
+        P(rows, "tp"),
+        P(rows, "tp"),
+        P("tp", rows),
         P("tp"),
         P("tp"),
         P("tp"),
         P("tp", None),
-        P("seq", "tp"),
-        P("seq", "tp"),
+        P(rows, "tp"),
+        P(rows, "tp"),
     )
     return jax.shard_map(
         per_device,
-        mesh=mesh,
+        mesh=split,
         in_specs=placed,
-        out_specs=(P("seq", "tp"), P("seq", "tp")),
+        out_specs=(P(rows, "tp"), P(rows, "tp")),
         check_vma=False,
     )

time: 755 us -> 263 us (0.35)
  the two profiles are of different devices: /device:TPU:480 before, /device:TPU:481 now
where the time goes in v1:
time: 263 us
  waiting for transfers between devices  138 us (52%)
  blocking collectives  57.8 us (22%)
  local copies, waits for them, and re-layouts  15.3 us (6%)
  between operations  14.1 us (5%)
  other arithmetic  13.2 us (5%)
  matrix products  12.6 us (5%)
  loops' own time  11.4 us (4%)
    all_gather x1, waiting for transfers between devices, carried_state(): far = lax.all_gather(far_packed, 'sz')  57.2 us
    all_gather x1, waiting for transfers between devices, per_device(): all_pairs = lax.all_gather(far_pairs, 'sx', axis=1)  42.9 us
    all_gather x1, waiting for transfers between devices, carried_state(): near = lax.all_gather(packed, 'sx')  37.8 us
    all_gather x1, blocking collectives, per_device(): far_pairs = lax.all_gather(pair, 'sz')  24.1 us
    all_to_all x1, blocking collectives, per_device(): exchanged = lax.all_to_all(partials, 'tp', 0, 0, tiled=True)  23.1 us
    all_gather x1, blocking collectives, carried_state(): assembled = lax.all_gather(entering, 'sx')  10.6 us
    another operation x1, loops' own time, per_device(): finished = lax.fori_loop(0, length // block_len, one_block, initial)  10.4 us
  transfers between devices with their start and end apart: 3, of which 3 were waited for; matrix products, arithmetic and copies ran while one was open for 2% of the time, Pallas kernels for 0%

profile of v1, /device:TPU:481, one launch (start us, length us, event | category | flops | bytes accessed | tf_op | source)
XLA Modules:
  0.0 262.6 jit_solution(5920610687277513414)
XLA Ops:
  7.9 0.8 multiply_bitcast_fusion.1
  9.1 0.8 multiply_bitcast_fusion
  9.8 1.1 copy.57
  11.7 0.8 pad_maximum_fusion
  12.7 37.8 %all-gather.9.cloned.1.call-done = f32[64,8320]{1,0:T(8,128)} async-done(((f32[16,8320]{1,0:T(8,128)}), f32[64,8320]{1,0:T(8,128)}) %all-gather.9.cloned.1.call-update) | async-done | bytes 2129936 | tf_op jit(solution)/shard_map/all_gather | solution.py:112
  50.5 0.9 slice_reduce_fusion.1
  51.7 2.9 %multiply_reduce_fusion.1 = (f32[16,8192]{1,0:T(8,128)S(1)}, f32[16,8192]{1,0:T(8,128)}) fusion(f32[4,16,8320]{2,1,0:T(8,128)} %bitcast.112, f32[4,16]{1,0:T(4,128)S(1)} %get-tuple-element.406, f32[4,16]{1,0:T(4,128)S(1)} %get-tuple-element.405), kind=kLoop, calls=%fused_computation.23 | loop fusion | flops 1835008 | bytes 3146240 | tf_op jit(solution)/shard_map/reduce_sum | solution.py:120
  55.6 2.9 %copy.56 = bf16[1024,1024]{1,0:T(8,128)(2,1)S(1)} copy(bf16[1024,1024]{0,1:T(8,128)(2,1)} %bitcast.114) | data formatting | bytes 4194304 | tf_op jit(solution)/shard_map/dot_general | solution.py:161
  58.6 1.5 convolution_bitcast_fusion.2
  60.1 1.1 copy.59
  61.2 57.2 %all-gather.11.cloned.1.call-done = f32[256,2176]{1,0:T(8,128)} async-done(((f32[16,2176]{1,0:T(8,128)}), f32[256,2176]{1,0:T(8,128)}) %all-gather.11.cloned.1.call-update) | async-done | bytes 2228240 | tf_op jit(solution)/shard_map/all_gather | solution.py:130
  118.5 1.0 slice_reduce_fusion
  119.7 1.8 fusion.16
  121.5 10.6 %all-gather.2 = f32[64,2048]{1,0:T(8,128)S(1)} all-gather(f32[16,2048]{1,0:T(8,128)S(1)} %fusion.16), channel_id=4, replica_groups=mesh['sz'=16,'sx'=4,'tp'=8] {'sx'}, dimensions={0}, use_global_device_ids=true | all-gather | bytes 655360 | tf_op jit(solution)/shard_map/all_gather | solution.py:133
  132.1 1.1 copy.48
  133.3 2.1 reshape.404
  135.4 1.2 bitcast_add_fusion
  136.6 2.0 fusion.19
  139.5 0.8 convolution_bitcast_fusion.3
  140.3 23.1 %all_to_all.5 = f32[8,64,128]{2,1,0:T(8,128)S(1)} all-to-all(f32[8,64,128]{2,1,0:T(8,128)S(1)} %convolution_bitcast_fusion.3), channel_id=1, replica_groups=mesh['sz'=16,'sx'=4,'tp'=8] {'tp'}, dimensions={0} | all-to-all | bytes 524288 | tf_op jit(solution)/shard_map/all_to_all | solution.py:165
  163.4 24.1 %all-gather.3 = bf16[32,1,64,128]{3,2,1,0:T(8,128)(2,1)} all-gather(bf16[2,1,64,128]{3,2,1,0:T(8,128)(2,1)S(1)} %pad_maximum_fusion.2), channel_id=5, replica_groups=mesh['sz'=16,'sx'=4,'tp'=8] {'sz'}, dimensions={0}, use_global_device_ids=true | all-gather | bytes 557056 | tf_op jit(solution)/shard_map/all_gather | solution.py:170
  188.3 42.9 %all-gather.13.cloned.1.call-done = bf16[16,8,1,64,128]{4,3,1,0,2:T(8,128)(2,1)} async-done(((bf16[16,2,1,64,128]{4,3,1,0,2:T(8,128)(2,1)}), bf16[16,8,1,64,128]{4,3,1,0,2:T(8,128)(2,1)}) %all-gather.13.cloned.1.call-update) | async-done | bytes 2097168 | tf_op jit(solution)/shard_map/all_gather | solution.py:171
  231.2 1.8 fusion.47
  233.0 22.2 %while.20 = (s32[]{:T(128)}, f32[1,256]{1,0:T(1,128)S(1)}, f32[1,256]{1,0:T(1,128)S(1)}, f32[1,256,128]{2,1,0:T(8,128)S(1)}, s32[]{:T(128)}, /*index=5*/bf16[1,4...) while((s32[]{:T(128)}, f32[1,256]{1,0:T(1,128)S(1)}, ...), condition=%wide.region_17.18_spmd.clone, body=%wide.region_12.17_spmd.clone.sunk | while | flops 34145032 | bytes 1270325 | solution.py:210
  (241 shorter events, 28.4 us)
Async XLA Ops:
  7.2 3.8 %copy-start = (bf16[64,128]{1,0:T(8,128)(2,1)S(1)}, bf16[64,128]{1,0:T(8,128)(2,1)}, u32[]{:S(2)}) copy-start(bf16[64,128]{1,0:T(8,128)(2,1)} %param.17) | copy-start | bytes 49156
  7.2 43.3 %all-gather.9.cloned.1.call-start = ((), (), s32[]{:S(2)}) async-start(), calls=%async_computation.1 | async-start | bytes 2662400 | tf_op jit(solution)/shard_map/all_gather | solution.py:112
  12.6 42.8 %copy-start.1 = (bf16[64,1024]{1,0:T(8,128)(2,1)S(1)}, bf16[64,1024]{1,0:T(8,128)(2,1)}, u32[]{:S(2)}) copy-start(bf16[64,1024]{1,0:T(8,128)(2,1)} %param.15) | copy-start | bytes 393220
  12.6 105.9 %all-gather.11.cloned.1.call-start = ((), (), s32[]{:S(2)}) async-start(), calls=%async_computation.2 | async-start | bytes 2367488 | tf_op jit(solution)/shard_map/all_gather | solution.py:130
  55.3 175.8 %all-gather.13.cloned.1.call-start = ((), (), s32[]{:S(2)}) async-start(), calls=%async_computation.3 | async-start | bytes 2621440 | tf_op jit(solution)/shard_map/all_gather | solution.py:171
  55.6 2.9 %copy-start.4 = (bf16[64,128]{1,0:T(8,128)(2,1)S(1)}, bf16[64,128]{1,0:T(8,128)(2,1)}, u32[]{:S(2)}) copy-start(bf16[64,128]{1,0:T(8,128)(2,1)} %param.18) | copy-start | bytes 49156
  121.5 15.1 %copy-start.8 = (f32[16]{0:T(128)S(1)}, f32[16]{0:T(128)}, u32[]{:S(2)}) copy-start(f32[16]{0:T(128)} %param.21) | copy-start | bytes 196
  136.6 2.6 copy-start.3
  136.6 2.8 %copy-start.7 = (f32[1024]{0:T(1024)S(1)}, f32[1024]{0:T(1024)}, u32[]{:S(2)}) copy-start(f32[1024]{0:T(1024)} %param.22) | copy-start | bytes 12292
  139.2 24.2 %copy-start.6 = (bf16[64,128]{1,0:T(8,128)(2,1)S(1)}, bf16[64,128]{1,0:T(8,128)(2,1)}, u32[]{:S(2)}) copy-start(bf16[64,128]{1,0:T(8,128)(2,1)} %param.25) | copy-start | bytes 49156
  139.5 48.1 %copy-start.2 = (bf16[64,1024]{1,0:T(8,128)(2,1)}, bf16[64,1024]{1,0:T(8,128)(2,1)S(1)}, u32[]{:S(2)}) copy-start(bf16[64,1024]{1,0:T(8,128)(2,1)S(1)} %multiply_convert_fusion) | copy-start | bytes 393220
  139.5 48.1 %copy-start.5 = (bf16[64,512]{1,0:T(8,128)(2,1)S(1)}, bf16[64,512]{1,0:T(8,128)(2,1)}, u32[]{:S(2)}) copy-start(bf16[64,512]{1,0:T(8,128)(2,1)} %param.24) | copy-start | bytes 196612
Sparse Core Ops, SparseCore 0:
  12.7 37.7 all-gather.8
  55.5 62.9 all-gather.10
  187.7 43.4 all-gather.12

commit v2 on v1

--- a/solution.py
+++ b/solution.py
@@ -10,6 +10,7 @@
 QHEADS = 32
 KVHEADS = 8
 HEAD_DIM = 128
+SEQ_AXES = ("sx", "zl", "zh")
 
 
 highest = lax.Precision.HIGHEST
@@ -101,38 +102,52 @@
     return jnp.where((jnp.arange(count) < upto)[:, None], spans, 0.0)
 
 
+def pack_decay(state, decay):
+    lanes = 128
+    return jnp.concatenate(
+        [state, jnp.broadcast_to(decay[..., None], decay.shape + (lanes,))], axis=-1
+    )
+
+
+def entering_top(axis, decay, state):
+    width = state.shape[1]
+    gathered = lax.all_gather(pack_decay(state, decay), axis)
+    weights = masked_weights(gathered[:, :, width], lax.axis_index(axis))
+    return jnp.sum(weights[:, :, None] * gathered[:, :, :width], axis=0)
+
+
+def entering_state(axes, decay, state):
+    if len(axes) == 1:
+        return entering_top(axes[0], decay, state)
+    axis = axes[0]
+    count = lax.axis_size(axis)
+    head_total, width = state.shape
+    chunk = width // count
+    pieces = jnp.transpose(state.reshape(head_total, count, chunk), (1, 0, 2))
+    packed = pack_decay(pieces, jnp.broadcast_to(decay, (count, head_total)))
+    received = lax.all_to_all(packed, axis, 0, 0, tiled=True)
+    decays = received[:, :, chunk]
+    states = received[:, :, :chunk]
+    member = jnp.arange(count)
+    prefixes = [
+        jnp.sum(masked_weights(decays, upto)[:, :, None] * states, axis=0)
+        for upto in range(count + 1)
+    ]
+    decay_before = [
+        jnp.prod(jnp.where((member < upto)[:, None], decays, 1.0), axis=0)
+        for upto in range(count + 1)
+    ]
+    group_in = entering_state(axes[1:], decay_before[count], prefixes[count])
+    outgoing = jnp.stack(
+        [decay_before[upto][:, None] * group_in + prefixes[upto] for upto in range(count)]
+    )
+    returned = lax.all_to_all(outgoing, axis, 0, 0, tiled=True)
+    return jnp.transpose(returned, (1, 0, 2)).reshape(head_total, width)
+
+
 def carried_state(totals, summary):
     head_total = totals.size
-    flat = summary.reshape(head_total, -1)
-    width = flat.shape[1]
-    lanes = 128
-    packed = jnp.concatenate(
-        [flat, jnp.broadcast_to(totals.reshape(head_total, 1), (head_total, lanes))], axis=1
-    )
-    near = lax.all_gather(packed, "sx")
-    near_count = near.shape[0]
-    here = lax.axis_index("sx")
-    near_decay = near[:, :, width]
-    near_state = near[:, :, :width]
-    own_weights = masked_weights(near_decay, here)
-    prefix = jnp.sum(own_weights[:, :, None] * near_state, axis=0)
-    group_weights = masked_weights(near_decay, near_count)
-    group_state = jnp.sum(group_weights[:, :, None] * near_state, axis=0)
-    group_decay = jnp.prod(near_decay, axis=0)
-    own_decay = jnp.prod(
-        jnp.where((jnp.arange(near_count) < here)[:, None], near_decay, 1.0), axis=0
-    )
-    chunk = width // near_count
-    piece = lax.dynamic_slice_in_dim(group_state, here * chunk, chunk, 1)
-    far_packed = jnp.concatenate(
-        [piece, jnp.broadcast_to(group_decay.reshape(head_total, 1), (head_total, lanes))], axis=1
-    )
-    far = lax.all_gather(far_packed, "sz")
-    far_weights = masked_weights(far[:, :, chunk], lax.axis_index("sz"))
-    entering = jnp.sum(far_weights[:, :, None] * far[:, :, :chunk], axis=0)
-    assembled = lax.all_gather(entering, "sx")
-    before = jnp.transpose(assembled, (1, 0, 2)).reshape(head_total, width)
-    state_in = own_decay[:, None] * before + prefix
+    state_in = entering_state(SEQ_AXES, totals.reshape(head_total), summary.reshape(head_total, -1))
     return state_in.reshape(summary.shape)
 
 
@@ -167,14 +182,12 @@
     values = jnp.transpose(values.reshape(tokens_here, kv_here, HEAD_DIM), (1, 0, 2))
     key_heads = jnp.transpose(keys.reshape(tokens_here, kv_here, HEAD_DIM), (1, 0, 2))
     pair = jnp.stack([key_heads, values])
-    far_pairs = lax.all_gather(pair, "sz")
-    all_pairs = lax.all_gather(far_pairs, "sx", axis=1)
-    all_pairs = jnp.transpose(all_pairs, (2, 3, 0, 1, 4, 5)).reshape(
-        2, kv_here, -1, HEAD_DIM
-    )
+    for axis in SEQ_AXES[::-1]:
+        pair = lax.all_gather(pair, axis)
+    all_pairs = jnp.transpose(pair, (3, 4, 2, 1, 0, 5, 6)).reshape(2, kv_here, -1, HEAD_DIM)
     key_portion = all_pairs[0]
     value_portion = all_pairs[1]
-    my_index = lax.axis_index("sz") * lax.axis_size("sx") + lax.axis_index("sx")
+    my_index = lax.axis_index(SEQ_AXES[::-1])
     query_sets = [
         (
             query_layout(queries, kv_here, per_kv),
@@ -215,12 +228,11 @@
 
 def solution(mesh):
     seq_count = mesh.shape["seq"]
-    near_count = 4 if seq_count % 4 == 0 else 1
     split = Mesh(
-        mesh.devices.reshape(seq_count // near_count, near_count, mesh.shape["tp"]),
-        ("sz", "sx", "tp"),
-    )
-    rows = ("sz", "sx")
+        mesh.devices.reshape(seq_count // 16, 4, 4, mesh.shape["tp"]),
+        SEQ_AXES[::-1] + ("tp",),
+    )
+    rows = SEQ_AXES[::-1]
     placed = (
         P(rows, "tp"),
         P(rows, "tp"),

time: 263 us -> 209 us (0.79)
  waiting for transfers between devices: 138 us -> 52.8 us
  starting transfers between devices: 0.12 us -> 17.4 us
  local copies, waits for them, and re-layouts: 15.3 us -> 23.6 us
  blocking collectives: 57.8 us -> 61.4 us
    all_gather x3 -> x1, waiting for transfers between devices: 138 us -> 39.1 us  [per_device(): pair = lax.all_gather(pair, axis)]
    all_to_all x0 -> x4, starting transfers between devices: none -> 17.3 us  [the longest x2 8.95 us: entering_state(): received = lax.all_to_all(packed, axis, 0, 0, tiled=True)]
    all_to_all x0 -> x4, waiting for transfers between devices: none -> 13.7 us  [the longest x2 12 us: entering_state(): received = lax.all_to_all(packed, axis, 0, 0, tiled=True)]
    all_gather x2 -> x3, blocking collectives: 34.7 us -> 43.2 us  [the longest x2 27.8 us: per_device(): pair = lax.all_gather(pair, axis)]
    all_to_all x1, blocking collectives: 23.1 us -> 18.2 us  [per_device(): exchanged = lax.all_to_all(partials, 'tp', 0, 0, tiled=True)]
    add x0 -> x4, local copies, waits for them, and re-layouts: none -> 3.81 us  [entering_state(): decay_before[upto][:, None] * group_in + prefixes[upto]]
    reduce_sum x2 -> x3, other arithmetic: 4.71 us -> 1.03 us  [the longest x2 0.94 us: entering_state(): jnp.sum(masked_weights(decays, upto)[:, :, None] * states, axis=0)]
  transfers between devices with their start and end apart: 3 -> 5, of which waited for: 3 -> 4; matrix products, arithmetic and copies ran while one was open for 2% -> 5% of each run, Pallas kernels for 0% -> 0%
where the time goes in v2:
time: 209 us; the launch traced here: 208 us
  blocking collectives  61.4 us (29%)
  waiting for transfers between devices  52.8 us (25%)
  local copies, waits for them, and re-layouts  23.6 us (11%)
  starting transfers between devices  17.4 us (8%)
  between operations  14.5 us (7%)
  other arithmetic  13.9 us (7%)
  matrix products  13.2 us (6%)
  loops' own time  11.4 us (5%)
    all_gather x1, waiting for transfers between devices, per_device(): pair = lax.all_gather(pair, axis)  39.1 us
    all_gather x2, blocking collectives, per_device(): pair = lax.all_gather(pair, axis)  27.8 us
    all_to_all x1, blocking collectives, per_device(): exchanged = lax.all_to_all(partials, 'tp', 0, 0, tiled=True)  18.2 us
    all_gather x1, blocking collectives, entering_top(): gathered = lax.all_gather(pack_decay(state, decay), axis)  15.4 us
    all_to_all x2, waiting for transfers between devices, entering_state(): received = lax.all_to_all(packed, axis, 0, 0, tiled=True)  12 us
    another operation x1, loops' own time, per_device(): finished = lax.fori_loop(0, length // block_len, one_block, initial)  10.4 us
    all_to_all x2, starting transfers between devices, entering_state(): received = lax.all_to_all(packed, axis, 0, 0, tiled=True)  8.95 us
    all_to_all x2, starting transfers between devices, entering_state(): returned = lax.all_to_all(outgoing, axis, 0, 0, tiled=True)  8.37 us
  transfers between devices with their start and end apart: 5, of which 4 were waited for; matrix products, arithmetic and copies ran while one was open for 5% of the time, Pallas kernels for 0%

profile of v2, /device:TPU:481, one launch (start us, length us, event | category | flops | bytes accessed | tf_op | source)
XLA Modules:
  0.0 208.2 jit_solution(13357291425733408386)
XLA Ops:
  9.0 1.3 multiply_bitcast_fusion
  13.2 4.0 %all-to-all-start = ((f32[4,16,2176]{2,1,0:T(8,128)}), f32[4,16,2176]{2,1,0:T(8,128)S(1)}, u32[]{:S(2)}, u32[]{:S(2)}) async-start(f32[4,16,2176]{2,1,0:T(8,128)} %pad_maximum_fusion), calls=%async_computation | async-start | bytes 1114112 | tf_op jit(solution)/shard_map/all_to_all | solution.py:128
  17.3 8.9 %all-to-all-done = f32[4,16,2176]{2,1,0:T(8,128)S(1)} async-done(((f32[4,16,2176]{2,1,0:T(8,128)}), f32[4,16,2176]{2,1,0:T(8,128)S(1)}, u32[]{:S(2)}, u32[]{:S(2)}) %all-to-all-start) | async-done | bytes 557088 | tf_op jit(solution)/shard_map/all_to_all | solution.py:128
  29.4 4.9 %all-to-all-start.1 = ((f32[4,16,640]{2,1,0:T(8,128)}), f32[4,16,640]{2,1,0:T(8,128)S(1)}, u32[]{:S(2)}, u32[]{:S(2)}) async-start(f32[4,16,640]{2,1,0:T(8,128)} %copy.127), calls=%async_computation.1 | async-start | bytes 327680 | tf_op jit(solution)/shard_map/all_to_all | solution.py:128
  34.3 3.2 %all-to-all-done.1 = f32[4,16,640]{2,1,0:T(8,128)S(1)} async-done(((f32[4,16,640]{2,1,0:T(8,128)}), f32[4,16,640]{2,1,0:T(8,128)S(1)}, u32[]{:S(2)}, u32[]{:S(2)}) %all-to-all-start.1) | async-done | bytes 163872 | tf_op jit(solution)/shard_map/all_to_all | solution.py:128
  38.0 15.4 %all-gather = f32[64,640]{1,0:T(8,128)S(1)} all-gather(f32[16,640]{1,0:T(8,128)S(1)} %pad_maximum_fusion.4), channel_id=2, replica_groups=mesh['zh'=4,'zl'=4,'sx'=4,'tp'=8] {'zh'}, dimensions={0}, use_global_device_ids=true | all-gather | bytes 204800 | tf_op jit(solution)/shard_map/all_gather | solution.py:114
  54.5 4.9 %all-to-all-start.2 = ((f32[4,16,512]{2,1,0:T(8,128)}), f32[4,16,512]{2,1,0:T(8,128)}, u32[]{:S(2)}, u32[]{:S(2)}) async-start(f32[4,16,512]{2,1,0:T(8,128)} %pad_maximum_fusion.3), calls=%async_computation.2 | async-start | bytes 262144 | tf_op jit(solution)/shard_map/all_to_all | solution.py:144
  62.0 1.3 copy.155
  63.4 2.2 %copy.128 = f32[16,4,512]{0,2,1:T(8,128)} copy(f32[16,4,512]{2,0,1:T(8,128)} %bitcast.25) | data formatting | bytes 262144 | tf_op jit(solution)/shard_map/transpose | solution.py:145
  65.6 3.7 %bitcast_add_fusion.3 = (f32[1,16,2048]{1,2,0:T(8,128)}, f32[1,16,2048]{1,2,0:T(8,128)}, f32[1,16,2048]{1,2,0:T(8,128)}, f32[1,16,2048]{1,2,0:T(8,128)}) fusion(f32[16,2048]{0,1:T(8,128)S(1)} %copy.152, f32[16,4,512]{0,2,1:T(8,128)} %copy.128, f32[16,2048]{0,1:T(8,128)S(1)} %copy.153, f32[16]{0:T(128)} %get-tuple-element.382, f32[16,2048]{0,1:T(8,128)S(1)} %copy.154, ...), kind=kLoop, calls=%fused_computation.29 | loop fusion | flops 229376 | bytes 1179840 | tf_op jit(solution)/shard_map/add | solution.py:142
  69.3 1.7 copy.133
  70.9 1.5 copy.134
  73.9 3.5 %all-to-all-start.3 = ((f32[4,16,2048]{2,1,0:T(8,128)}), f32[4,16,2048]{2,1,0:T(8,128)S(1)}, u32[]{:S(2)}, u32[]{:S(2)}) async-start(f32[4,16,2048]{2,1,0:T(8,128)} %pad_maximum_fusion.1), calls=%async_computation.3 | async-start | bytes 1048576 | tf_op jit(solution)/shard_map/all_to_all | solution.py:144
  78.3 2.9 %copy.150 = bf16[1024,1024]{1,0:T(8,128)(2,1)S(1)} copy(bf16[1024,1024]{0,1:T(8,128)(2,1)} %bitcast.150) | data formatting | bytes 4194304 | tf_op jit(solution)/shard_map/dot_general | solution.py:176
  81.2 1.5 convolution_bitcast_fusion.2
  82.7 1.6 all-to-all-done.3
  85.5 1.3 reshape.798
  86.8 2.0 fusion.18
  90.5 18.2 %all_to_all.25 = f32[8,64,128]{2,1,0:T(8,128)S(1)} all-to-all(f32[8,64,128]{2,1,0:T(8,128)S(1)} %convolution_bitcast_fusion.3), channel_id=1, replica_groups=mesh['zh'=4,'zl'=4,'sx'=4,'tp'=8] {'tp'}, dimensions={0} | all-to-all | bytes 524288 | tf_op jit(solution)/shard_map/all_to_all | solution.py:180
  108.7 15.0 %all-gather.1 = bf16[8,1,64,128]{3,2,1,0:T(8,128)(2,1)S(1)} all-gather(bf16[2,1,64,128]{3,2,1,0:T(8,128)(2,1)S(1)} %pad_maximum_fusion.5), channel_id=3, replica_groups=mesh['zh'=4,'zl'=4,'sx'=4,'tp'=8] {'zh'}, dimensions={0}, use_global_device_ids=true | all-gather | bytes 163840 | tf_op jit(solution)/shard_map/all_gather | solution.py:186
  123.7 12.8 %all-gather.2 = bf16[16,2,1,64,128]{4,3,2,1,0:T(8,128)(2,1)} all-gather(bf16[4,2,1,64,128]{4,3,2,1,0:T(8,128)(2,1)S(1)} %bitcast.162), channel_id=4, replica_groups=mesh['zh'=4,'zl'=4,'sx'=4,'tp'=8] {'zl'}, dimensions={0}, use_global_device_ids=true | all-gather | bytes 655360 | tf_op jit(solution)/shard_map/all_gather | solution.py:186
  137.3 39.1 %all-gather.6.cloned.1.call-done = bf16[16,4,2,1,64,128]{5,4,3,2,1,0:T(8,128)(2,1)} async-done(((bf16[4,4,2,1,64,128]{5,4,3,2,1,0:T(8,128)(2,1)}), bf16[16,4,2,1,64,128]{5,4,3,2,1,0:T(8,128)(2,1)}) %all-gather.6.cloned.1.call-update) | async-done | bytes 2097168 | tf_op jit(solution)/shard_map/all_gather | solution.py:186
  176.4 1.7 fusion.49
  178.3 22.2 %while.20 = (s32[]{:T(128)}, f32[1,256]{1,0:T(1,128)S(1)}, f32[1,256]{1,0:T(1,128)S(1)}, f32[1,256,128]{2,1,0:T(8,128)S(1)}, s32[]{:T(128)}, /*index=5*/bf16[1,4...) while((s32[]{:T(128)}, f32[1,256]{1,0:T(1,128)S(1)}, ...), condition=%wide.region_37.38_spmd.clone, body=%wide.region_32.37_spmd.clone.sunk | while | flops 34145032 | bytes 1270325 | solution.py:223
  (284 shorter events, 41.4 us)
Async XLA Ops:
  7.2 4.3 %copy-start = (bf16[64,128]{1,0:T(8,128)(2,1)S(1)}, bf16[64,128]{1,0:T(8,128)(2,1)}, u32[]{:S(2)}) copy-start(bf16[64,128]{1,0:T(8,128)(2,1)} %param.17) | copy-start | bytes 49156
  8.8 2.6 %copy-start.6 = (f32[1,16,64]{2,1,0:T(8,128)}, f32[1,16,64]{2,1,0:T(8,128)S(1)}, u32[]{:S(2)}) copy-start(f32[1,16,64]{2,1,0:T(8,128)S(1)} %reduce_window_sum.11) | copy-start | bytes 12292
  13.2 12.9 %all-to-all-start = ((f32[4,16,2176]{2,1,0:T(8,128)}), f32[4,16,2176]{2,1,0:T(8,128)S(1)}, u32[]{:S(2)}, u32[]{:S(2)}) async-start(f32[4,16,2176]{2,1,0:T(8,128)} %pad_maximum_fusion), calls=%async_computation | async-start | bytes 1114112 | tf_op jit(solution)/shard_map/all_to_all | solution.py:128
  28.2 31.1 %copy-start.8 = (bf16[64,128]{1,0:T(8,128)(2,1)S(1)}, bf16[64,128]{1,0:T(8,128)(2,1)}, u32[]{:S(2)}) copy-start(bf16[64,128]{1,0:T(8,128)(2,1)} %param.18) | copy-start | bytes 49156
  29.4 8.1 %all-to-all-start.1 = ((f32[4,16,640]{2,1,0:T(8,128)}), f32[4,16,640]{2,1,0:T(8,128)S(1)}, u32[]{:S(2)}, u32[]{:S(2)}) async-start(f32[4,16,640]{2,1,0:T(8,128)} %copy.127), calls=%async_computation.1 | async-start | bytes 327680 | tf_op jit(solution)/shard_map/all_to_all | solution.py:128
  54.5 8.9 %all-to-all-start.2 = ((f32[4,16,512]{2,1,0:T(8,128)}), f32[4,16,512]{2,1,0:T(8,128)}, u32[]{:S(2)}, u32[]{:S(2)}) async-start(f32[4,16,512]{2,1,0:T(8,128)} %pad_maximum_fusion.3), calls=%async_computation.2 | async-start | bytes 262144 | tf_op jit(solution)/shard_map/all_to_all | solution.py:144
  69.3 3.2 %copy-start.2 = (f32[1,16,2048]{1,2,0:T(8,128)S(1)}, f32[1,16,2048]{1,2,0:T(8,128)}, u32[]{:S(2)}) copy-start(f32[1,16,2048]{1,2,0:T(8,128)} %get-tuple-element.424) | copy-start | bytes 393220
  69.3 3.5 %copy-start.1 = (f32[1,16,2048]{1,2,0:T(8,128)S(1)}, f32[1,16,2048]{1,2,0:T(8,128)}, u32[]{:S(2)}) copy-start(f32[1,16,2048]{1,2,0:T(8,128)} %get-tuple-element.425) | copy-start | bytes 393220
  72.5 5.6 %copy-start.3 = (bf16[64,1024]{1,0:T(8,128)(2,1)S(1)}, bf16[64,1024]{1,0:T(8,128)(2,1)}, u32[]{:S(2)}) copy-start(bf16[64,1024]{1,0:T(8,128)(2,1)} %param.15) | copy-start | bytes 393220
  73.9 10.4 %all-to-all-start.3 = ((f32[4,16,2048]{2,1,0:T(8,128)}), f32[4,16,2048]{2,1,0:T(8,128)S(1)}, u32[]{:S(2)}, u32[]{:S(2)}) async-start(f32[4,16,2048]{2,1,0:T(8,128)} %pad_maximum_fusion.1), calls=%async_computation.3 | async-start | bytes 1048576 | tf_op jit(solution)/shard_map/all_to_all | solution.py:144
  77.4 99.0 %all-gather.6.cloned.1.call-start = ((), (), s32[]{:S(2)}) async-start(), calls=%async_computation.5 | async-start | bytes 2621440 | tf_op jit(solution)/shard_map/all_gather | solution.py:186
  78.2 3.0 %copy-start.7 = (f32[1,16,64]{2,1,0:T(8,128)S(1)}, f32[1,16,64]{2,1,0:T(8,128)}, u32[]{:S(2)}) copy-start(f32[1,16,64]{2,1,0:T(8,128)} %copy-done.6) | copy-start | bytes 12292
  78.2 3.0 %copy-start.11 = (f32[64,64]{1,0:T(8,128)S(1)}, f32[64,64]{1,0:T(8,128)}, u32[]{:S(2)}) copy-start(f32[64,64]{1,0:T(8,128)} %fusion.50) | copy-start | bytes 49156
  78.2 3.0 %copy-start.13 = (pred[64,64]{1,0:T(8,128)(4,1)S(1)}, pred[64,64]{1,0:T(8,128)(4,1)}, u32[]{:S(2)}) copy-start(pred[64,64]{1,0:T(8,128)(4,1)} %iota_compare_fusion) | copy-start | bytes 12292
  78.3 3.0 %copy-start.14 = (f32[16,64]{1,0:T(8,128)S(1)}, f32[16,64]{1,0:T(8,128)}, u32[]{:S(2)}) copy-start(f32[16,64]{1,0:T(8,128)} %get-tuple-element.431) | copy-start | bytes 12292
  81.2 5.6 %copy-start.9 = (bf16[64,128]{1,0:T(8,128)(2,1)S(1)}, bf16[64,128]{1,0:T(8,128)(2,1)}, u32[]{:S(2)}) copy-start(bf16[64,128]{1,0:T(8,128)(2,1)} %param.18) | copy-start | bytes 49156
  81.2 5.6 %copy-start.16 = (f32[16]{0:T(128)S(1)}, f32[16]{0:T(128)}, u32[]{:S(2)}) copy-start(f32[16]{0:T(128)} %param.21) | copy-start | bytes 196
  86.8 2.6 %copy-start.5 = (bf16[64,1024]{1,0:T(8,128)(2,1)S(1)}, bf16[64,1024]{1,0:T(8,128)(2,1)}, u32[]{:S(2)}) copy-start(bf16[64,1024]{1,0:T(8,128)(2,1)} %param.16) | copy-start | bytes 393220
  86.8 2.8 %copy-start.15 = (f32[1024]{0:T(1024)S(1)}, f32[1024]{0:T(1024)}, u32[]{:S(2)}) copy-start(f32[1024]{0:T(1024)} %param.22) | copy-start | bytes 12292
  89.4 19.3 %copy-start.12 = (bf16[64,128]{1,0:T(8,128)(2,1)S(1)}, bf16[64,128]{1,0:T(8,128)(2,1)}, u32[]{:S(2)}) copy-start(bf16[64,128]{1,0:T(8,128)(2,1)} %param.25) | copy-start | bytes 49156
  89.7 46.9 %copy-start.4 = (bf16[64,1024]{1,0:T(8,128)(2,1)}, bf16[64,1024]{1,0:T(8,128)(2,1)S(1)}, u32[]{:S(2)}) copy-start(bf16[64,1024]{1,0:T(8,128)(2,1)S(1)} %multiply_convert_fusion) | copy-start | bytes 393220
  89.7 46.9 %copy-start.10 = (bf16[64,512]{1,0:T(8,128)(2,1)S(1)}, bf16[64,512]{1,0:T(8,128)(2,1)}, u32[]{:S(2)}) copy-start(bf16[64,512]{1,0:T(8,128)(2,1)} %param.24) | copy-start | bytes 196612
Sparse Core Ops, SparseCore 0:
  136.7 39.6 all-gather.5

commit v3 on v2

--- a/solution.py
+++ b/solution.py
@@ -93,6 +93,12 @@
     return lax.cond(key_first <= jnp.max(query_pos), update, unchanged, running)
 
 
+def gather_by_exchange(block, axis):
+    count = lax.axis_size(axis)
+    repeated = jnp.broadcast_to(block[None], (count,) + block.shape)
+    return lax.all_to_all(repeated, axis, 0, 0, tiled=True)
+
+
 def masked_weights(decays, upto):
     count = decays.shape[0]
     earlier = jnp.arange(count)[:, None]
@@ -111,7 +117,7 @@
 
 def entering_top(axis, decay, state):
     width = state.shape[1]
-    gathered = lax.all_gather(pack_decay(state, decay), axis)
+    gathered = gather_by_exchange(pack_decay(state, decay), axis)
     weights = masked_weights(gathered[:, :, width], lax.axis_index(axis))
     return jnp.sum(weights[:, :, None] * gathered[:, :, :width], axis=0)
 
@@ -183,7 +189,7 @@
     key_heads = jnp.transpose(keys.reshape(tokens_here, kv_here, HEAD_DIM), (1, 0, 2))
     pair = jnp.stack([key_heads, values])
     for axis in SEQ_AXES[::-1]:
-        pair = lax.all_gather(pair, axis)
+        pair = gather_by_exchange(pair, axis)
     all_pairs = jnp.transpose(pair, (3, 4, 2, 1, 0, 5, 6)).reshape(2, kv_here, -1, HEAD_DIM)
     key_portion = all_pairs[0]
     value_portion = all_pairs[1]

time: 209 us -> 196 us (0.938)
  the two profiles are of different devices: /device:TPU:481 before, /device:TPU:480 now
where the time goes in v3:
time: 196 us; the launch traced here: 195 us
  blocking collectives  55.9 us (29%)
  waiting for transfers between devices  45.4 us (23%)
  starting transfers between devices  28.8 us (15%)
  local copies, waits for them, and re-layouts  25.1 us (13%)
  other arithmetic  13.9 us (7%)
  matrix products  13.2 us (7%)
  loops' own time  11.4 us (6%)
    all_to_all x2, blocking collectives, gather_by_exchange(): return lax.all_to_all(repeated, axis, 0, 0, tiled=True)  35.3 us
    all_to_all x2, waiting for transfers between devices, gather_by_exchange(): return lax.all_to_all(repeated, axis, 0, 0, tiled=True)  32.8 us
    all_to_all x2, starting transfers between devices, gather_by_exchange(): return lax.all_to_all(repeated, axis, 0, 0, tiled=True)  13.9 us
    all_to_all x1, blocking collectives, per_device(): exchanged = lax.all_to_all(partials, 'tp', 0, 0, tiled=True)  11.8 us
    all_to_all x2, starting transfers between devices, entering_state(): returned = lax.all_to_all(outgoing, axis, 0, 0, tiled=True)  10.5 us
    another operation x1, loops' own time, per_device(): finished = lax.fori_loop(0, length // block_len, one_block, initial)  10.4 us
    all_to_all x1, waiting for transfers between devices, entering_state(): received = lax.all_to_all(packed, axis, 0, 0, tiled=True)  9.76 us
    all_to_all x1, blocking collectives, entering_state(): received = lax.all_to_all(packed, axis, 0, 0, tiled=True)  8.75 us
  transfers between devices with their start and end apart: 5, of which 4 were waited for; matrix products, arithmetic and copies ran while one was open for 5% of the time, Pallas kernels for 0%

profile of v3, /device:TPU:480, one launch (start us, length us, event | category | flops | bytes accessed | tf_op | source)
XLA Modules:
  0.0 195.0 jit_solution(13276373374397618836)
XLA Ops:
  2.5 1.3 multiply_bitcast_fusion
  6.7 4.3 %all-to-all-start = ((f32[4,16,2176]{2,1,0:T(8,128)}), f32[4,16,2176]{2,1,0:T(8,128)S(1)}, u32[]{:S(2)}, u32[]{:S(2)}) async-start(f32[4,16,2176]{2,1,0:T(8,128)} %pad_maximum_fusion), calls=%async_computation | async-start | bytes 1114112 | tf_op jit(solution)/shard_map/all_to_all | solution.py:134
  11.1 9.8 %all-to-all-done = f32[4,16,2176]{2,1,0:T(8,128)S(1)} async-done(((f32[4,16,2176]{2,1,0:T(8,128)}), f32[4,16,2176]{2,1,0:T(8,128)S(1)}, u32[]{:S(2)}, u32[]{:S(2)}) %all-to-all-start) | async-done | bytes 557088 | tf_op jit(solution)/shard_map/all_to_all | solution.py:134
  23.4 8.7 %all_to_all.45 = f32[4,16,640]{2,1,0:T(8,128)S(1)} all-to-all(f32[4,16,640]{2,1,0:T(8,128)S(1)} %copy.123), channel_id=1, replica_groups=mesh['zh'=4,'zl'=4,'sx'=4,'tp'=8] {'zl'}, dimensions={0} | all-to-all | bytes 327680 | tf_op jit(solution)/shard_map/all_to_all | solution.py:134
  33.3 10.2 %all-to-all-start.2 = ((f32[4,16,640]{2,1,0:T(8,128)}), f32[4,16,640]{2,1,0:T(8,128)S(1)}, u32[]{:S(2)}, u32[]{:S(2)}) async-start(f32[4,16,640]{2,1,0:T(8,128)} %broadcast_in_dim.399), calls=%async_computation.2 | async-start | bytes 327680 | tf_op jit(solution)/shard_map/all_to_all | solution.py:99
  44.0 8.1 %all-to-all-done.2 = f32[4,16,640]{2,1,0:T(8,128)S(1)} async-done(((f32[4,16,640]{2,1,0:T(8,128)}), f32[4,16,640]{2,1,0:T(8,128)S(1)}, u32[]{:S(2)}, u32[]{:S(2)}) %all-to-all-start.2) | async-done | bytes 163872 | tf_op jit(solution)/shard_map/all_to_all | solution.py:99
  53.7 7.1 %all-to-all-start.3 = ((f32[4,16,512]{2,1,0:T(8,128)}), f32[4,16,512]{2,1,0:T(8,128)}, u32[]{:S(2)}, u32[]{:S(2)}) async-start(f32[4,16,512]{2,1,0:T(8,128)} %pad_maximum_fusion.3), calls=%async_computation.3 | async-start | bytes 262144 | tf_op jit(solution)/shard_map/all_to_all | solution.py:150
  63.4 1.3 copy.162
  64.8 2.2 %copy.134 = f32[16,4,512]{0,2,1:T(8,128)} copy(f32[16,4,512]{2,0,1:T(8,128)} %bitcast.24) | data formatting | bytes 262144 | tf_op jit(solution)/shard_map/transpose | solution.py:151
  67.0 3.7 %bitcast_add_fusion.3 = (f32[1,16,2048]{1,2,0:T(8,128)}, f32[1,16,2048]{1,2,0:T(8,128)}, f32[1,16,2048]{1,2,0:T(8,128)}, f32[1,16,2048]{1,2,0:T(8,128)}) fusion(f32[16,2048]{0,1:T(8,128)S(1)} %copy.159, f32[16,4,512]{0,2,1:T(8,128)} %copy.134, f32[16,2048]{0,1:T(8,128)S(1)} %copy.160, f32[16]{0:T(128)} %get-tuple-element.382, f32[16,2048]{0,1:T(8,128)S(1)} %copy.161, ...), kind=kLoop, calls=%fused_computation.30 | loop fusion | flops 229376 | bytes 1179840 | tf_op jit(solution)/shard_map/add | solution.py:148
  70.7 1.7 copy.139
  72.3 1.5 copy.140
  75.3 3.5 %all-to-all-start.4 = ((f32[4,16,2048]{2,1,0:T(8,128)}), f32[4,16,2048]{2,1,0:T(8,128)S(1)}, u32[]{:S(2)}, u32[]{:S(2)}) async-start(f32[4,16,2048]{2,1,0:T(8,128)} %pad_maximum_fusion.1), calls=%async_computation.4 | async-start | bytes 1048576 | tf_op jit(solution)/shard_map/all_to_all | solution.py:150
  79.6 2.9 %copy.155 = bf16[1024,1024]{1,0:T(8,128)(2,1)S(1)} copy(bf16[1024,1024]{0,1:T(8,128)(2,1)} %bitcast.147) | data formatting | bytes 4194304 | tf_op jit(solution)/shard_map/dot_general | solution.py:182
  82.6 1.5 convolution_bitcast_fusion.2
  84.0 2.8 %all-to-all-done.4 = f32[4,16,2048]{2,1,0:T(8,128)S(1)} async-done(((f32[4,16,2048]{2,1,0:T(8,128)}), f32[4,16,2048]{2,1,0:T(8,128)S(1)}, u32[]{:S(2)}, u32[]{:S(2)}) %all-to-all-start.4) | async-done | bytes 524320 | tf_op jit(solution)/shard_map/all_to_all | solution.py:150
  89.4 2.0 %fusion.18 = f32[64,1,16,64]{3,0,2,1:T(8,128)S(1)} fusion(f32[64,1,16,64]{3,0,2,1:T(8,128)} %convolution_bitcast_fusion.2, f32[16,64,128]{2,1,0:T(8,128)S(1)} %reshape.808, f32[64,1,16,64]{3,2,0,1:T(8,128)S(1)} %reshape.817, f32[16]{0:T(128)S(1)} %copy-done.16, f32[64,16]{0,1:T(8,128)S(1)} %exponential_bitcast_fusion, bf16[64,128]{1,0:T(8,128)(2,1)S(1)} %copy-done.9), kind=kOutput, calls=%fused_computation.25 | convolution fusion | flops 100925440 | bytes 1331264 | tf_op jit(solution)/shard_map/tgn,gkpn->tgkp/dot_general | solution.py:35
  93.0 11.8 %all_to_all.46 = f32[8,64,128]{2,1,0:T(8,128)S(1)} all-to-all(f32[8,64,128]{2,1,0:T(8,128)S(1)} %convolution_bitcast_fusion.3), channel_id=1, replica_groups=mesh['zh'=4,'zl'=4,'sx'=4,'tp'=8] {'tp'}, dimensions={0} | all-to-all | bytes 524288 | tf_op jit(solution)/shard_map/all_to_all | solution.py:186
  104.9 19.6 %all_to_all.47 = bf16[4,2,1,64,128]{4,3,1,2,0:T(8,128)(2,1)S(1)} all-to-all(bf16[4,2,1,64,128]{4,3,1,2,0:T(8,128)(2,1)S(1)} %broadcast_in_dim.412), channel_id=1, replica_groups=mesh['zh'=4,'zl'=4,'sx'=4,'tp'=8] {'zh'}, dimensions={0} | all-to-all | bytes 262144 | tf_op jit(solution)/shard_map/all_to_all | solution.py:99
  124.6 15.8 %all_to_all.48 = bf16[4,4,2,1,64,128]{5,4,1,2,3,0:T(8,128)(2,1)S(1)} all-to-all(bf16[4,4,2,1,64,128]{5,4,1,2,3,0:T(8,128)(2,1)S(1)} %broadcast_in_dim.414), channel_id=1, replica_groups=mesh['zh'=4,'zl'=4,'sx'=4,'tp'=8] {'zl'}, dimensions={0} | all-to-all | bytes 1048576 | tf_op jit(solution)/shard_map/all_to_all | solution.py:99
  140.4 1.9 broadcast_in_dim.416
  142.3 3.7 %all-to-all-start.8 = ((bf16[4,4,4,2,1,64,128]{6,5,1,2,4,3,0:T(8,128)(2,1)}), bf16[4,4,4,2,1,64,128]{6,5,1,2,4,3,0:T(8,128)(2,1)S(1)}, u32[]{:S(2)}, u32[]{:S(2)}) async-start(bf16[4,4,4,2,1,64,128]{6,5,1,2,4,3,0:T(8,128)(2,1)} %broadcast_in_dim.416), calls=%async_computation.8 | async-start | bytes 4194304 | tf_op jit(solution)/shard_map/all_to_all | solution.py:99
  146.8 24.7 %all-to-all-done.8 = bf16[4,4,4,2,1,64,128]{6,5,1,2,4,3,0:T(8,128)(2,1)S(1)} async-done(((bf16[4,4,4,2,1,64,128]{6,5,1,2,4,3,0:T(8,128)(2,1)}), bf16[4,4,4,2,1,64,128]{6,5,1,2,4,3,0:T(8,128)(2,1)S(1)}, u32[]{:S(2)}, u32[]{:S(2)}) %all-to-all-start.8) | async-done | bytes 2097184 | tf_op jit(solution)/shard_map/all_to_all | solution.py:99
  171.9 22.2 %while.20 = (s32[]{:T(128)}, f32[1,256]{1,0:T(1,128)S(1)}, f32[1,256]{1,0:T(1,128)S(1)}, f32[1,256,128]{2,1,0:T(8,128)S(1)}, s32[]{:T(128)}, /*index=5*/bf16[1,4...) while((s32[]{:T(128)}, f32[1,256]{1,0:T(1,128)S(1)}, ...), condition=%wide.region_37.38_spmd.clone, body=%wide.region_32.37_spmd.clone.sunk | while | flops 34145032 | bytes 1270325 | solution.py:229
  (297 shorter events, 44.1 us)
Async XLA Ops:
  0.6 4.3 %copy-start = (bf16[64,128]{1,0:T(8,128)(2,1)S(1)}, bf16[64,128]{1,0:T(8,128)(2,1)}, u32[]{:S(2)}) copy-start(bf16[64,128]{1,0:T(8,128)(2,1)} %param.17) | copy-start | bytes 49156
  2.3 2.6 %copy-start.6 = (f32[1,16,64]{2,1,0:T(8,128)}, f32[1,16,64]{2,1,0:T(8,128)S(1)}, u32[]{:S(2)}) copy-start(f32[1,16,64]{2,1,0:T(8,128)S(1)} %reduce_window_sum.11) | copy-start | bytes 12292
  6.7 14.1 %all-to-all-start = ((f32[4,16,2176]{2,1,0:T(8,128)}), f32[4,16,2176]{2,1,0:T(8,128)S(1)}, u32[]{:S(2)}, u32[]{:S(2)}) async-start(f32[4,16,2176]{2,1,0:T(8,128)} %pad_maximum_fusion), calls=%async_computation | async-start | bytes 1114112 | tf_op jit(solution)/shard_map/all_to_all | solution.py:134
  33.3 18.8 %all-to-all-start.2 = ((f32[4,16,640]{2,1,0:T(8,128)}), f32[4,16,640]{2,1,0:T(8,128)S(1)}, u32[]{:S(2)}, u32[]{:S(2)}) async-start(f32[4,16,640]{2,1,0:T(8,128)} %broadcast_in_dim.399), calls=%async_computation.2 | async-start | bytes 327680 | tf_op jit(solution)/shard_map/all_to_all | solution.py:99
  52.5 8.2 %copy-start.8 = (bf16[64,128]{1,0:T(8,128)(2,1)S(1)}, bf16[64,128]{1,0:T(8,128)(2,1)}, u32[]{:S(2)}) copy-start(bf16[64,128]{1,0:T(8,128)(2,1)} %param.18) | copy-start | bytes 49156
  53.7 11.1 %all-to-all-start.3 = ((f32[4,16,512]{2,1,0:T(8,128)}), f32[4,16,512]{2,1,0:T(8,128)}, u32[]{:S(2)}, u32[]{:S(2)}) async-start(f32[4,16,512]{2,1,0:T(8,128)} %pad_maximum_fusion.3), calls=%async_computation.3 | async-start | bytes 262144 | tf_op jit(solution)/shard_map/all_to_all | solution.py:150
  70.7 3.2 %copy-start.2 = (f32[1,16,2048]{1,2,0:T(8,128)S(1)}, f32[1,16,2048]{1,2,0:T(8,128)}, u32[]{:S(2)}) copy-start(f32[1,16,2048]{1,2,0:T(8,128)} %get-tuple-element.424) | copy-start | bytes 393220
  70.7 3.5 %copy-start.1 = (f32[1,16,2048]{1,2,0:T(8,128)S(1)}, f32[1,16,2048]{1,2,0:T(8,128)}, u32[]{:S(2)}) copy-start(f32[1,16,2048]{1,2,0:T(8,128)} %get-tuple-element.425) | copy-start | bytes 393220
  73.9 5.6 %copy-start.3 = (bf16[64,1024]{1,0:T(8,128)(2,1)S(1)}, bf16[64,1024]{1,0:T(8,128)(2,1)}, u32[]{:S(2)}) copy-start(bf16[64,1024]{1,0:T(8,128)(2,1)} %param.15) | copy-start | bytes 393220
  75.3 11.5 %all-to-all-start.4 = ((f32[4,16,2048]{2,1,0:T(8,128)}), f32[4,16,2048]{2,1,0:T(8,128)S(1)}, u32[]{:S(2)}, u32[]{:S(2)}) async-start(f32[4,16,2048]{2,1,0:T(8,128)} %pad_maximum_fusion.1), calls=%async_computation.4 | async-start | bytes 1048576 | tf_op jit(solution)/shard_map/all_to_all | solution.py:150
  79.6 3.0 %copy-start.7 = (f32[1,16,64]{2,1,0:T(8,128)S(1)}, f32[1,16,64]{2,1,0:T(8,128)}, u32[]{:S(2)}) copy-start(f32[1,16,64]{2,1,0:T(8,128)} %copy-done.6) | copy-start | bytes 12292
  79.6 3.0 %copy-start.11 = (f32[64,64]{1,0:T(8,128)S(1)}, f32[64,64]{1,0:T(8,128)}, u32[]{:S(2)}) copy-start(f32[64,64]{1,0:T(8,128)} %fusion.50) | copy-start | bytes 49156
  79.6 3.0 %copy-start.13 = (pred[64,64]{1,0:T(8,128)(4,1)S(1)}, pred[64,64]{1,0:T(8,128)(4,1)}, u32[]{:S(2)}) copy-start(pred[64,64]{1,0:T(8,128)(4,1)} %iota_compare_fusion) | copy-start | bytes 12292
  79.6 3.0 %copy-start.14 = (f32[16,64]{1,0:T(8,128)S(1)}, f32[16,64]{1,0:T(8,128)}, u32[]{:S(2)}) copy-start(f32[16,64]{1,0:T(8,128)} %get-tuple-element.431) | copy-start | bytes 12292
  82.5 6.8 %copy-start.9 = (bf16[64,128]{1,0:T(8,128)(2,1)S(1)}, bf16[64,128]{1,0:T(8,128)(2,1)}, u32[]{:S(2)}) copy-start(bf16[64,128]{1,0:T(8,128)(2,1)} %param.18) | copy-start | bytes 49156
  82.5 6.8 %copy-start.16 = (f32[16]{0:T(128)S(1)}, f32[16]{0:T(128)}, u32[]{:S(2)}) copy-start(f32[16]{0:T(128)} %param.21) | copy-start | bytes 196
  89.4 2.6 %copy-start.5 = (bf16[64,1024]{1,0:T(8,128)(2,1)S(1)}, bf16[64,1024]{1,0:T(8,128)(2,1)}, u32[]{:S(2)}) copy-start(bf16[64,1024]{1,0:T(8,128)(2,1)} %param.16) | copy-start | bytes 393220
  89.4 2.8 %copy-start.15 = (f32[1024]{0:T(1024)S(1)}, f32[1024]{0:T(1024)}, u32[]{:S(2)}) copy-start(f32[1024]{0:T(1024)} %param.22) | copy-start | bytes 12292
  91.9 12.9 %copy-start.12 = (bf16[64,128]{1,0:T(8,128)(2,1)S(1)}, bf16[64,128]{1,0:T(8,128)(2,1)}, u32[]{:S(2)}) copy-start(bf16[64,128]{1,0:T(8,128)(2,1)} %param.25) | copy-start | bytes 49156
  92.2 32.3 %copy-start.4 = (bf16[64,1024]{1,0:T(8,128)(2,1)}, bf16[64,1024]{1,0:T(8,128)(2,1)S(1)}, u32[]{:S(2)}) copy-start(bf16[64,1024]{1,0:T(8,128)(2,1)S(1)} %multiply_convert_fusion) | copy-start | bytes 393220
  142.3 3.8 %copy-start.10 = (bf16[64,512]{1,0:T(8,128)(2,1)S(1)}, bf16[64,512]{1,0:T(8,128)(2,1)}, u32[]{:S(2)}) copy-start(bf16[64,512]{1,0:T(8,128)(2,1)} %param.24) | copy-start | bytes 196612
  142.3 29.2 %all-to-all-start.8 = ((bf16[4,4,4,2,1,64,128]{6,5,1,2,4,3,0:T(8,128)(2,1)}), bf16[4,4,4,2,1,64,128]{6,5,1,2,4,3,0:T(8,128)(2,1)S(1)}, u32[]{:S(2)}, u32[]{:S(2)}) async-start(bf16[4,4,4,2,1,64,128]{6,5,1,2,4,3,0:T(8,128)(2,1)} %broadcast_in_dim.416), calls=%async_computation.8 | async-start | bytes 4194304 | tf_op jit(solution)/shard_map/all_to_all | solution.py:99

commit v4 on v3

--- a/solution.py
+++ b/solution.py
@@ -10,7 +10,8 @@
 QHEADS = 32
 KVHEADS = 8
 HEAD_DIM = 128
-SEQ_AXES = ("sx", "zl", "zh")
+SEQ_AXES = (("zl", "sx"), "zh")
+ROWS = ("zh", "zl", "sx")
 
 
 highest = lax.Precision.HIGHEST
@@ -188,12 +189,11 @@
     values = jnp.transpose(values.reshape(tokens_here, kv_here, HEAD_DIM), (1, 0, 2))
     key_heads = jnp.transpose(keys.reshape(tokens_here, kv_here, HEAD_DIM), (1, 0, 2))
     pair = jnp.stack([key_heads, values])
-    for axis in SEQ_AXES[::-1]:
-        pair = gather_by_exchange(pair, axis)
-    all_pairs = jnp.transpose(pair, (3, 4, 2, 1, 0, 5, 6)).reshape(2, kv_here, -1, HEAD_DIM)
+    pair = gather_by_exchange(gather_by_exchange(pair, "zh"), ("zl", "sx"))
+    all_pairs = jnp.transpose(pair, (2, 3, 1, 0, 4, 5)).reshape(2, kv_here, -1, HEAD_DIM)
     key_portion = all_pairs[0]
     value_portion = all_pairs[1]
-    my_index = lax.axis_index(SEQ_AXES[::-1])
+    my_index = lax.axis_index(ROWS)
     query_sets = [
         (
             query_layout(queries, kv_here, per_kv),
@@ -236,9 +236,9 @@
     seq_count = mesh.shape["seq"]
     split = Mesh(
         mesh.devices.reshape(seq_count // 16, 4, 4, mesh.shape["tp"]),
-        SEQ_AXES[::-1] + ("tp",),
-    )
-    rows = SEQ_AXES[::-1]
+        ROWS + ("tp",),
+    )
+    rows = ROWS
     placed = (
         P(rows, "tp"),
         P(rows, "tp"),

time: 196 us -> 221 us (1.13)
  the two profiles are of different devices: /device:TPU:480 before, /device:TPU:448 now
where the time goes in v4:
time: 221 us; the launch traced here: 219 us
  waiting for transfers between devices  76.3 us (35%)
  local copies, waits for them, and re-layouts  46.1 us (21%)
  blocking collectives  30.2 us (14%)
  starting transfers between devices  27.5 us (12%)
  other arithmetic  14 us (6%)
  matrix products  12.1 us (5%)
  loops' own time  11.4 us (5%)
    all_to_all x2, waiting for transfers between devices, gather_by_exchange(): return lax.all_to_all(repeated, axis, 0, 0, tiled=True)  51 us
    all_to_all x1, blocking collectives, gather_by_exchange(): return lax.all_to_all(repeated, axis, 0, 0, tiled=True)  18.4 us
    all_to_all x1, waiting for transfers between devices, entering_state(): received = lax.all_to_all(packed, axis, 0, 0, tiled=True)  16.9 us
    add x16, local copies, waits for them, and re-layouts, entering_state(): decay_before[upto][:, None] * group_in + prefixes[upto]  16.8 us
    unnamed x62, local copies, waits for them, and re-layouts  16 us
    all_to_all x2, starting transfers between devices, gather_by_exchange(): return lax.all_to_all(repeated, axis, 0, 0, tiled=True)  15.4 us
    all_to_all x1, blocking collectives, per_device(): exchanged = lax.all_to_all(partials, 'tp', 0, 0, tiled=True)  11.8 us
    another operation x1, loops' own time, per_device(): finished = lax.fori_loop(0, length // block_len, one_block, initial)  10.4 us
  transfers between devices with their start and end apart: 4, of which 4 were waited for; matrix products, arithmetic and copies ran while one was open for 5% of the time, Pallas kernels for 0%

profile of v4, /device:TPU:448, one launch (start us, length us, event | category | flops | bytes accessed | tf_op | source)
XLA Modules:
  0.0 219.0 jit_solution(4716608759761863122)
XLA Ops:
  2.9 1.3 multiply_bitcast_fusion
  7.1 7.1 %all-to-all-start = ((f32[16,16,640]{2,1,0:T(8,128)}), f32[16,16,640]{2,1,0:T(8,128)S(1)}, u32[]{:S(2)}, u32[]{:S(2)}) async-start(f32[16,16,640]{2,1,0:T(8,128)} %pad_maximum_fusion), calls=%async_computation | async-start | bytes 1310720 | tf_op jit(solution)/shard_map/all_to_all | solution.py:135
  14.6 16.9 %all-to-all-done = f32[16,16,640]{2,1,0:T(8,128)S(1)} async-done(((f32[16,16,640]{2,1,0:T(8,128)}), f32[16,16,640]{2,1,0:T(8,128)S(1)}, u32[]{:S(2)}, u32[]{:S(2)}) %all-to-all-start) | async-done | bytes 655392 | tf_op jit(solution)/shard_map/all_to_all | solution.py:135
  35.7 10.2 %all-to-all-start.1 = ((f32[4,16,640]{2,1,0:T(8,128)}), f32[4,16,640]{2,1,0:T(8,128)S(1)}, u32[]{:S(2)}, u32[]{:S(2)}) async-start(f32[4,16,640]{2,1,0:T(8,128)} %broadcast_in_dim.603), calls=%async_computation.1 | async-start | bytes 327680 | tf_op jit(solution)/shard_map/all_to_all | solution.py:100
  51.6 4.8 %all-to-all-done.1 = f32[4,16,640]{2,1,0:T(8,128)S(1)} async-done(((f32[4,16,640]{2,1,0:T(8,128)}), f32[4,16,640]{2,1,0:T(8,128)S(1)}, u32[]{:S(2)}, u32[]{:S(2)}) %all-to-all-start.1) | async-done | bytes 163872 | tf_op jit(solution)/shard_map/all_to_all | solution.py:100
  56.8 2.6 %bitcast_add_fusion.1 = (f32[1,16,512]{1,2,0:T(8,128)}, f32[1,16,512]{1,2,0:T(8,128)}, f32[1,16,512]{1,2,0:T(8,128)}, f32[1,16,512]{1,2,0:T(8,128)}, f32[1,16,51...) fusion(f32[16,512]{0,1:T(8,128)S(1)} %copy.199, f32[16,512]{0,1:T(8,128)S(1)} %copy.184, ...), kind=kLoop, calls=%fused_computation.62 | loop fusion | flops 106496 | bytes 491904 | tf_op jit(solution)/shard_map/add | solution.py:149
  60.4 1.7 copy.166
  62.1 1.7 copy.167
  66.9 1.7 copy.157
  68.6 2.0 bitcast_add_fusion
  72.7 1.1 copy.159
  87.9 5.0 %all-to-all-start.2 = ((f32[16,16,512]{2,1,0:T(8,128)}), f32[16,16,512]{2,1,0:T(8,128)S(1)}, u32[]{:S(2)}, u32[]{:S(2)}) async-start(f32[16,16,512]{2,1,0:T(8,128)} %constant_dynamic-update-slice_fusion), calls=%async_computation.2 | async-start | bytes 1048576 | tf_op jit(solution)/shard_map/all_to_all | solution.py:151
  93.1 2.9 %copy.183 = bf16[1024,1024]{1,0:T(8,128)(2,1)S(1)} copy(bf16[1024,1024]{0,1:T(8,128)(2,1)} %bitcast.200) | data formatting | bytes 4194304 | tf_op jit(solution)/shard_map/dot_general | solution.py:183
  96.2 1.5 convolution_bitcast_fusion.2
  97.6 8.5 %all-to-all-done.2 = f32[16,16,512]{2,1,0:T(8,128)S(1)} async-done(((f32[16,16,512]{2,1,0:T(8,128)}), f32[16,16,512]{2,1,0:T(8,128)S(1)}, u32[]{:S(2)}, u32[]{:S(2)}) %all-to-all-start.2) | async-done | bytes 524320 | tf_op jit(solution)/shard_map/all_to_all | solution.py:151
  106.1 1.1 copy.173
  107.2 1.1 reshape.1562
  108.3 2.0 fusion.18
  112.0 11.8 %all_to_all.30 = f32[8,64,128]{2,1,0:T(8,128)S(1)} all-to-all(f32[8,64,128]{2,1,0:T(8,128)S(1)} %convolution_bitcast_fusion.3), channel_id=1, replica_groups=mesh['zh'=4,'zl'=4,'sx'=4,'tp'=8] {'tp'}, dimensions={0} | all-to-all | bytes 524288 | tf_op jit(solution)/shard_map/all_to_all | solution.py:187
  123.9 18.4 %all_to_all.31 = bf16[4,2,1,64,128]{4,3,1,2,0:T(8,128)(2,1)S(1)} all-to-all(bf16[4,2,1,64,128]{4,3,1,2,0:T(8,128)(2,1)S(1)} %broadcast_in_dim.642), channel_id=1, replica_groups=mesh['zh'=4,'zl'=4,'sx'=4,'tp'=8] {'zh'}, dimensions={0} | all-to-all | bytes 262144 | tf_op jit(solution)/shard_map/all_to_all | solution.py:100
  142.2 1.9 broadcast_in_dim.644
  144.1 5.2 %all-to-all-start.5 = ((bf16[16,4,2,1,64,128]{5,4,1,3,2,0:T(8,128)(2,1)}), bf16[16,4,2,1,64,128]{5,4,1,3,2,0:T(8,128)(2,1)S(1)}, u32[]{:S(2)}, u32[]{:S(2)}) async-start(bf16[16,4,2,1,64,128]{5,4,1,3,2,0:T(8,128)(2,1)} %broadcast_in_dim.644), calls=%async_computation.5 | async-start | bytes 4194304 | tf_op jit(solution)/shard_map/all_to_all | solution.py:100
  150.1 46.2 %all-to-all-done.5 = bf16[16,4,2,1,64,128]{5,4,1,3,2,0:T(8,128)(2,1)S(1)} async-done(((bf16[16,4,2,1,64,128]{5,4,1,3,2,0:T(8,128)(2,1)}), bf16[16,4,2,1,64,128]{5,4,1,3,2,0:T(8,128)(2,1)S(1)}, u32[]{:S(2)}, u32[]{:S(2)}) %all-to-all-start.5) | async-done | bytes 2097184 | tf_op jit(solution)/shard_map/all_to_all | solution.py:100
  196.7 21.6 %while.20 = (s32[]{:T(128)}, f32[1,256]{1,0:T(1,128)S(1)}, f32[1,256]{1,0:T(1,128)S(1)}, f32[1,256,128]{2,1,0:T(8,128)S(1)}, s32[]{:T(128)}, /*index=5*/bf16[1,4...) while((s32[]{:T(128)}, f32[1,256]{1,0:T(1,128)S(1)}, ...), condition=%wide.region_60.61_spmd.clone, body=%wide.region_55.60_spmd.clone.sunk | while | flops 34145032 | bytes 1270325 | solution.py:229
  (330 shorter events, 60.9 us)
Async XLA Ops:
  0.6 4.7 %copy-start = (bf16[64,128]{1,0:T(8,128)(2,1)S(1)}, bf16[64,128]{1,0:T(8,128)(2,1)}, u32[]{:S(2)}) copy-start(bf16[64,128]{1,0:T(8,128)(2,1)} %param.17) | copy-start | bytes 49156
  2.3 0.6 copy-start.7
  7.1 24.5 %all-to-all-start = ((f32[16,16,640]{2,1,0:T(8,128)}), f32[16,16,640]{2,1,0:T(8,128)S(1)}, u32[]{:S(2)}, u32[]{:S(2)}) async-start(f32[16,16,640]{2,1,0:T(8,128)} %pad_maximum_fusion), calls=%async_computation | async-start | bytes 1310720 | tf_op jit(solution)/shard_map/all_to_all | solution.py:135
  35.7 20.6 %all-to-all-start.1 = ((f32[4,16,640]{2,1,0:T(8,128)}), f32[4,16,640]{2,1,0:T(8,128)S(1)}, u32[]{:S(2)}, u32[]{:S(2)}) async-start(f32[4,16,640]{2,1,0:T(8,128)} %broadcast_in_dim.603), calls=%async_computation.1 | async-start | bytes 327680 | tf_op jit(solution)/shard_map/all_to_all | solution.py:100
  70.6 7.7 %copy-start.6 = (f32[1,16,512]{2,1,0:T(8,128)S(1)}, f32[1,16,512]{2,1,0:T(8,128)}, u32[]{:S(2)}) copy-start(f32[1,16,512]{2,1,0:T(8,128)} %copy.157) | copy-start | bytes 98308
  70.6 13.1 %copy-start.5 = (f32[1,16,512]{2,1,0:T(8,128)S(1)}, f32[1,16,512]{2,1,0:T(8,128)}, u32[]{:S(2)}) copy-start(f32[1,16,512]{2,1,0:T(8,128)} %copy.166) | copy-start | bytes 98308
  70.6 13.7 %copy-start.4 = (f32[1,16,512]{2,1,0:T(8,128)S(1)}, f32[1,16,512]{2,1,0:T(8,128)}, u32[]{:S(2)}) copy-start(f32[1,16,512]{2,1,0:T(8,128)} %copy.167) | copy-start | bytes 98308
  72.7 20.2 %copy-start.1 = (bf16[64,1024]{1,0:T(8,128)(2,1)S(1)}, bf16[64,1024]{1,0:T(8,128)(2,1)}, u32[]{:S(2)}) copy-start(bf16[64,1024]{1,0:T(8,128)(2,1)} %param.15) | copy-start | bytes 393220
  87.9 18.2 %all-to-all-start.2 = ((f32[16,16,512]{2,1,0:T(8,128)}), f32[16,16,512]{2,1,0:T(8,128)S(1)}, u32[]{:S(2)}, u32[]{:S(2)}) async-start(f32[16,16,512]{2,1,0:T(8,128)} %constant_dynamic-update-slice_fusion), calls=%async_computation.2 | async-start | bytes 1048576 | tf_op jit(solution)/shard_map/all_to_all | solution.py:151
  93.1 2.9 %copy-start.9 = (bf16[64,128]{1,0:T(8,128)(2,1)S(1)}, bf16[64,128]{1,0:T(8,128)(2,1)}, u32[]{:S(2)}) copy-start(bf16[64,128]{1,0:T(8,128)(2,1)} %param.18) | copy-start | bytes 49156
  93.1 3.1 %copy-start.8 = (f32[1,16,64]{2,1,0:T(8,128)S(1)}, f32[1,16,64]{2,1,0:T(8,128)}, u32[]{:S(2)}) copy-start(f32[1,16,64]{2,1,0:T(8,128)} %copy-done.7) | copy-start | bytes 12292
  93.1 3.0 %copy-start.12 = (f32[16,64]{1,0:T(8,128)S(1)}, f32[16,64]{1,0:T(8,128)}, u32[]{:S(2)}) copy-start(f32[16,64]{1,0:T(8,128)} %get-tuple-element.472) | copy-start | bytes 12292
  108.3 2.6 %copy-start.3 = (bf16[64,1024]{1,0:T(8,128)(2,1)S(1)}, bf16[64,1024]{1,0:T(8,128)(2,1)}, u32[]{:S(2)}) copy-start(bf16[64,1024]{1,0:T(8,128)(2,1)} %param.16) | copy-start | bytes 393220
  110.4 0.7 copy-start.13
  110.9 12.9 %copy-start.11 = (bf16[64,128]{1,0:T(8,128)(2,1)S(1)}, bf16[64,128]{1,0:T(8,128)(2,1)}, u32[]{:S(2)}) copy-start(bf16[64,128]{1,0:T(8,128)(2,1)} %param.25) | copy-start | bytes 49156
  111.2 32.9 %copy-start.2 = (bf16[64,1024]{1,0:T(8,128)(2,1)}, bf16[64,1024]{1,0:T(8,128)(2,1)S(1)}, u32[]{:S(2)}) copy-start(bf16[64,1024]{1,0:T(8,128)(2,1)S(1)} %multiply_convert_fusion) | copy-start | bytes 393220
  144.1 5.2 %copy-start.10 = (bf16[64,512]{1,0:T(8,128)(2,1)S(1)}, bf16[64,512]{1,0:T(8,128)(2,1)}, u32[]{:S(2)}) copy-start(bf16[64,512]{1,0:T(8,128)(2,1)} %param.24) | copy-start | bytes 196612
  144.1 52.1 %all-to-all-start.5 = ((bf16[16,4,2,1,64,128]{5,4,1,3,2,0:T(8,128)(2,1)}), bf16[16,4,2,1,64,128]{5,4,1,3,2,0:T(8,128)(2,1)S(1)}, u32[]{:S(2)}, u32[]{:S(2)}) async-start(bf16[16,4,2,1,64,128]{5,4,1,3,2,0:T(8,128)(2,1)} %broadcast_in_dim.644), calls=%async_computation.5 | async-start | bytes 4194304 | tf_op jit(solution)/shard_map/all_to_all | solution.py:100

commit v5 on v3

--- a/solution.py
+++ b/solution.py
@@ -99,6 +99,18 @@
     return lax.all_to_all(repeated, axis, 0, 0, tiled=True)
 
 
+def gather_shifted(block, axis, wrap):
+    count = lax.axis_size(axis)
+    here = lax.axis_index(axis)
+    shifted = [block]
+    for shift in range(1, count):
+        last = count if wrap else count - shift
+        pairs = [(source, (source + shift) % count) for source in range(last)]
+        shifted.append(lax.ppermute(block, axis, pairs))
+    stacked = jnp.stack(shifted)
+    return stacked[(here - jnp.arange(count)) % count]
+
+
 def masked_weights(decays, upto):
     count = decays.shape[0]
     earlier = jnp.arange(count)[:, None]
@@ -117,7 +129,7 @@
 
 def entering_top(axis, decay, state):
     width = state.shape[1]
-    gathered = gather_by_exchange(pack_decay(state, decay), axis)
+    gathered = gather_shifted(pack_decay(state, decay), axis, False)
     weights = masked_weights(gathered[:, :, width], lax.axis_index(axis))
     return jnp.sum(weights[:, :, None] * gathered[:, :, :width], axis=0)
 
@@ -188,8 +200,9 @@
     values = jnp.transpose(values.reshape(tokens_here, kv_here, HEAD_DIM), (1, 0, 2))
     key_heads = jnp.transpose(keys.reshape(tokens_here, kv_here, HEAD_DIM), (1, 0, 2))
     pair = jnp.stack([key_heads, values])
-    for axis in SEQ_AXES[::-1]:
-        pair = gather_by_exchange(pair, axis)
+    pair = gather_shifted(pair, "zh", False)
+    pair = gather_shifted(pair, "zl", True)
+    pair = gather_by_exchange(pair, "sx")
     all_pairs = jnp.transpose(pair, (3, 4, 2, 1, 0, 5, 6)).reshape(2, kv_here, -1, HEAD_DIM)
     key_portion = all_pairs[0]
     value_portion = all_pairs[1]

time: 196 us -> 201 us (1.026)
  blocking collectives: 55.9 us -> 11.8 us
  waiting for transfers between devices: 45.4 us -> 79.2 us
  starting transfers between devices: 28.8 us -> 42.7 us
    all_to_all x3 -> x0, blocking collectives: 44.1 us -> none  [the longest x2 35.3 us: gather_by_exchange(): return lax.all_to_all(repeated, axis, 0, 0, tiled=True)]
    ppermute x0 -> x9, waiting for transfers between devices: none -> 36.7 us  [gather_shifted(): shifted.append(lax.ppermute(block, axis, pairs))]
    ppermute x0 -> x9, starting transfers between devices: none -> 18.3 us  [gather_shifted(): shifted.append(lax.ppermute(block, axis, pairs))]
    all_to_all x2 -> x1, starting transfers between devices: 13.9 us -> 3.74 us  [gather_by_exchange(): return lax.all_to_all(repeated, axis, 0, 0, tiled=True)]
    all_to_all x2 -> x1, waiting for transfers between devices: 32.8 us -> 26 us  [gather_by_exchange(): return lax.all_to_all(repeated, axis, 0, 0, tiled=True)]
    all_to_all x1 -> x2, starting transfers between devices: 4.29 us -> 9.5 us  [entering_state(): received = lax.all_to_all(packed, axis, 0, 0, tiled=True)]
    all_to_all x1 -> x2, waiting for transfers between devices: 9.76 us -> 13.7 us  [entering_state(): received = lax.all_to_all(packed, axis, 0, 0, tiled=True)]
    add x8 -> x4, local copies, waits for them, and re-layouts: 4.23 us -> 3.81 us  [entering_state(): decay_before[upto][:, None] * group_in + prefixes[upto]]
  transfers between devices with their start and end apart: 5 -> 14, of which waited for: 4 -> 11; matrix products, arithmetic and copies ran while one was open for 5% -> 5% of each run, Pallas kernels for 0% -> 0%
where the time goes in v5:
time: 201 us; the launch traced here: 200 us
  waiting for transfers between devices  79.2 us (39%)
  starting transfers between devices  42.7 us (21%)
  local copies, waits for them, and re-layouts  25.9 us (13%)
  other arithmetic  14 us (7%)
  matrix products  13.2 us (7%)
  blocking collectives  11.8 us (6%)
  loops' own time  11.4 us (6%)
    ppermute x9, waiting for transfers between devices, gather_shifted(): shifted.append(lax.ppermute(block, axis, pairs))  36.7 us
    all_to_all x1, waiting for transfers between devices, gather_by_exchange(): return lax.all_to_all(repeated, axis, 0, 0, tiled=True)  26 us
    ppermute x9, starting transfers between devices, gather_shifted(): shifted.append(lax.ppermute(block, axis, pairs))  18.3 us
    all_to_all x2, waiting for transfers between devices, entering_state(): received = lax.all_to_all(packed, axis, 0, 0, tiled=True)  13.7 us
    all_to_all x1, blocking collectives, per_device(): exchanged = lax.all_to_all(partials, 'tp', 0, 0, tiled=True)  11.8 us
    all_to_all x2, starting transfers between devices, entering_state(): returned = lax.all_to_all(outgoing, axis, 0, 0, tiled=True)  11.2 us
    another operation x1, loops' own time, per_device(): finished = lax.fori_loop(0, length // block_len, one_block, initial)  10.4 us
    all_to_all x2, starting transfers between devices, entering_state(): received = lax.all_to_all(packed, axis, 0, 0, tiled=True)  9.5 us
  transfers between devices with their start and end apart: 14, of which 11 were waited for; matrix products, arithmetic and copies ran while one was open for 5% of the time, Pallas kernels for 0%

profile of v5, /device:TPU:480, one launch (start us, length us, event | category | flops | bytes accessed | tf_op | source)
XLA Modules:
  0.0 199.5 jit_solution(6096338413482233542)
XLA Ops:
  6.7 4.3 %all-to-all-start = ((f32[4,16,2176]{2,1,0:T(8,128)}), f32[4,16,2176]{2,1,0:T(8,128)S(1)}, u32[]{:S(2)}, u32[]{:S(2)}) async-start(f32[4,16,2176]{2,1,0:T(8,128)} %pad_maximum_fusion), calls=%async_computation | async-start | bytes 1114112 | tf_op jit(solution)/shard_map/all_to_all | solution.py:146
  11.1 9.8 %all-to-all-done = f32[4,16,2176]{2,1,0:T(8,128)S(1)} async-done(((f32[4,16,2176]{2,1,0:T(8,128)}), f32[4,16,2176]{2,1,0:T(8,128)S(1)}, u32[]{:S(2)}, u32[]{:S(2)}) %all-to-all-start) | async-done | bytes 557088 | tf_op jit(solution)/shard_map/all_to_all | solution.py:146
  24.0 5.2 %all-to-all-start.1 = ((f32[4,16,640]{2,1,0:T(8,128)}), f32[4,16,640]{2,1,0:T(8,128)S(1)}, u32[]{:S(2)}, u32[]{:S(2)}) async-start(f32[4,16,640]{2,1,0:T(8,128)} %copy.133), calls=%async_computation.1 | async-start | bytes 327680 | tf_op jit(solution)/shard_map/all_to_all | solution.py:146
  29.2 3.9 %all-to-all-done.1 = f32[4,16,640]{2,1,0:T(8,128)S(1)} async-done(((f32[4,16,640]{2,1,0:T(8,128)}), f32[4,16,640]{2,1,0:T(8,128)S(1)}, u32[]{:S(2)}, u32[]{:S(2)}) %all-to-all-start.1) | async-done | bytes 163872 | tf_op jit(solution)/shard_map/all_to_all | solution.py:146
  37.5 6.0 %collective-permute-done = f32[16,640]{1,0:T(8,128)S(1)} collective-permute-done((f32[16,640]{1,0:T(8,128)S(1)}, f32[16,640]{1,0:T(8,128)S(1)}, u32[]{:S(2)}, u32[]{:S(2)}) %collective-permute-start) | collective-permute-done | bytes 40992 | tf_op jit(solution)/shard_map/ppermute | solution.py:109
  43.6 6.1 %collective-permute-done.1 = f32[16,640]{1,0:T(8,128)S(1)} collective-permute-done((f32[16,640]{1,0:T(8,128)S(1)}, f32[16,640]{1,0:T(8,128)S(1)}, u32[]{:S(2)}, u32[]{:S(2)}) %collective-permute-start.1) | collective-permute-done | bytes 40992 | tf_op jit(solution)/shard_map/ppermute | solution.py:109
  49.6 2.4 %collective-permute-done.2 = f32[16,640]{1,0:T(8,128)S(1)} collective-permute-done((f32[16,640]{1,0:T(8,128)S(1)}, f32[16,640]{1,0:T(8,128)S(1)}, u32[]{:S(2)}, u32[]{:S(2)}) %collective-permute-start.2) | collective-permute-done | bytes 40992 | tf_op jit(solution)/shard_map/ppermute | solution.py:109
  53.7 7.7 %all-to-all-start.2 = ((f32[4,16,512]{2,1,0:T(8,128)}), f32[4,16,512]{2,1,0:T(8,128)}, u32[]{:S(2)}, u32[]{:S(2)}) async-start(f32[4,16,512]{2,1,0:T(8,128)} %pad_maximum_fusion.4), calls=%async_computation.2 | async-start | bytes 262144 | tf_op jit(solution)/shard_map/all_to_all | solution.py:162
  65.4 2.2 %copy.134 = f32[16,4,512]{0,2,1:T(8,128)} copy(f32[16,4,512]{2,0,1:T(8,128)} %bitcast.29) | data formatting | bytes 262144 | tf_op jit(solution)/shard_map/transpose | solution.py:163
  67.6 3.7 %bitcast_add_fusion.3 = (f32[1,16,2048]{1,2,0:T(8,128)}, f32[1,16,2048]{1,2,0:T(8,128)}, f32[1,16,2048]{1,2,0:T(8,128)}, f32[1,16,2048]{1,2,0:T(8,128)}) fusion(f32[16,2048]{0,1:T(8,128)S(1)} %copy.158, f32[16,4,512]{0,2,1:T(8,128)} %copy.134, f32[16,2048]{0,1:T(8,128)S(1)} %copy.159, f32[16]{0:T(128)} %get-tuple-element.382, f32[16,2048]{0,1:T(8,128)S(1)} %copy.160, ...), kind=kLoop, calls=%fused_computation.33 | loop fusion | flops 229376 | bytes 1179840 | tf_op jit(solution)/shard_map/add | solution.py:160
  76.0 3.5 %all-to-all-start.3 = ((f32[4,16,2048]{2,1,0:T(8,128)}), f32[4,16,2048]{2,1,0:T(8,128)S(1)}, u32[]{:S(2)}, u32[]{:S(2)}) async-start(f32[4,16,2048]{2,1,0:T(8,128)} %pad_maximum_fusion.1), calls=%async_computation.3 | async-start | bytes 1048576 | tf_op jit(solution)/shard_map/all_to_all | solution.py:162
  80.3 2.9 %copy.156 = bf16[1024,1024]{1,0:T(8,128)(2,1)S(1)} copy(bf16[1024,1024]{0,1:T(8,128)(2,1)} %bitcast.169) | data formatting | bytes 4194304 | tf_op jit(solution)/shard_map/dot_general | solution.py:194
  84.7 2.8 %all-to-all-done.3 = f32[4,16,2048]{2,1,0:T(8,128)S(1)} async-done(((f32[4,16,2048]{2,1,0:T(8,128)}), f32[4,16,2048]{2,1,0:T(8,128)S(1)}, u32[]{:S(2)}, u32[]{:S(2)}) %all-to-all-start.3) | async-done | bytes 524320 | tf_op jit(solution)/shard_map/all_to_all | solution.py:162
  90.0 2.0 %fusion.18 = f32[64,1,16,64]{3,0,2,1:T(8,128)S(1)} fusion(f32[64,1,16,64]{3,0,2,1:T(8,128)} %convolution_bitcast_fusion.2, f32[16,64,128]{2,1,0:T(8,128)S(1)} %reshape.899, f32[64,1,16,64]{3,2,0,1:T(8,128)S(1)} %reshape.908, f32[16]{0:T(128)S(1)} %copy-done.17, f32[64,16]{0,1:T(8,128)S(1)} %exponential_bitcast_fusion, bf16[64,128]{1,0:T(8,128)(2,1)S(1)} %copy-done.9), kind=kOutput, calls=%fused_computation.28 | convolution fusion | flops 100925440 | bytes 1331264 | tf_op jit(solution)/shard_map/tgn,gkpn->tgkp/dot_general | solution.py:35
  93.6 11.8 %all_to_all.30 = f32[8,64,128]{2,1,0:T(8,128)S(1)} all-to-all(f32[8,64,128]{2,1,0:T(8,128)S(1)} %convolution_bitcast_fusion.3), channel_id=1, replica_groups=mesh['zh'=4,'zl'=4,'sx'=4,'tp'=8] {'tp'}, dimensions={0} | all-to-all | bytes 524288 | tf_op jit(solution)/shard_map/all_to_all | solution.py:198
  109.4 6.6 %collective-permute-done.3 = bf16[2,1,64,128]{3,2,0,1:T(8,128)(2,1)S(1)} collective-permute-done((bf16[2,1,64,128]{3,2,0,1:T(8,128)(2,1)S(1)}, bf16[2,1,64,128]{3,2,0,1:T(8,128)(2,1)S(1)}, u32[]{:S(2)}, u32[]{:S(2)}) %collective-permute-start.3) | collective-permute-done | bytes 32800 | tf_op jit(solution)/shard_map/ppermute | solution.py:109
  116.0 5.5 %collective-permute-done.4 = bf16[2,1,64,128]{3,2,0,1:T(8,128)(2,1)S(1)} collective-permute-done((bf16[2,1,64,128]{3,2,0,1:T(8,128)(2,1)S(1)}, bf16[2,1,64,128]{3,2,0,1:T(8,128)(2,1)S(1)}, u32[]{:S(2)}, u32[]{:S(2)}) %collective-permute-start.4) | collective-permute-done | bytes 32800 | tf_op jit(solution)/shard_map/ppermute | solution.py:109
  121.5 2.5 %collective-permute-done.5 = bf16[2,1,64,128]{3,2,1,0:T(8,128)(2,1)S(1)} collective-permute-done((bf16[2,1,64,128]{3,2,1,0:T(8,128)(2,1)S(1)}, bf16[2,1,64,128]{3,2,1,0:T(8,128)(2,1)S(1)}, u32[]{:S(2)}, u32[]{:S(2)}) %collective-permute-start.5) | collective-permute-done | bytes 32800 | tf_op jit(solution)/shard_map/ppermute | solution.py:109
  124.7 6.1 %collective-permute-start.6 = (bf16[4,2,1,64,128]{4,3,1,0,2:T(8,128)(2,1)S(1)}, bf16[4,2,1,64,128]{4,3,1,0,2:T(8,128)(2,1)S(1)}, u32[]{:S(2)}, u32[]{:S(2)}) collective-permute-start(bf16[4,2,1,64,128]{4,3,1,0,2:T(8,128)(2,1)S(1)} %bitcast.179), channel_id=1, source_target_pairs={{0,32},{32,64},{64,96},{96,0},{1,33},{33,65},{65,97},{97,1},{2,34}... | collective-permute-start | bytes 393224 | tf_op jit(solution)/shard_map/ppermute | solution.py:109
  132.8 2.5 %collective-permute-start.8 = (bf16[4,2,1,64,128]{4,3,1,0,2:T(8,128)(2,1)S(1)}, bf16[4,2,1,64,128]{4,3,1,0,2:T(8,128)(2,1)S(1)}, u32[]{:S(2)}, u32[]{:S(2)}) collective-permute-start(bf16[4,2,1,64,128]{4,3,1,0,2:T(8,128)(2,1)S(1)} %bitcast.181), channel_id=1, source_target_pairs={{0,96},{32,0},{64,32},{96,64},{1,97},{33,1},{65,33},{97,65},{2,98}... | collective-permute-start | bytes 393224 | tf_op jit(solution)/shard_map/ppermute | solution.py:109
  135.3 7.6 %collective-permute-done.7 = bf16[4,2,1,64,128]{4,3,1,0,2:T(8,128)(2,1)S(1)} collective-permute-done((bf16[4,2,1,64,128]{4,3,1,0,2:T(8,128)(2,1)S(1)}, bf16[4,2,1,64,128]{4,3,1,0,2:T(8,128)(2,1)S(1)}, u32[]{:S(2)}, u32[]{:S(2)}) %collective-permute-start.7) | collective-permute-done | bytes 131104 | tf_op jit(solution)/shard_map/ppermute | solution.py:109
  145.6 3.7 %all-to-all-start.5 = ((bf16[4,4,4,2,1,64,128]{6,5,1,2,4,3,0:T(8,128)(2,1)}), bf16[4,4,4,2,1,64,128]{6,5,1,2,4,3,0:T(8,128)(2,1)S(1)}, u32[]{:S(2)}, u32[]{:S(2)}) async-start(bf16[4,4,4,2,1,64,128]{6,5,1,2,4,3,0:T(8,128)(2,1)} %broadcast_in_dim.392), calls=%async_computation.5 | async-start | bytes 4194304 | tf_op jit(solution)/shard_map/all_to_all | solution.py:99
  150.1 26.0 %all-to-all-done.5 = bf16[4,4,4,2,1,64,128]{6,5,1,2,4,3,0:T(8,128)(2,1)S(1)} async-done(((bf16[4,4,4,2,1,64,128]{6,5,1,2,4,3,0:T(8,128)(2,1)}), bf16[4,4,4,2,1,64,128]{6,5,1,2,4,3,0:T(8,128)(2,1)S(1)}, u32[]{:S(2)}, u32[]{:S(2)}) %all-to-all-start.5) | async-done | bytes 2097184 | tf_op jit(solution)/shard_map/all_to_all | solution.py:99
  176.5 22.2 %while.20 = (s32[]{:T(128)}, f32[1,256]{1,0:T(1,128)S(1)}, f32[1,256]{1,0:T(1,128)S(1)}, f32[1,256,128]{2,1,0:T(8,128)S(1)}, s32[]{:T(128)}, /*index=5*/bf16[1,4...) while((s32[]{:T(128)}, f32[1,256]{1,0:T(1,128)S(1)}, ...), condition=%wide.region_37.38_spmd.clone, body=%wide.region_32.37_spmd.clone.sunk | while | flops 34145032 | bytes 1270325 | solution.py:242
  (311 shorter events, 63.7 us)
Async XLA Ops:
  0.6 4.3 %copy-start = (bf16[64,128]{1,0:T(8,128)(2,1)S(1)}, bf16[64,128]{1,0:T(8,128)(2,1)}, u32[]{:S(2)}) copy-start(bf16[64,128]{1,0:T(8,128)(2,1)} %param.17) | copy-start | bytes 49156
  6.7 14.1 %all-to-all-start = ((f32[4,16,2176]{2,1,0:T(8,128)}), f32[4,16,2176]{2,1,0:T(8,128)S(1)}, u32[]{:S(2)}, u32[]{:S(2)}) async-start(f32[4,16,2176]{2,1,0:T(8,128)} %pad_maximum_fusion), calls=%async_computation | async-start | bytes 1114112 | tf_op jit(solution)/shard_map/all_to_all | solution.py:146
  22.8 38.6 %copy-start.8 = (bf16[64,128]{1,0:T(8,128)(2,1)S(1)}, bf16[64,128]{1,0:T(8,128)(2,1)}, u32[]{:S(2)}) copy-start(bf16[64,128]{1,0:T(8,128)(2,1)} %param.18) | copy-start | bytes 49156
  24.0 9.2 %all-to-all-start.1 = ((f32[4,16,640]{2,1,0:T(8,128)}), f32[4,16,640]{2,1,0:T(8,128)S(1)}, u32[]{:S(2)}, u32[]{:S(2)}) async-start(f32[4,16,640]{2,1,0:T(8,128)} %copy.133), calls=%async_computation.1 | async-start | bytes 327680 | tf_op jit(solution)/shard_map/all_to_all | solution.py:146
  33.6 9.9 %collective-permute-start = (f32[16,640]{1,0:T(8,128)S(1)}, f32[16,640]{1,0:T(8,128)S(1)}, u32[]{:S(2)}, u32[]{:S(2)}) collective-permute-start(f32[16,640]{1,0:T(8,128)S(1)} %get-tuple-element.427), channel_id=1, source_target_pairs={{0,128},{128,256},{256,384},{1,129},{129,257},{257,385},{2,130},{1... | collective-permute-start | bytes 122888 | tf_op jit(solution)/shard_map/ppermute | solution.py:109
  34.9 14.7 %collective-permute-start.1 = (f32[16,640]{1,0:T(8,128)S(1)}, f32[16,640]{1,0:T(8,128)S(1)}, u32[]{:S(2)}, u32[]{:S(2)}) collective-permute-start(f32[16,640]{1,0:T(8,128)S(1)} %get-tuple-element.427), channel_id=1, source_target_pairs={{0,256},{128,384},{1,257},{129,385},{2,258},{130,386},{3,259},{131... | collective-permute-start | bytes 122888 | tf_op jit(solution)/shard_map/ppermute | solution.py:109
  36.2 15.8 %collective-permute-start.2 = (f32[16,640]{1,0:T(8,128)S(1)}, f32[16,640]{1,0:T(8,128)S(1)}, u32[]{:S(2)}, u32[]{:S(2)}) collective-permute-start(f32[16,640]{1,0:T(8,128)S(1)} %get-tuple-element.427), channel_id=1, source_target_pairs={{0,384},{1,385},{2,386},{3,387},{4,388},{5,389},{6,390},{7,391},{8... | collective-permute-start | bytes 122888 | tf_op jit(solution)/shard_map/ppermute | solution.py:109
  37.5 15.4 %copy-start.15 = (s32[1024]{0:T(1024)}, s32[1024]{0:T(1024)S(1)}, u32[]{:S(2)}) copy-start(s32[1024]{0:T(1024)S(1)} %pad_clamp_fusion.1) | copy-start | bytes 12292
  53.7 11.7 %all-to-all-start.2 = ((f32[4,16,512]{2,1,0:T(8,128)}), f32[4,16,512]{2,1,0:T(8,128)}, u32[]{:S(2)}, u32[]{:S(2)}) async-start(f32[4,16,512]{2,1,0:T(8,128)} %pad_maximum_fusion.4), calls=%async_computation.2 | async-start | bytes 262144 | tf_op jit(solution)/shard_map/all_to_all | solution.py:162
  71.3 3.5 %copy-start.1 = (f32[1,16,2048]{1,2,0:T(8,128)S(1)}, f32[1,16,2048]{1,2,0:T(8,128)}, u32[]{:S(2)}) copy-start(f32[1,16,2048]{1,2,0:T(8,128)} %get-tuple-element.425) | copy-start | bytes 393220
  74.5 5.6 %copy-start.3 = (bf16[64,1024]{1,0:T(8,128)(2,1)S(1)}, bf16[64,1024]{1,0:T(8,128)(2,1)}, u32[]{:S(2)}) copy-start(bf16[64,1024]{1,0:T(8,128)(2,1)} %param.15) | copy-start | bytes 393220
  76.0 11.5 %all-to-all-start.3 = ((f32[4,16,2048]{2,1,0:T(8,128)}), f32[4,16,2048]{2,1,0:T(8,128)S(1)}, u32[]{:S(2)}, u32[]{:S(2)}) async-start(f32[4,16,2048]{2,1,0:T(8,128)} %pad_maximum_fusion.1), calls=%async_computation.3 | async-start | bytes 1048576 | tf_op jit(solution)/shard_map/all_to_all | solution.py:162
  83.1 6.8 %copy-start.9 = (bf16[64,128]{1,0:T(8,128)(2,1)S(1)}, bf16[64,128]{1,0:T(8,128)(2,1)}, u32[]{:S(2)}) copy-start(bf16[64,128]{1,0:T(8,128)(2,1)} %param.18) | copy-start | bytes 49156
  83.1 6.8 %copy-start.17 = (f32[16]{0:T(128)S(1)}, f32[16]{0:T(128)}, u32[]{:S(2)}) copy-start(f32[16]{0:T(128)} %param.21) | copy-start | bytes 196
  92.5 12.9 %copy-start.12 = (bf16[64,128]{1,0:T(8,128)(2,1)S(1)}, bf16[64,128]{1,0:T(8,128)(2,1)}, u32[]{:S(2)}) copy-start(bf16[64,128]{1,0:T(8,128)(2,1)} %param.25) | copy-start | bytes 49156
  92.9 50.1 %copy-start.4 = (bf16[64,1024]{1,0:T(8,128)(2,1)}, bf16[64,1024]{1,0:T(8,128)(2,1)S(1)}, u32[]{:S(2)}) copy-start(bf16[64,1024]{1,0:T(8,128)(2,1)S(1)} %multiply_convert_fusion) | copy-start | bytes 393220
  105.5 10.5 %collective-permute-start.3 = (bf16[2,1,64,128]{3,2,0,1:T(8,128)(2,1)S(1)}, bf16[2,1,64,128]{3,2,0,1:T(8,128)(2,1)S(1)}, u32[]{:S(2)}, u32[]{:S(2)}) collective-permute-start(bf16[2,1,64,128]{3,2,0,1:T(8,128)(2,1)S(1)} %get-tuple-element.429), channel_id=1, source_target_pairs={{0,128},{128,256},{256,384},{1,129},{129,257},{257,385},{2,130},{1... | collective-permute-start | bytes 98312 | tf_op jit(solution)/shard_map/ppermute | solution.py:109
  106.8 14.7 %collective-permute-start.4 = (bf16[2,1,64,128]{3,2,0,1:T(8,128)(2,1)S(1)}, bf16[2,1,64,128]{3,2,0,1:T(8,128)(2,1)S(1)}, u32[]{:S(2)}, u32[]{:S(2)}) collective-permute-start(bf16[2,1,64,128]{3,2,0,1:T(8,128)(2,1)S(1)} %get-tuple-element.429), channel_id=1, source_target_pairs={{0,256},{128,384},{1,257},{129,385},{2,258},{130,386},{3,259},{131... | collective-permute-start | bytes 98312 | tf_op jit(solution)/shard_map/ppermute | solution.py:109
  108.1 15.9 %collective-permute-start.5 = (bf16[2,1,64,128]{3,2,1,0:T(8,128)(2,1)S(1)}, bf16[2,1,64,128]{3,2,1,0:T(8,128)(2,1)S(1)}, u32[]{:S(2)}, u32[]{:S(2)}) collective-permute-start(bf16[2,1,64,128]{3,2,1,0:T(8,128)(2,1)S(1)} %get-tuple-element.430), channel_id=1, source_target_pairs={{0,384},{1,385},{2,386},{3,387},{4,388},{5,389},{6,390},{7,391},{8... | collective-permute-start | bytes 98312 | tf_op jit(solution)/shard_map/ppermute | solution.py:109
  124.7 10.6 %collective-permute-start.6 = (bf16[4,2,1,64,128]{4,3,1,0,2:T(8,128)(2,1)S(1)}, bf16[4,2,1,64,128]{4,3,1,0,2:T(8,128)(2,1)S(1)}, u32[]{:S(2)}, u32[]{:S(2)}) collective-permute-start(bf16[4,2,1,64,128]{4,3,1,0,2:T(8,128)(2,1)S(1)} %bitcast.179), channel_id=1, source_target_pairs={{0,32},{32,64},{64,96},{96,0},{1,33},{33,65},{65,97},{97,1},{2,34}... | collective-permute-start | bytes 393224 | tf_op jit(solution)/shard_map/ppermute | solution.py:109
  130.8 12.1 %collective-permute-start.7 = (bf16[4,2,1,64,128]{4,3,1,0,2:T(8,128)(2,1)S(1)}, bf16[4,2,1,64,128]{4,3,1,0,2:T(8,128)(2,1)S(1)}, u32[]{:S(2)}, u32[]{:S(2)}) collective-permute-start(bf16[4,2,1,64,128]{4,3,1,0,2:T(8,128)(2,1)S(1)} %bitcast.180), channel_id=1, source_target_pairs={{0,64},{32,96},{64,0},{96,32},{1,65},{33,97},{65,1},{97,33},{2,66}... | collective-permute-start | bytes 393224 | tf_op jit(solution)/shard_map/ppermute | solution.py:109
  132.8 10.2 %collective-permute-start.8 = (bf16[4,2,1,64,128]{4,3,1,0,2:T(8,128)(2,1)S(1)}, bf16[4,2,1,64,128]{4,3,1,0,2:T(8,128)(2,1)S(1)}, u32[]{:S(2)}, u32[]{:S(2)}) collective-permute-start(bf16[4,2,1,64,128]{4,3,1,0,2:T(8,128)(2,1)S(1)} %bitcast.181), channel_id=1, source_target_pairs={{0,96},{32,0},{64,32},{96,64},{1,97},{33,1},{65,33},{97,65},{2,98}... | collective-permute-start | bytes 393224 | tf_op jit(solution)/shard_map/ppermute | solution.py:109
  145.6 3.8 %copy-start.10 = (bf16[64,512]{1,0:T(8,128)(2,1)S(1)}, bf16[64,512]{1,0:T(8,128)(2,1)}, u32[]{:S(2)}) copy-start(bf16[64,512]{1,0:T(8,128)(2,1)} %param.24) | copy-start | bytes 196612
  145.6 30.5 %all-to-all-start.5 = ((bf16[4,4,4,2,1,64,128]{6,5,1,2,4,3,0:T(8,128)(2,1)}), bf16[4,4,4,2,1,64,128]{6,5,1,2,4,3,0:T(8,128)(2,1)S(1)}, u32[]{:S(2)}, u32[]{:S(2)}) async-start(bf16[4,4,4,2,1,64,128]{6,5,1,2,4,3,0:T(8,128)(2,1)} %broadcast_in_dim.392), calls=%async_computation.5 | async-start | bytes 4194304 | tf_op jit(solution)/shard_map/all_to_all | solution.py:99
  (8 other events, 22.9 us)

commit v6 on v3

--- a/solution.py
+++ b/solution.py
@@ -60,37 +60,6 @@
     result = (running_out / running_sum[..., None]).astype(jnp.bfloat16)
     result = result.reshape(kv_here, per_kv, count_rows, HEAD_DIM)
     return jnp.transpose(result, (2, 0, 1, 3)).reshape(count_rows, kv_here * per_kv * HEAD_DIM)
-
-
-def attend(running, query_set, key_slab, value_slab, key_first):
-    query_block, query_pos = query_set
-    score_scale = 1.0 / math.sqrt(HEAD_DIM)
-    key_pos = key_first + jnp.arange(key_slab.shape[1], dtype=jnp.int32)
-
-    def update(current):
-        running_max, running_sum, running_out = current
-        scores = (
-            jnp.einsum("hrd,hcd->hrc", query_block, key_slab, preferred_element_type=jnp.float32)
-            * score_scale
-        )
-        allowed = key_pos[None, :] <= query_pos[:, None]
-        scores = jnp.where(allowed[None], scores, -jnp.inf)
-        new_max = jnp.maximum(running_max, jnp.max(scores, axis=2))
-        weights = jnp.exp(scores - new_max[..., None])
-        shrink = jnp.exp(running_max - new_max)
-        new_sum = running_sum * shrink + jnp.sum(weights, axis=2)
-        new_out = running_out * shrink[..., None] + jnp.einsum(
-            "hrc,hcd->hrd",
-            weights.astype(jnp.bfloat16),
-            value_slab,
-            preferred_element_type=jnp.float32,
-        )
-        return (new_max, new_sum, new_out)
-
-    def unchanged(current):
-        return current
-
-    return lax.cond(key_first <= jnp.max(query_pos), update, unchanged, running)
 
 
 def gather_by_exchange(block, axis):
@@ -194,41 +163,21 @@
     key_portion = all_pairs[0]
     value_portion = all_pairs[1]
     my_index = lax.axis_index(SEQ_AXES[::-1])
-    query_sets = [
-        (
-            query_layout(queries, kv_here, per_kv),
-            row_positions(my_index * tokens_here, tokens_here, per_kv),
-        )
-    ]
-    initial = tuple(
-        (
-            (
-                jnp.full((kv_here, query_set[0].shape[1]), -jnp.inf, jnp.float32),
-                jnp.zeros((kv_here, query_set[0].shape[1]), jnp.float32),
-                jnp.zeros((kv_here, query_set[0].shape[1], HEAD_DIM), jnp.float32),
-            )
-            for query_set in query_sets
-        )
-    )
-    length = key_portion.shape[1]
-    block_len = length
-    for multiple in (1, 2, 4):
-        block_len = multiple * tokens_here
-
-    def one_block(block_index, current):
-        offset = block_index * block_len
-        key_slab = lax.dynamic_slice_in_dim(key_portion, offset, block_len, 1)
-        value_slab = lax.dynamic_slice_in_dim(value_portion, offset, block_len, 1)
-        return tuple(
-            (
-                attend(current[set_index], query_sets[set_index], key_slab, value_slab, offset)
-                for set_index in range(len(query_sets))
-            )
-        )
-
-    finished = lax.fori_loop(0, length // block_len, one_block, initial)
-    outputs = [set_output(finished_set, kv_here, per_kv) for finished_set in finished]
-    attention = outputs[0]
+    query_block = query_layout(queries, kv_here, per_kv)
+    query_pos = row_positions(my_index * tokens_here, tokens_here, per_kv)
+    key_pos = jnp.arange(key_portion.shape[1], dtype=jnp.int32)
+    scores = jnp.einsum(
+        "hrd,hcd->hrc", query_block, key_portion, preferred_element_type=jnp.float32
+    ) * (1.0 / math.sqrt(HEAD_DIM))
+    allowed = key_pos[None, :] <= query_pos[:, None]
+    scores = jnp.where(allowed[None], scores, -jnp.inf)
+    row_max = jnp.max(scores, axis=2, keepdims=True)
+    weights = jnp.exp(scores - row_max)
+    total = jnp.sum(weights, axis=2)
+    weighted = jnp.einsum(
+        "hrc,hcd->hrd", weights.astype(jnp.bfloat16), value_portion, preferred_element_type=jnp.float32
+    )
+    attention = set_output((row_max, total, weighted), kv_here, per_kv)
     return (mamba_out, attention)
 
 

time: 196 us -> 183 us (0.934)
  the two profiles are of different devices: /device:TPU:480 before, /device:TPU:16 now
where the time goes in v6:
time: 183 us; the launch traced here: 182 us
  blocking collectives  56 us (31%)
  waiting for transfers between devices  49.9 us (27%)
  starting transfers between devices  27.9 us (15%)
  local copies, waits for them, and re-layouts  25.7 us (14%)
  other arithmetic  12.9 us (7%)
  matrix products  8.03 us (4%)
    all_to_all x2, waiting for transfers between devices, gather_by_exchange(): return lax.all_to_all(repeated, axis, 0, 0, tiled=True)  36.8 us
    all_to_all x2, blocking collectives, gather_by_exchange(): return lax.all_to_all(repeated, axis, 0, 0, tiled=True)  34.6 us
    all_to_all x2, starting transfers between devices, gather_by_exchange(): return lax.all_to_all(repeated, axis, 0, 0, tiled=True)  16.2 us
    all_to_all x1, blocking collectives, entering_state(): received = lax.all_to_all(packed, axis, 0, 0, tiled=True)  12.4 us
    all_to_all x1, waiting for transfers between devices, entering_state(): received = lax.all_to_all(packed, axis, 0, 0, tiled=True)  9.76 us
    all_to_all x1, blocking collectives, per_device(): exchanged = lax.all_to_all(partials, 'tp', 0, 0, tiled=True)  8.98 us
    all_to_all x2, starting transfers between devices, entering_state(): returned = lax.all_to_all(outgoing, axis, 0, 0, tiled=True)  7.4 us
    add x8, local copies, waits for them, and re-layouts, entering_state(): decay_before[upto][:, None] * group_in + prefixes[upto]  5.4 us
  transfers between devices with their start and end apart: 5, of which 5 were waited for; matrix products, arithmetic and copies ran while one was open for 6% of the time, Pallas kernels for 0%

profile of v6, /device:TPU:16, one launch (start us, length us, event | category | flops | bytes accessed | tf_op | source)
XLA Modules:
  0.0 181.5 jit_solution(17786235037185600083)
XLA Ops:
  6.7 4.3 %all-to-all-start = ((f32[4,16,2176]{2,1,0:T(8,128)}), f32[4,16,2176]{2,1,0:T(8,128)S(1)}, u32[]{:S(2)}, u32[]{:S(2)}) async-start(f32[4,16,2176]{2,1,0:T(8,128)} %pad_maximum_fusion), calls=%async_computation | async-start | bytes 1114112 | tf_op jit(solution)/shard_map/all_to_all | solution.py:103
  11.1 9.8 %all-to-all-done = f32[4,16,2176]{2,1,0:T(8,128)S(1)} async-done(((f32[4,16,2176]{2,1,0:T(8,128)}), f32[4,16,2176]{2,1,0:T(8,128)S(1)}, u32[]{:S(2)}, u32[]{:S(2)}) %all-to-all-start) | async-done | bytes 557088 | tf_op jit(solution)/shard_map/all_to_all | solution.py:103
  23.4 12.4 %all_to_all.45 = f32[4,16,640]{2,1,0:T(8,128)S(1)} all-to-all(f32[4,16,640]{2,1,0:T(8,128)S(1)} %copy.136), channel_id=1, replica_groups=mesh['zh'=4,'zl'=4,'sx'=4,'tp'=8] {'zl'}, dimensions={0} | all-to-all | bytes 327680 | tf_op jit(solution)/shard_map/all_to_all | solution.py:103
  36.9 12.4 %all-to-all-start.2 = ((f32[4,16,640]{2,1,0:T(8,128)}), f32[4,16,640]{2,1,0:T(8,128)S(1)}, u32[]{:S(2)}, u32[]{:S(2)}) async-start(f32[4,16,640]{2,1,0:T(8,128)} %broadcast_in_dim.389), calls=%async_computation.2 | async-start | bytes 327680 | tf_op jit(solution)/shard_map/all_to_all | solution.py:68
  49.9 12.8 %all-to-all-done.2 = f32[4,16,640]{2,1,0:T(8,128)S(1)} async-done(((f32[4,16,640]{2,1,0:T(8,128)}), f32[4,16,640]{2,1,0:T(8,128)S(1)}, u32[]{:S(2)}, u32[]{:S(2)}) %all-to-all-start.2) | async-done | bytes 163872 | tf_op jit(solution)/shard_map/all_to_all | solution.py:68
  64.3 3.9 %all-to-all-start.3 = ((f32[4,16,512]{2,1,0:T(8,128)}), f32[4,16,512]{2,1,0:T(8,128)}, u32[]{:S(2)}, u32[]{:S(2)}) async-start(f32[4,16,512]{2,1,0:T(8,128)} %pad_maximum_fusion.3), calls=%async_computation.3 | async-start | bytes 262144 | tf_op jit(solution)/shard_map/all_to_all | solution.py:119
  71.0 1.3 copy.175
  72.3 2.0 %all-to-all-done.3 = f32[4,16,512]{2,1,0:T(8,128)} async-done(((f32[4,16,512]{2,1,0:T(8,128)}), f32[4,16,512]{2,1,0:T(8,128)}, u32[]{:S(2)}, u32[]{:S(2)}) %all-to-all-start.3) | async-done | bytes 131104 | tf_op jit(solution)/shard_map/all_to_all | solution.py:119
  74.3 2.2 %copy.147 = f32[16,4,512]{0,2,1:T(8,128)} copy(f32[16,4,512]{2,0,1:T(8,128)} %bitcast.15) | data formatting | bytes 262144 | tf_op jit(solution)/shard_map/transpose | solution.py:120
  76.5 3.7 %bitcast_add_fusion.3 = (f32[1,16,2048]{1,2,0:T(8,128)}, f32[1,16,2048]{1,2,0:T(8,128)}, f32[1,16,2048]{1,2,0:T(8,128)}, f32[1,16,2048]{1,2,0:T(8,128)}) fusion(f32[16,2048]{0,1:T(8,128)S(1)} %copy.172, f32[16,4,512]{0,2,1:T(8,128)} %copy.147, f32[16,2048]{0,1:T(8,128)S(1)} %copy.173, f32[16]{0:T(128)} %get-tuple-element.12, f32[16,2048]{0,1:T(8,128)S(1)} %copy.174, ...), kind=kLoop, calls=%fused_computation.21 | loop fusion | flops 229376 | bytes 1179840 | tf_op jit(solution)/shard_map/add | solution.py:117
  80.2 1.6 copy.155
  81.8 1.5 copy.154
  83.3 1.5 copy.153
  86.0 3.5 %all-to-all-start.4 = ((f32[4,16,2048]{2,1,0:T(8,128)}), f32[4,16,2048]{2,1,0:T(8,128)S(1)}, u32[]{:S(2)}, u32[]{:S(2)}) async-start(f32[4,16,2048]{2,1,0:T(8,128)} %pad_maximum_fusion.1), calls=%async_computation.4 | async-start | bytes 1048576 | tf_op jit(solution)/shard_map/all_to_all | solution.py:119
  90.2 2.9 %copy.168 = bf16[1024,1024]{1,0:T(8,128)(2,1)S(1)} copy(bf16[1024,1024]{0,1:T(8,128)(2,1)} %bitcast.129) | data formatting | bytes 4194304 | tf_op jit(solution)/shard_map/dot_general | solution.py:151
  93.1 2.3 %convolution_bitcast_fusion.1 = f32[64,1,16,64]{3,0,2,1:T(8,128)} fusion(bf16[64,16,64]{0,2,1:T(8,128)(2,1)S(1)} %bitcast.134, f32[16,64]{1,0:T(8,128)} %get-tuple-element.39, f32[16,64]{1,0:T(8,128)} %bitcast.141, f32[64,64]{1,0:T(8,128)} %fusion.47, pred[64,64]{1,0:T(8,128)(4,1)} %iota_compare_fusion.1), kind=kOutput, calls=%fused_computation.11 | convolution fusion | flops 50593792 | bytes 421888 | tf_op jit(solution)/shard_map/gkts,sgkp->tgkp/dot_general | solution.py:28
  96.1 1.4 all-to-all-done.4
  100.0 2.0 %fusion.9 = f32[64,1,16,64]{3,0,2,1:T(8,128)S(1)} fusion(f32[64,1,16,64]{3,0,2,1:T(8,128)} %convolution_bitcast_fusion.1, f32[16,64,128]{2,1,0:T(8,128)S(1)} %reshape.786, f32[64,1,16,64]{3,2,0,1:T(8,128)S(1)} %reshape.797, f32[16]{0:T(128)} %param.17, f32[64,16]{0,1:T(8,128)S(1)} %exponential_bitcast_fusion, bf16[64,128]{1,0:T(8,128)(2,1)} %param.14), kind=kOutput, calls=%fused_computation.14 | convolution fusion | flops 100925440 | bytes 1331264 | tf_op jit(solution)/shard_map/tgn,gkpn->tgkp/dot_general | solution.py:35
  104.3 9.0 %all_to_all.46 = f32[8,64,128]{2,1,0:T(8,128)S(1)} all-to-all(f32[8,64,128]{2,1,0:T(8,128)S(1)} %convolution_bitcast_fusion.2), channel_id=1, replica_groups=mesh['zh'=4,'zl'=4,'sx'=4,'tp'=8] {'tp'}, dimensions={0} | all-to-all | bytes 524288 | tf_op jit(solution)/shard_map/all_to_all | solution.py:155
  113.3 19.7 %all_to_all.47 = bf16[4,2,1,64,128]{4,3,1,2,0:T(8,128)(2,1)S(1)} all-to-all(bf16[4,2,1,64,128]{4,3,1,2,0:T(8,128)(2,1)S(1)} %broadcast_in_dim.399), channel_id=1, replica_groups=mesh['zh'=4,'zl'=4,'sx'=4,'tp'=8] {'zh'}, dimensions={0} | all-to-all | bytes 262144 | tf_op jit(solution)/shard_map/all_to_all | solution.py:68
  133.2 14.9 %all_to_all.48 = bf16[4,4,2,1,64,128]{5,4,1,2,3,0:T(8,128)(2,1)S(1)} all-to-all(bf16[4,4,2,1,64,128]{5,4,1,2,3,0:T(8,128)(2,1)S(1)} %broadcast_in_dim.401), channel_id=1, replica_groups=mesh['zh'=4,'zl'=4,'sx'=4,'tp'=8] {'zl'}, dimensions={0} | all-to-all | bytes 1048576 | tf_op jit(solution)/shard_map/all_to_all | solution.py:68
  148.1 1.9 %broadcast_in_dim.403 = bf16[4,4,4,2,1,64,128]{6,5,1,2,4,3,0:T(8,128)(2,1)} broadcast(bf16[4,4,2,64,128]{4,3,0,1,2:T(8,128)(2,1)S(1)} %copy.162), dimensions={1,2,3,5,6} | broadcast | bytes 2621440 | tf_op jit(solution)/shard_map/broadcast_in_dim | solution.py:67
  150.0 3.8 %all-to-all-start.8 = ((bf16[4,4,4,2,1,64,128]{6,5,1,2,4,3,0:T(8,128)(2,1)}), bf16[4,4,4,2,1,64,128]{6,5,1,2,4,3,0:T(8,128)(2,1)S(1)}, u32[]{:S(2)}, u32[]{:S(2)}) async-start(bf16[4,4,4,2,1,64,128]{6,5,1,2,4,3,0:T(8,128)(2,1)} %broadcast_in_dim.403), calls=%async_computation.8 | async-start | bytes 4194304 | tf_op jit(solution)/shard_map/all_to_all | solution.py:68
  154.0 23.9 %all-to-all-done.8 = bf16[4,4,4,2,1,64,128]{6,5,1,2,4,3,0:T(8,128)(2,1)S(1)} async-done(((bf16[4,4,4,2,1,64,128]{6,5,1,2,4,3,0:T(8,128)(2,1)}), bf16[4,4,4,2,1,64,128]{6,5,1,2,4,3,0:T(8,128)(2,1)S(1)}, u32[]{:S(2)}, u32[]{:S(2)}) %all-to-all-start.8) | async-done | bytes 2097184 | tf_op jit(solution)/shard_map/all_to_all | solution.py:68
  (104 shorter events, 25.7 us)
Async XLA Ops:
  0.6 4.3 %copy-start = (bf16[64,128]{1,0:T(8,128)(2,1)S(1)}, bf16[64,128]{1,0:T(8,128)(2,1)}, u32[]{:S(2)}) copy-start(bf16[64,128]{1,0:T(8,128)(2,1)} %param.13) | copy-start | bytes 49156
  2.3 2.6 %copy-start.5 = (f32[1,16,64]{2,1,0:T(8,128)}, f32[1,16,64]{2,1,0:T(8,128)S(1)}, u32[]{:S(2)}) copy-start(f32[1,16,64]{2,1,0:T(8,128)S(1)} %reduce_window_sum.11) | copy-start | bytes 12292
  6.7 14.1 %all-to-all-start = ((f32[4,16,2176]{2,1,0:T(8,128)}), f32[4,16,2176]{2,1,0:T(8,128)S(1)}, u32[]{:S(2)}, u32[]{:S(2)}) async-start(f32[4,16,2176]{2,1,0:T(8,128)} %pad_maximum_fusion), calls=%async_computation | async-start | bytes 1114112 | tf_op jit(solution)/shard_map/all_to_all | solution.py:103
  23.2 45.1 %copy-start.6 = (bf16[64,128]{1,0:T(8,128)(2,1)S(1)}, bf16[64,128]{1,0:T(8,128)(2,1)}, u32[]{:S(2)}) copy-start(bf16[64,128]{1,0:T(8,128)(2,1)} %param.14) | copy-start | bytes 49156
  36.9 25.8 %all-to-all-start.2 = ((f32[4,16,640]{2,1,0:T(8,128)}), f32[4,16,640]{2,1,0:T(8,128)S(1)}, u32[]{:S(2)}, u32[]{:S(2)}) async-start(f32[4,16,640]{2,1,0:T(8,128)} %broadcast_in_dim.389), calls=%async_computation.2 | async-start | bytes 327680 | tf_op jit(solution)/shard_map/all_to_all | solution.py:68
  64.3 9.9 %all-to-all-start.3 = ((f32[4,16,512]{2,1,0:T(8,128)}), f32[4,16,512]{2,1,0:T(8,128)}, u32[]{:S(2)}, u32[]{:S(2)}) async-start(f32[4,16,512]{2,1,0:T(8,128)} %pad_maximum_fusion.3), calls=%async_computation.3 | async-start | bytes 262144 | tf_op jit(solution)/shard_map/all_to_all | solution.py:119
  80.1 4.7 %copy-start.1 = (f32[1,16,2048]{1,2,0:T(8,128)S(1)}, f32[1,16,2048]{1,2,0:T(8,128)}, u32[]{:S(2)}) copy-start(f32[1,16,2048]{1,2,0:T(8,128)} %get-tuple-element.30) | copy-start | bytes 393220
  80.1 9.9 %copy-start.2 = (bf16[64,1024]{1,0:T(8,128)(2,1)S(1)}, bf16[64,1024]{1,0:T(8,128)(2,1)}, u32[]{:S(2)}) copy-start(bf16[64,1024]{1,0:T(8,128)(2,1)} %param.11) | copy-start | bytes 393220
  86.0 11.5 %all-to-all-start.4 = ((f32[4,16,2048]{2,1,0:T(8,128)}), f32[4,16,2048]{2,1,0:T(8,128)S(1)}, u32[]{:S(2)}, u32[]{:S(2)}) async-start(f32[4,16,2048]{2,1,0:T(8,128)} %pad_maximum_fusion.1), calls=%async_computation.4 | async-start | bytes 1048576 | tf_op jit(solution)/shard_map/all_to_all | solution.py:119
  93.1 9.4 %copy-start.4 = (bf16[64,1024]{1,0:T(8,128)(2,1)S(1)}, bf16[64,1024]{1,0:T(8,128)(2,1)}, u32[]{:S(2)}) copy-start(bf16[64,1024]{1,0:T(8,128)(2,1)} %param.12) | copy-start | bytes 393220
  100.0 13.3 %copy-start.8 = (bf16[64,128]{1,0:T(8,128)(2,1)S(1)}, bf16[64,128]{1,0:T(8,128)(2,1)}, u32[]{:S(2)}) copy-start(bf16[64,128]{1,0:T(8,128)(2,1)} %param.21) | copy-start | bytes 49156
  103.5 46.5 %copy-start.3 = (bf16[64,1024]{1,0:T(8,128)(2,1)}, bf16[64,1024]{1,0:T(8,128)(2,1)S(1)}, u32[]{:S(2)}) copy-start(bf16[64,1024]{1,0:T(8,128)(2,1)S(1)} %multiply_convert_fusion) | copy-start | bytes 393220
  148.1 5.7 %copy-start.7 = (bf16[64,512]{1,0:T(8,128)(2,1)S(1)}, bf16[64,512]{1,0:T(8,128)(2,1)}, u32[]{:S(2)}) copy-start(bf16[64,512]{1,0:T(8,128)(2,1)} %param.20) | copy-start | bytes 196612
  150.0 27.9 %all-to-all-start.8 = ((bf16[4,4,4,2,1,64,128]{6,5,1,2,4,3,0:T(8,128)(2,1)}), bf16[4,4,4,2,1,64,128]{6,5,1,2,4,3,0:T(8,128)(2,1)S(1)}, u32[]{:S(2)}, u32[]{:S(2)}) async-start(bf16[4,4,4,2,1,64,128]{6,5,1,2,4,3,0:T(8,128)(2,1)} %broadcast_in_dim.403), calls=%async_computation.8 | async-start | bytes 4194304 | tf_op jit(solution)/shard_map/all_to_all | solution.py:68

commit v7 on v6

--- a/solution.py
+++ b/solution.py
@@ -78,17 +78,15 @@
 
 
 def pack_decay(state, decay):
-    lanes = 128
-    return jnp.concatenate(
-        [state, jnp.broadcast_to(decay[..., None], decay.shape + (lanes,))], axis=-1
-    )
+    extra = jnp.broadcast_to(decay[..., None, None], decay.shape + (8, state.shape[-1]))
+    return jnp.concatenate([state, extra], axis=-2)
 
 
 def entering_top(axis, decay, state):
-    width = state.shape[1]
+    rows = state.shape[-2]
     gathered = gather_by_exchange(pack_decay(state, decay), axis)
-    weights = masked_weights(gathered[:, :, width], lax.axis_index(axis))
-    return jnp.sum(weights[:, :, None] * gathered[:, :, :width], axis=0)
+    weights = masked_weights(gathered[:, :, rows, 0], lax.axis_index(axis))
+    return jnp.sum(weights[:, :, None, None] * gathered[:, :, :rows], axis=0)
 
 
 def entering_state(axes, decay, state):
@@ -96,16 +94,15 @@
         return entering_top(axes[0], decay, state)
     axis = axes[0]
     count = lax.axis_size(axis)
-    head_total, width = state.shape
-    chunk = width // count
-    pieces = jnp.transpose(state.reshape(head_total, count, chunk), (1, 0, 2))
-    packed = pack_decay(pieces, jnp.broadcast_to(decay, (count, head_total)))
+    head_total, rows, lanes = state.shape
+    part = head_total // count
+    packed = pack_decay(state.reshape(count, part, rows, lanes), decay.reshape(count, part))
     received = lax.all_to_all(packed, axis, 0, 0, tiled=True)
-    decays = received[:, :, chunk]
-    states = received[:, :, :chunk]
+    decays = received[:, :, rows, 0]
+    states = received[:, :, :rows]
     member = jnp.arange(count)
     prefixes = [
-        jnp.sum(masked_weights(decays, upto)[:, :, None] * states, axis=0)
+        jnp.sum(masked_weights(decays, upto)[:, :, None, None] * states, axis=0)
         for upto in range(count + 1)
     ]
     decay_before = [
@@ -114,15 +111,20 @@
     ]
     group_in = entering_state(axes[1:], decay_before[count], prefixes[count])
     outgoing = jnp.stack(
-        [decay_before[upto][:, None] * group_in + prefixes[upto] for upto in range(count)]
+        [
+            decay_before[upto][:, None, None] * group_in + prefixes[upto]
+            for upto in range(count)
+        ]
     )
     returned = lax.all_to_all(outgoing, axis, 0, 0, tiled=True)
-    return jnp.transpose(returned, (1, 0, 2)).reshape(head_total, width)
+    return returned.reshape(head_total, rows, lanes)
 
 
 def carried_state(totals, summary):
     head_total = totals.size
-    state_in = entering_state(SEQ_AXES, totals.reshape(head_total), summary.reshape(head_total, -1))
+    state_in = entering_state(
+        SEQ_AXES, totals.reshape(head_total), summary.reshape((head_total,) + summary.shape[-2:])
+    )
     return state_in.reshape(summary.shape)
 
 

time: 183 us -> 171 us (0.934)
  local copies, waits for them, and re-layouts: 25.7 us -> 11.8 us
  waiting for transfers between devices: 49.9 us -> 55 us
  other arithmetic: 12.9 us -> 11 us
    add x8 -> x0, local copies, waits for them, and re-layouts: 5.4 us -> none  [entering_state(): decay_before[upto][:, None] * group_in + prefixes[upto]]
    unnamed x25 -> x17, local copies, waits for them, and re-layouts: 4.36 us -> 0.68 us
    transpose x2 -> x0, local copies, waits for them, and re-layouts: 3.38 us -> none  [entering_state(): return jnp.transpose(returned, (1, 0, 2)).reshape(head_total, width)]
    all_to_all x2, waiting for transfers between devices: 3.41 us -> 6.66 us  [entering_state(): returned = lax.all_to_all(outgoing, axis, 0, 0, tiled=True)]
    another operation x6 -> x1, local copies, waits for them, and re-layouts: 3.02 us -> 1.12 us
  transfers between devices with their start and end apart: 5 -> 5, of which waited for: 5 -> 5; matrix products, arithmetic and copies ran while one was open for 6% -> 4% of each run, Pallas kernels for 0% -> 0%
where the time goes in v7:
time: 171 us; the launch traced here: 170 us
  blocking collectives  56 us (33%)
  waiting for transfers between devices  55 us (32%)
  starting transfers between devices  27.2 us (16%)
  local copies, waits for them, and re-layouts  11.8 us (7%)
  other arithmetic  11 us (6%)
  matrix products  7.85 us (5%)
    all_to_all x2, waiting for transfers between devices, gather_by_exchange(): return lax.all_to_all(repeated, axis, 0, 0, tiled=True)  38.2 us
    all_to_all x2, blocking collectives, gather_by_exchange(): return lax.all_to_all(repeated, axis, 0, 0, tiled=True)  34.7 us
    all_to_all x2, starting transfers between devices, gather_by_exchange(): return lax.all_to_all(repeated, axis, 0, 0, tiled=True)  16 us
    all_to_all x1, blocking collectives, entering_state(): received = lax.all_to_all(packed, axis, 0, 0, tiled=True)  12.4 us
    all_to_all x1, waiting for transfers between devices, entering_state(): received = lax.all_to_all(packed, axis, 0, 0, tiled=True)  10.1 us
    all_to_all x1, blocking collectives, per_device(): exchanged = lax.all_to_all(partials, 'tp', 0, 0, tiled=True)  8.98 us
    all_to_all x2, starting transfers between devices, entering_state(): returned = lax.all_to_all(outgoing, axis, 0, 0, tiled=True)  6.79 us
    all_to_all x2, waiting for transfers between devices, entering_state(): returned = lax.all_to_all(outgoing, axis, 0, 0, tiled=True)  6.66 us
  transfers between devices with their start and end apart: 5, of which 5 were waited for; matrix products, arithmetic and copies ran while one was open for 4% of the time, Pallas kernels for 0%

profile of v7, /device:TPU:16, one launch (start us, length us, event | category | flops | bytes accessed | tf_op | source)
XLA Modules:
  0.0 169.8 jit_solution(13290750425253606278)
XLA Ops:
  2.6 1.3 multiply_bitcast_fusion.1
  4.0 1.1 reshape.1076
  6.1 0.9 pad_maximum_fusion
  6.9 4.4 %all-to-all-start = ((f32[4,4,72,128]{3,2,1,0:T(8,128)}), f32[4,4,72,128]{3,2,1,0:T(8,128)S(1)}, u32[]{:S(2)}, u32[]{:S(2)}) async-start(f32[4,4,72,128]{3,2,1,0:T(8,128)} %pad_maximum_fusion), calls=%async_computation | async-start | bytes 1179648 | tf_op jit(solution)/shard_map/all_to_all | solution.py:100
  11.4 10.1 %all-to-all-done = f32[4,4,72,128]{3,2,1,0:T(8,128)S(1)} async-done(((f32[4,4,72,128]{3,2,1,0:T(8,128)}), f32[4,4,72,128]{3,2,1,0:T(8,128)S(1)}, u32[]{:S(2)}, u32[]{:S(2)}) %all-to-all-start) | async-done | bytes 589856 | tf_op jit(solution)/shard_map/all_to_all | solution.py:100
  22.2 12.4 %all_to_all.45 = f32[4,1,72,128]{3,2,1,0:T(8,128)S(1)} all-to-all(f32[4,1,72,128]{3,2,1,0:T(8,128)S(1)} %pad_maximum_fusion.2), channel_id=1, replica_groups=mesh['zh'=4,'zl'=4,'sx'=4,'tp'=8] {'zl'}, dimensions={0} | all-to-all | bytes 294912 | tf_op jit(solution)/shard_map/all_to_all | solution.py:100
  37.1 12.4 %all-to-all-start.2 = ((f32[4,1,72,128]{3,2,1,0:T(8,128)}), f32[4,1,72,128]{3,2,1,0:T(8,128)S(1)}, u32[]{:S(2)}, u32[]{:S(2)}) async-start(f32[4,1,72,128]{3,2,1,0:T(8,128)} %broadcast_in_dim.334), calls=%async_computation.2 | async-start | bytes 294912 | tf_op jit(solution)/shard_map/all_to_all | solution.py:68
  49.5 13.3 %all-to-all-done.2 = f32[4,1,72,128]{3,2,1,0:T(8,128)S(1)} async-done(((f32[4,1,72,128]{3,2,1,0:T(8,128)}), f32[4,1,72,128]{3,2,1,0:T(8,128)S(1)}, u32[]{:S(2)}, u32[]{:S(2)}) %all-to-all-start.2) | async-done | bytes 147488 | tf_op jit(solution)/shard_map/all_to_all | solution.py:68
  63.1 2.0 %add_bitcast_fusion.3 = (f32[1,1,64,128]{3,2,1,0:T(8,128)S(1)}, f32[1,1,64,128]{3,2,1,0:T(8,128)S(1)}, f32[1,1,64,128]{3,2,1,0:T(8,128)S(1)}, f32[1,1,64,128]{3,2,1,0:T(8,128)S(1)}) fusion(f32[64,128]{1,0:T(8,128)S(1)} %fusion.32, f32[64,128]{1,0:T(8,128)S(1)} %get-tuple-element.7, f32[64,128]{1,0:T(8,128)S(1)} %get-tuple-element.10, f32[]{:T(128)} %get-tuple-element.24, ...), kind=kLoop, calls=%fused_computation.70 | loop fusion | flops 57344 | bytes 294924 | tf_op jit(solution)/shard_map/add | solution.py:115
  65.7 3.3 %all-to-all-start.3 = ((f32[4,1,64,128]{3,2,1,0:T(8,128)}), f32[4,1,64,128]{3,2,1,0:T(8,128)S(1)}, u32[]{:S(2)}, u32[]{:S(2)}) async-start(f32[4,1,64,128]{3,2,1,0:T(8,128)} %pad_maximum_fusion.3), calls=%async_computation.3 | async-start | bytes 262144 | tf_op jit(solution)/shard_map/all_to_all | solution.py:119
  69.8 5.1 %all-to-all-done.3 = f32[4,1,64,128]{3,2,1,0:T(8,128)S(1)} async-done(((f32[4,1,64,128]{3,2,1,0:T(8,128)}), f32[4,1,64,128]{3,2,1,0:T(8,128)S(1)}, u32[]{:S(2)}, u32[]{:S(2)}) %all-to-all-start.3) | async-done | bytes 131104 | tf_op jit(solution)/shard_map/all_to_all | solution.py:119
  75.9 3.5 %all-to-all-start.4 = ((f32[4,4,64,128]{3,2,1,0:T(8,128)}), f32[4,4,64,128]{3,2,1,0:T(8,128)S(1)}, u32[]{:S(2)}, u32[]{:S(2)}) async-start(f32[4,4,64,128]{3,2,1,0:T(8,128)} %pad_maximum_fusion.1), calls=%async_computation.4 | async-start | bytes 1048576 | tf_op jit(solution)/shard_map/all_to_all | solution.py:119
  80.1 2.9 %copy.86 = bf16[1024,1024]{1,0:T(8,128)(2,1)S(1)} copy(bf16[1024,1024]{0,1:T(8,128)(2,1)} %bitcast.127) | data formatting | bytes 4194304 | tf_op jit(solution)/shard_map/dot_general | solution.py:153
  83.0 2.1 %convolution_bitcast_fusion.1 = f32[64,1,16,64]{3,0,2,1:T(8,128)} fusion(bf16[64,16,64]{2,1,0:T(8,128)(2,1)S(1)} %reshape.1076, f32[16,64]{1,0:T(8,128)} %get-tuple-element.41, f32[16,64]{1,0:T(8,128)} %bitcast.137, f32[64,64]{1,0:T(8,128)} %fusion.53, pred[64,64]{1,0:T(8,128)(4,1)} %iota_compare_fusion.1), kind=kOutput, calls=%fused_computation.11 | convolution fusion | flops 50593792 | bytes 421888 | tf_op jit(solution)/shard_map/gkts,sgkp->tgkp/dot_general | solution.py:28
  85.9 1.5 all-to-all-done.4
  87.4 2.0 %fusion.9 = f32[64,1,16,64]{3,0,2,1:T(8,128)S(1)} fusion(f32[64,1,16,64]{3,0,2,1:T(8,128)} %convolution_bitcast_fusion.1, f32[16,64,128]{2,1,0:T(8,128)S(1)} %bitcast.126, f32[64,1,16,64]{3,2,0,1:T(8,128)S(1)} %reshape.1090, f32[16]{0:T(128)} %param.17, f32[64,16]{0,1:T(8,128)S(1)} %exponential_bitcast_fusion, bf16[64,128]{1,0:T(8,128)(2,1)} %param.14), kind=kOutput, calls=%fused_computation.14 | convolution fusion | flops 100925440 | bytes 1331264 | tf_op jit(solution)/shard_map/tgn,gkpn->tgkp/dot_general | solution.py:35
  91.0 9.0 %all_to_all.46 = f32[8,64,128]{2,1,0:T(8,128)S(1)} all-to-all(f32[8,64,128]{2,1,0:T(8,128)S(1)} %convolution_bitcast_fusion.2), channel_id=1, replica_groups=mesh['zh'=4,'zl'=4,'sx'=4,'tp'=8] {'tp'}, dimensions={0} | all-to-all | bytes 524288 | tf_op jit(solution)/shard_map/all_to_all | solution.py:157
  100.8 19.4 %all_to_all.47 = bf16[4,2,1,64,128]{4,3,1,2,0:T(8,128)(2,1)S(1)} all-to-all(bf16[4,2,1,64,128]{4,3,1,2,0:T(8,128)(2,1)S(1)} %broadcast_in_dim.344), channel_id=1, replica_groups=mesh['zh'=4,'zl'=4,'sx'=4,'tp'=8] {'zh'}, dimensions={0} | all-to-all | bytes 262144 | tf_op jit(solution)/shard_map/all_to_all | solution.py:68
  120.3 15.3 %all_to_all.48 = bf16[4,4,2,1,64,128]{5,4,1,2,3,0:T(8,128)(2,1)S(1)} all-to-all(bf16[4,4,2,1,64,128]{5,4,1,2,3,0:T(8,128)(2,1)S(1)} %broadcast_in_dim.346), channel_id=1, replica_groups=mesh['zh'=4,'zl'=4,'sx'=4,'tp'=8] {'zl'}, dimensions={0} | all-to-all | bytes 1048576 | tf_op jit(solution)/shard_map/all_to_all | solution.py:68
  135.6 1.9 %broadcast_in_dim.348 = bf16[4,4,4,2,1,64,128]{6,5,1,2,4,3,0:T(8,128)(2,1)} broadcast(bf16[4,4,2,64,128]{4,3,0,1,2:T(8,128)(2,1)S(1)} %copy.80), dimensions={1,2,3,5,6} | broadcast | bytes 2621440 | tf_op jit(solution)/shard_map/broadcast_in_dim | solution.py:67
  137.5 3.6 %all-to-all-start.8 = ((bf16[4,4,4,2,1,64,128]{6,5,1,2,4,3,0:T(8,128)(2,1)}), bf16[4,4,4,2,1,64,128]{6,5,1,2,4,3,0:T(8,128)(2,1)S(1)}, u32[]{:S(2)}, u32[]{:S(2)}) async-start(bf16[4,4,4,2,1,64,128]{6,5,1,2,4,3,0:T(8,128)(2,1)} %broadcast_in_dim.348), calls=%async_computation.8 | async-start | bytes 4194304 | tf_op jit(solution)/shard_map/all_to_all | solution.py:68
  141.3 25.0 %all-to-all-done.8 = bf16[4,4,4,2,1,64,128]{6,5,1,2,4,3,0:T(8,128)(2,1)S(1)} async-done(((bf16[4,4,4,2,1,64,128]{6,5,1,2,4,3,0:T(8,128)(2,1)}), bf16[4,4,4,2,1,64,128]{6,5,1,2,4,3,0:T(8,128)(2,1)S(1)}, u32[]{:S(2)}, u32[]{:S(2)}) %all-to-all-start.8) | async-done | bytes 2097184 | tf_op jit(solution)/shard_map/all_to_all | solution.py:68
  166.7 0.9 fusion.52
  168.2 0.9 fusion.13
  (82 shorter events, 14.6 us)
Async XLA Ops:
  0.6 5.0 %copy-start = (bf16[64,128]{1,0:T(8,128)(2,1)S(1)}, bf16[64,128]{1,0:T(8,128)(2,1)}, u32[]{:S(2)}) copy-start(bf16[64,128]{1,0:T(8,128)(2,1)} %param.13) | copy-start | bytes 49156
  2.3 1.6 copy-start.4
  5.3 63.7 %copy-start.5 = (bf16[64,128]{1,0:T(8,128)(2,1)S(1)}, bf16[64,128]{1,0:T(8,128)(2,1)}, u32[]{:S(2)}) copy-start(bf16[64,128]{1,0:T(8,128)(2,1)} %param.14) | copy-start | bytes 49156
  6.9 73.1 %copy-start.1 = (bf16[64,1024]{1,0:T(8,128)(2,1)S(1)}, bf16[64,1024]{1,0:T(8,128)(2,1)}, u32[]{:S(2)}) copy-start(bf16[64,1024]{1,0:T(8,128)(2,1)} %param.11) | copy-start | bytes 393220
  6.9 14.6 %all-to-all-start = ((f32[4,4,72,128]{3,2,1,0:T(8,128)}), f32[4,4,72,128]{3,2,1,0:T(8,128)S(1)}, u32[]{:S(2)}, u32[]{:S(2)}) async-start(f32[4,4,72,128]{3,2,1,0:T(8,128)} %pad_maximum_fusion), calls=%async_computation | async-start | bytes 1179648 | tf_op jit(solution)/shard_map/all_to_all | solution.py:100
  37.1 25.7 %all-to-all-start.2 = ((f32[4,1,72,128]{3,2,1,0:T(8,128)}), f32[4,1,72,128]{3,2,1,0:T(8,128)S(1)}, u32[]{:S(2)}, u32[]{:S(2)}) async-start(f32[4,1,72,128]{3,2,1,0:T(8,128)} %broadcast_in_dim.334), calls=%async_computation.2 | async-start | bytes 294912 | tf_op jit(solution)/shard_map/all_to_all | solution.py:68
  65.7 9.2 %all-to-all-start.3 = ((f32[4,1,64,128]{3,2,1,0:T(8,128)}), f32[4,1,64,128]{3,2,1,0:T(8,128)S(1)}, u32[]{:S(2)}, u32[]{:S(2)}) async-start(f32[4,1,64,128]{3,2,1,0:T(8,128)} %pad_maximum_fusion.3), calls=%async_computation.3 | async-start | bytes 262144 | tf_op jit(solution)/shard_map/all_to_all | solution.py:119
  75.9 11.5 %all-to-all-start.4 = ((f32[4,4,64,128]{3,2,1,0:T(8,128)}), f32[4,4,64,128]{3,2,1,0:T(8,128)S(1)}, u32[]{:S(2)}, u32[]{:S(2)}) async-start(f32[4,4,64,128]{3,2,1,0:T(8,128)} %pad_maximum_fusion.1), calls=%async_computation.4 | async-start | bytes 1048576 | tf_op jit(solution)/shard_map/all_to_all | solution.py:119
  80.1 9.8 %copy-start.3 = (bf16[64,1024]{1,0:T(8,128)(2,1)S(1)}, bf16[64,1024]{1,0:T(8,128)(2,1)}, u32[]{:S(2)}) copy-start(bf16[64,1024]{1,0:T(8,128)(2,1)} %param.12) | copy-start | bytes 393220
  85.2 5.0 %copy-start.7 = (f32[1024]{0:T(1024)S(1)}, f32[1024]{0:T(1024)}, u32[]{:S(2)}) copy-start(f32[1024]{0:T(1024)} %param.18) | copy-start | bytes 12292
  90.2 47.2 %copy-start.2 = (bf16[64,1024]{1,0:T(8,128)(2,1)}, bf16[64,1024]{1,0:T(8,128)(2,1)S(1)}, u32[]{:S(2)}) copy-start(bf16[64,1024]{1,0:T(8,128)(2,1)S(1)} %multiply_convert_fusion) | copy-start | bytes 393220
  135.6 5.7 %copy-start.6 = (bf16[64,512]{1,0:T(8,128)(2,1)S(1)}, bf16[64,512]{1,0:T(8,128)(2,1)}, u32[]{:S(2)}) copy-start(bf16[64,512]{1,0:T(8,128)(2,1)} %param.20) | copy-start | bytes 196612
  137.5 28.8 %all-to-all-start.8 = ((bf16[4,4,4,2,1,64,128]{6,5,1,2,4,3,0:T(8,128)(2,1)}), bf16[4,4,4,2,1,64,128]{6,5,1,2,4,3,0:T(8,128)(2,1)S(1)}, u32[]{:S(2)}, u32[]{:S(2)}) async-start(bf16[4,4,4,2,1,64,128]{6,5,1,2,4,3,0:T(8,128)(2,1)} %broadcast_in_dim.348), calls=%async_computation.8 | async-start | bytes 4194304 | tf_op jit(solution)/shard_map/all_to_all | solution.py:68

commit v8 on v7

--- a/solution.py
+++ b/solution.py
@@ -159,9 +159,8 @@
     values = jnp.transpose(values.reshape(tokens_here, kv_here, HEAD_DIM), (1, 0, 2))
     key_heads = jnp.transpose(keys.reshape(tokens_here, kv_here, HEAD_DIM), (1, 0, 2))
     pair = jnp.stack([key_heads, values])
-    for axis in SEQ_AXES[::-1]:
-        pair = gather_by_exchange(pair, axis)
-    all_pairs = jnp.transpose(pair, (3, 4, 2, 1, 0, 5, 6)).reshape(2, kv_here, -1, HEAD_DIM)
+    pair = gather_by_exchange(gather_by_exchange(pair, ("zh", "zl")), "sx")
+    all_pairs = jnp.transpose(pair, (2, 3, 1, 0, 4, 5)).reshape(2, kv_here, -1, HEAD_DIM)
     key_portion = all_pairs[0]
     value_portion = all_pairs[1]
     my_index = lax.axis_index(SEQ_AXES[::-1])

time: 171 us -> 169 us (0.988)
  the two profiles are of different devices: /device:TPU:16 before, /device:TPU:32 now
where the time goes in v8:
time: 169 us; the launch traced here: 168 us
  blocking collectives  56 us (33%)
  waiting for transfers between devices  52.7 us (31%)
  starting transfers between devices  27.7 us (16%)
  local copies, waits for them, and re-layouts  11.8 us (7%)
  other arithmetic  11 us (7%)
  matrix products  7.85 us (5%)
    all_to_all x2, waiting for transfers between devices, gather_by_exchange(): return lax.all_to_all(repeated, axis, 0, 0, tiled=True)  36.6 us
    all_to_all x1, blocking collectives, gather_by_exchange(): return lax.all_to_all(repeated, axis, 0, 0, tiled=True)  33.1 us
    all_to_all x2, starting transfers between devices, gather_by_exchange(): return lax.all_to_all(repeated, axis, 0, 0, tiled=True)  16 us
    all_to_all x1, blocking collectives, per_device(): exchanged = lax.all_to_all(partials, 'tp', 0, 0, tiled=True)  11.8 us
    all_to_all x1, blocking collectives, entering_state(): received = lax.all_to_all(packed, axis, 0, 0, tiled=True)  11.1 us
    all_to_all x1, waiting for transfers between devices, entering_state(): received = lax.all_to_all(packed, axis, 0, 0, tiled=True)  10.1 us
    all_to_all x2, starting transfers between devices, entering_state(): returned = lax.all_to_all(outgoing, axis, 0, 0, tiled=True)  7.23 us
    all_to_all x2, waiting for transfers between devices, entering_state(): returned = lax.all_to_all(outgoing, axis, 0, 0, tiled=True)  5.95 us
  transfers between devices with their start and end apart: 5, of which 5 were waited for; matrix products, arithmetic and copies ran while one was open for 4% of the time, Pallas kernels for 0%

profile of v8, /device:TPU:32, one launch (start us, length us, event | category | flops | bytes accessed | tf_op | source)
XLA Modules:
  0.0 167.9 jit_solution(6617347674019524951)
XLA Ops:
  2.6 1.3 multiply_bitcast_fusion.1
  4.0 1.1 reshape.1073
  6.1 0.9 pad_maximum_fusion
  6.9 4.4 %all-to-all-start = ((f32[4,4,72,128]{3,2,1,0:T(8,128)}), f32[4,4,72,128]{3,2,1,0:T(8,128)S(1)}, u32[]{:S(2)}, u32[]{:S(2)}) async-start(f32[4,4,72,128]{3,2,1,0:T(8,128)} %pad_maximum_fusion), calls=%async_computation | async-start | bytes 1179648 | tf_op jit(solution)/shard_map/all_to_all | solution.py:100
  11.4 10.1 %all-to-all-done = f32[4,4,72,128]{3,2,1,0:T(8,128)S(1)} async-done(((f32[4,4,72,128]{3,2,1,0:T(8,128)}), f32[4,4,72,128]{3,2,1,0:T(8,128)S(1)}, u32[]{:S(2)}, u32[]{:S(2)}) %all-to-all-start) | async-done | bytes 589856 | tf_op jit(solution)/shard_map/all_to_all | solution.py:100
  22.2 11.1 %all_to_all.40 = f32[4,1,72,128]{3,2,1,0:T(8,128)S(1)} all-to-all(f32[4,1,72,128]{3,2,1,0:T(8,128)S(1)} %pad_maximum_fusion.2), channel_id=1, replica_groups=mesh['zh'=4,'zl'=4,'sx'=4,'tp'=8] {'zl'}, dimensions={0} | all-to-all | bytes 294912 | tf_op jit(solution)/shard_map/all_to_all | solution.py:100
  35.8 12.4 %all-to-all-start.2 = ((f32[4,1,72,128]{3,2,1,0:T(8,128)}), f32[4,1,72,128]{3,2,1,0:T(8,128)S(1)}, u32[]{:S(2)}, u32[]{:S(2)}) async-start(f32[4,1,72,128]{3,2,1,0:T(8,128)} %broadcast_in_dim.326), calls=%async_computation.2 | async-start | bytes 294912 | tf_op jit(solution)/shard_map/all_to_all | solution.py:68
  48.2 14.2 %all-to-all-done.2 = f32[4,1,72,128]{3,2,1,0:T(8,128)S(1)} async-done(((f32[4,1,72,128]{3,2,1,0:T(8,128)}), f32[4,1,72,128]{3,2,1,0:T(8,128)S(1)}, u32[]{:S(2)}, u32[]{:S(2)}) %all-to-all-start.2) | async-done | bytes 147488 | tf_op jit(solution)/shard_map/all_to_all | solution.py:68
  62.7 2.0 %add_bitcast_fusion.3 = (f32[1,1,64,128]{3,2,1,0:T(8,128)S(1)}, f32[1,1,64,128]{3,2,1,0:T(8,128)S(1)}, f32[1,1,64,128]{3,2,1,0:T(8,128)S(1)}, f32[1,1,64,128]{3,2,1,0:T(8,128)S(1)}) fusion(f32[64,128]{1,0:T(8,128)S(1)} %fusion.32, f32[64,128]{1,0:T(8,128)S(1)} %get-tuple-element.7, f32[64,128]{1,0:T(8,128)S(1)} %get-tuple-element.10, f32[]{:T(128)} %get-tuple-element.24, ...), kind=kLoop, calls=%fused_computation.70 | loop fusion | flops 57344 | bytes 294924 | tf_op jit(solution)/shard_map/add | solution.py:115
  65.4 3.8 %all-to-all-start.3 = ((f32[4,1,64,128]{3,2,1,0:T(8,128)}), f32[4,1,64,128]{3,2,1,0:T(8,128)S(1)}, u32[]{:S(2)}, u32[]{:S(2)}) async-start(f32[4,1,64,128]{3,2,1,0:T(8,128)} %pad_maximum_fusion.3), calls=%async_computation.3 | async-start | bytes 262144 | tf_op jit(solution)/shard_map/all_to_all | solution.py:119
  69.9 4.4 %all-to-all-done.3 = f32[4,1,64,128]{3,2,1,0:T(8,128)S(1)} async-done(((f32[4,1,64,128]{3,2,1,0:T(8,128)}), f32[4,1,64,128]{3,2,1,0:T(8,128)S(1)}, u32[]{:S(2)}, u32[]{:S(2)}) %all-to-all-start.3) | async-done | bytes 131104 | tf_op jit(solution)/shard_map/all_to_all | solution.py:119
  74.4 0.8 pad_maximum_fusion.1
  75.2 3.5 %all-to-all-start.4 = ((f32[4,4,64,128]{3,2,1,0:T(8,128)}), f32[4,4,64,128]{3,2,1,0:T(8,128)S(1)}, u32[]{:S(2)}, u32[]{:S(2)}) async-start(f32[4,4,64,128]{3,2,1,0:T(8,128)} %pad_maximum_fusion.1), calls=%async_computation.4 | async-start | bytes 1048576 | tf_op jit(solution)/shard_map/all_to_all | solution.py:119
  79.5 2.9 %copy.83 = bf16[1024,1024]{1,0:T(8,128)(2,1)S(1)} copy(bf16[1024,1024]{0,1:T(8,128)(2,1)} %bitcast.126) | data formatting | bytes 4194304 | tf_op jit(solution)/shard_map/dot_general | solution.py:153
  82.4 2.1 %convolution_bitcast_fusion.1 = f32[64,1,16,64]{3,0,2,1:T(8,128)} fusion(bf16[64,16,64]{2,1,0:T(8,128)(2,1)S(1)} %reshape.1073, f32[16,64]{1,0:T(8,128)} %get-tuple-element.41, f32[16,64]{1,0:T(8,128)} %bitcast.135, f32[64,64]{1,0:T(8,128)} %fusion.53, pred[64,64]{1,0:T(8,128)(4,1)} %iota_compare_fusion.1), kind=kOutput, calls=%fused_computation.11 | convolution fusion | flops 50593792 | bytes 421888 | tf_op jit(solution)/shard_map/gkts,sgkp->tgkp/dot_general | solution.py:28
  85.2 1.5 all-to-all-done.4
  86.8 2.0 %fusion.9 = f32[64,1,16,64]{3,0,2,1:T(8,128)S(1)} fusion(f32[64,1,16,64]{3,0,2,1:T(8,128)} %convolution_bitcast_fusion.1, f32[16,64,128]{2,1,0:T(8,128)S(1)} %bitcast.125, f32[64,1,16,64]{3,2,0,1:T(8,128)S(1)} %reshape.1087, f32[16]{0:T(128)} %param.17, f32[64,16]{0,1:T(8,128)S(1)} %exponential_bitcast_fusion, bf16[64,128]{1,0:T(8,128)(2,1)} %param.14), kind=kOutput, calls=%fused_computation.14 | convolution fusion | flops 100925440 | bytes 1331264 | tf_op jit(solution)/shard_map/tgn,gkpn->tgkp/dot_general | solution.py:35
  90.4 11.8 %all_to_all.41 = f32[8,64,128]{2,1,0:T(8,128)S(1)} all-to-all(f32[8,64,128]{2,1,0:T(8,128)S(1)} %convolution_bitcast_fusion.2), channel_id=1, replica_groups=mesh['zh'=4,'zl'=4,'sx'=4,'tp'=8] {'tp'}, dimensions={0} | all-to-all | bytes 524288 | tf_op jit(solution)/shard_map/all_to_all | solution.py:157
  103.0 33.1 %all_to_all.42 = bf16[16,2,1,64,128]{4,3,1,2,0:T(8,128)(2,1)S(1)} all-to-all(bf16[16,2,1,64,128]{4,3,1,2,0:T(8,128)(2,1)S(1)} %broadcast_in_dim.336), channel_id=1, replica_groups=mesh['zh'=4,'zl'=4,'sx'=4,'tp'=8] {'zh','zl'}, dimensions={0} | all-to-all | bytes 1048576 | tf_op jit(solution)/shard_map/all_to_all | solution.py:68
  136.2 1.9 %broadcast_in_dim.338 = bf16[4,16,2,1,64,128]{5,4,1,3,2,0:T(8,128)(2,1)} broadcast(bf16[16,2,64,128]{3,2,0,1:T(8,128)(2,1)S(1)} %copy.77), dimensions={1,2,4,5} | broadcast | bytes 2621440 | tf_op jit(solution)/shard_map/broadcast_in_dim | solution.py:67
  138.1 3.6 %all-to-all-start.7 = ((bf16[4,16,2,1,64,128]{5,4,1,3,2,0:T(8,128)(2,1)}), bf16[4,16,2,1,64,128]{5,4,1,3,2,0:T(8,128)(2,1)S(1)}, u32[]{:S(2)}, u32[]{:S(2)}) async-start(bf16[4,16,2,1,64,128]{5,4,1,3,2,0:T(8,128)(2,1)} %broadcast_in_dim.338), calls=%async_computation.7 | async-start | bytes 4194304 | tf_op jit(solution)/shard_map/all_to_all | solution.py:68
  141.8 22.4 %all-to-all-done.7 = bf16[4,16,2,1,64,128]{5,4,1,3,2,0:T(8,128)(2,1)S(1)} async-done(((bf16[4,16,2,1,64,128]{5,4,1,3,2,0:T(8,128)(2,1)}), bf16[4,16,2,1,64,128]{5,4,1,3,2,0:T(8,128)(2,1)S(1)}, u32[]{:S(2)}, u32[]{:S(2)}) %all-to-all-start.7) | async-done | bytes 2097184 | tf_op jit(solution)/shard_map/all_to_all | solution.py:68
  164.7 0.9 fusion.52
  166.3 0.9 fusion.13
  (79 shorter events, 13.7 us)
Async XLA Ops:
  0.6 5.0 %copy-start = (bf16[64,128]{1,0:T(8,128)(2,1)S(1)}, bf16[64,128]{1,0:T(8,128)(2,1)}, u32[]{:S(2)}) copy-start(bf16[64,128]{1,0:T(8,128)(2,1)} %param.13) | copy-start | bytes 49156
  2.3 1.6 copy-start.4
  5.3 63.8 %copy-start.5 = (bf16[64,128]{1,0:T(8,128)(2,1)S(1)}, bf16[64,128]{1,0:T(8,128)(2,1)}, u32[]{:S(2)}) copy-start(bf16[64,128]{1,0:T(8,128)(2,1)} %param.14) | copy-start | bytes 49156
  6.9 72.4 %copy-start.1 = (bf16[64,1024]{1,0:T(8,128)(2,1)S(1)}, bf16[64,1024]{1,0:T(8,128)(2,1)}, u32[]{:S(2)}) copy-start(bf16[64,1024]{1,0:T(8,128)(2,1)} %param.11) | copy-start | bytes 393220
  6.9 14.6 %all-to-all-start = ((f32[4,4,72,128]{3,2,1,0:T(8,128)}), f32[4,4,72,128]{3,2,1,0:T(8,128)S(1)}, u32[]{:S(2)}, u32[]{:S(2)}) async-start(f32[4,4,72,128]{3,2,1,0:T(8,128)} %pad_maximum_fusion), calls=%async_computation | async-start | bytes 1179648 | tf_op jit(solution)/shard_map/all_to_all | solution.py:100
  35.8 26.6 %all-to-all-start.2 = ((f32[4,1,72,128]{3,2,1,0:T(8,128)}), f32[4,1,72,128]{3,2,1,0:T(8,128)S(1)}, u32[]{:S(2)}, u32[]{:S(2)}) async-start(f32[4,1,72,128]{3,2,1,0:T(8,128)} %broadcast_in_dim.326), calls=%async_computation.2 | async-start | bytes 294912 | tf_op jit(solution)/shard_map/all_to_all | solution.py:68
  65.4 8.9 %all-to-all-start.3 = ((f32[4,1,64,128]{3,2,1,0:T(8,128)}), f32[4,1,64,128]{3,2,1,0:T(8,128)S(1)}, u32[]{:S(2)}, u32[]{:S(2)}) async-start(f32[4,1,64,128]{3,2,1,0:T(8,128)} %pad_maximum_fusion.3), calls=%async_computation.3 | async-start | bytes 262144 | tf_op jit(solution)/shard_map/all_to_all | solution.py:119
  75.2 11.5 %all-to-all-start.4 = ((f32[4,4,64,128]{3,2,1,0:T(8,128)}), f32[4,4,64,128]{3,2,1,0:T(8,128)S(1)}, u32[]{:S(2)}, u32[]{:S(2)}) async-start(f32[4,4,64,128]{3,2,1,0:T(8,128)} %pad_maximum_fusion.1), calls=%async_computation.4 | async-start | bytes 1048576 | tf_op jit(solution)/shard_map/all_to_all | solution.py:119
  79.5 9.8 %copy-start.3 = (bf16[64,1024]{1,0:T(8,128)(2,1)S(1)}, bf16[64,1024]{1,0:T(8,128)(2,1)}, u32[]{:S(2)}) copy-start(bf16[64,1024]{1,0:T(8,128)(2,1)} %param.12) | copy-start | bytes 393220
  84.5 5.0 %copy-start.7 = (f32[1024]{0:T(1024)S(1)}, f32[1024]{0:T(1024)}, u32[]{:S(2)}) copy-start(f32[1024]{0:T(1024)} %param.18) | copy-start | bytes 12292
  89.6 48.5 %copy-start.2 = (bf16[64,1024]{1,0:T(8,128)(2,1)}, bf16[64,1024]{1,0:T(8,128)(2,1)S(1)}, u32[]{:S(2)}) copy-start(bf16[64,1024]{1,0:T(8,128)(2,1)S(1)} %multiply_convert_fusion) | copy-start | bytes 393220
  136.2 5.7 %copy-start.6 = (bf16[64,512]{1,0:T(8,128)(2,1)S(1)}, bf16[64,512]{1,0:T(8,128)(2,1)}, u32[]{:S(2)}) copy-start(bf16[64,512]{1,0:T(8,128)(2,1)} %param.20) | copy-start | bytes 196612
  138.1 26.2 %all-to-all-start.7 = ((bf16[4,16,2,1,64,128]{5,4,1,3,2,0:T(8,128)(2,1)}), bf16[4,16,2,1,64,128]{5,4,1,3,2,0:T(8,128)(2,1)S(1)}, u32[]{:S(2)}, u32[]{:S(2)}) async-start(bf16[4,16,2,1,64,128]{5,4,1,3,2,0:T(8,128)(2,1)} %broadcast_in_dim.338), calls=%async_computation.7 | async-start | bytes 4194304 | tf_op jit(solution)/shard_map/all_to_all | solution.py:68

commit v9 on v8

--- a/solution.py
+++ b/solution.py
@@ -10,7 +10,8 @@
 QHEADS = 32
 KVHEADS = 8
 HEAD_DIM = 128
-SEQ_AXES = ("sx", "zl", "zh")
+SEQ_AXES = (("zl", "sx"), "zh")
+ROWS = ("zh", "zl", "sx")
 
 
 highest = lax.Precision.HIGHEST
@@ -101,21 +102,21 @@
     decays = received[:, :, rows, 0]
     states = received[:, :, :rows]
     member = jnp.arange(count)
-    prefixes = [
-        jnp.sum(masked_weights(decays, upto)[:, :, None, None] * states, axis=0)
-        for upto in range(count + 1)
-    ]
-    decay_before = [
-        jnp.prod(jnp.where((member < upto)[:, None], decays, 1.0), axis=0)
-        for upto in range(count + 1)
-    ]
+    bounds = jnp.arange(count + 1)
+    earlier = member[None, :, None]
+    between = (member[None, None, :] > member[None, :, None]) & (
+        member[None, None, :] < bounds[:, None, None]
+    )
+    spans = jnp.prod(
+        jnp.where(between[:, :, :, None], decays[None, None, :, :], 1.0), axis=2
+    )
+    weights = jnp.where(earlier < bounds[:, None, None], spans, 0.0)
+    prefixes = jnp.sum(weights[:, :, :, None, None] * states[None], axis=1)
+    decay_before = jnp.prod(
+        jnp.where(earlier < bounds[:, None, None], decays[None], 1.0), axis=1
+    )
     group_in = entering_state(axes[1:], decay_before[count], prefixes[count])
-    outgoing = jnp.stack(
-        [
-            decay_before[upto][:, None, None] * group_in + prefixes[upto]
-            for upto in range(count)
-        ]
-    )
+    outgoing = decay_before[:count, :, None, None] * group_in[None] + prefixes[:count]
     returned = lax.all_to_all(outgoing, axis, 0, 0, tiled=True)
     return returned.reshape(head_total, rows, lanes)
 
@@ -163,7 +164,7 @@
     all_pairs = jnp.transpose(pair, (2, 3, 1, 0, 4, 5)).reshape(2, kv_here, -1, HEAD_DIM)
     key_portion = all_pairs[0]
     value_portion = all_pairs[1]
-    my_index = lax.axis_index(SEQ_AXES[::-1])
+    my_index = lax.axis_index(ROWS)
     query_block = query_layout(queries, kv_here, per_kv)
     query_pos = row_positions(my_index * tokens_here, tokens_here, per_kv)
     key_pos = jnp.arange(key_portion.shape[1], dtype=jnp.int32)
@@ -186,9 +187,9 @@
     seq_count = mesh.shape["seq"]
     split = Mesh(
         mesh.devices.reshape(seq_count // 16, 4, 4, mesh.shape["tp"]),
-        SEQ_AXES[::-1] + ("tp",),
-    )
-    rows = SEQ_AXES[::-1]
+        ROWS + ("tp",),
+    )
+    rows = ROWS
     placed = (
         P(rows, "tp"),
         P(rows, "tp"),

time: 169 us -> 163 us (0.964)
  blocking collectives: 56 us -> 45.6 us
  waiting for transfers between devices: 52.7 us -> 57.8 us
  other arithmetic: 11 us -> 7.5 us
  starting transfers between devices: 27.7 us -> 30 us
    all_to_all x1 -> x0, blocking collectives: 11.1 us -> none  [entering_state(): received = lax.all_to_all(packed, axis, 0, 0, tiled=True)]
    all_to_all x1, waiting for transfers between devices: 10.1 us -> 15.7 us  [entering_state(): received = lax.all_to_all(packed, axis, 0, 0, tiled=True)]
    all_to_all x1, starting transfers between devices: 4.42 us -> 8.87 us  [entering_state(): received = lax.all_to_all(packed, axis, 0, 0, tiled=True)]
    all_to_all x2 -> x1, starting transfers between devices: 7.23 us -> 5.09 us  [entering_state(): returned = lax.all_to_all(outgoing, axis, 0, 0, tiled=True)]
    all_to_all x2 -> x1, waiting for transfers between devices: 5.95 us -> 4.52 us  [entering_state(): returned = lax.all_to_all(outgoing, axis, 0, 0, tiled=True)]
  transfers between devices with their start and end apart: 5 -> 4, of which waited for: 5 -> 4; matrix products, arithmetic and copies ran while one was open for 4% -> 4% of each run, Pallas kernels for 0% -> 0%
where the time goes in v9:
time: 163 us; the launch traced here: 162 us
  waiting for transfers between devices  57.8 us (35%)
  blocking collectives  45.6 us (28%)
  starting transfers between devices  30 us (18%)
  local copies, waits for them, and re-layouts  12.4 us (8%)
  matrix products  8.09 us (5%)
  other arithmetic  7.5 us (5%)
    all_to_all x2, waiting for transfers between devices, gather_by_exchange(): return lax.all_to_all(repeated, axis, 0, 0, tiled=True)  37.6 us
    all_to_all x1, blocking collectives, gather_by_exchange(): return lax.all_to_all(repeated, axis, 0, 0, tiled=True)  33.8 us
    all_to_all x2, starting transfers between devices, gather_by_exchange(): return lax.all_to_all(repeated, axis, 0, 0, tiled=True)  16 us
    all_to_all x1, waiting for transfers between devices, entering_state(): received = lax.all_to_all(packed, axis, 0, 0, tiled=True)  15.7 us
    all_to_all x1, blocking collectives, per_device(): exchanged = lax.all_to_all(partials, 'tp', 0, 0, tiled=True)  11.8 us
    all_to_all x1, starting transfers between devices, entering_state(): received = lax.all_to_all(packed, axis, 0, 0, tiled=True)  8.87 us
    all_to_all x1, starting transfers between devices, entering_state(): returned = lax.all_to_all(outgoing, axis, 0, 0, tiled=True)  5.09 us
    all_to_all x1, waiting for transfers between devices, entering_state(): returned = lax.all_to_all(outgoing, axis, 0, 0, tiled=True)  4.52 us
  transfers between devices with their start and end apart: 4, of which 4 were waited for; matrix products, arithmetic and copies ran while one was open for 4% of the time, Pallas kernels for 0%

profile of v9, /device:TPU:32, one launch (start us, length us, event | category | flops | bytes accessed | tf_op | source)
XLA Modules:
  0.0 162.2 jit_solution(2620891404975854853)
XLA Ops:
  1.3 0.8 multiply_bitcast_fusion.1
  2.9 1.3 multiply_bitcast_fusion
  4.2 1.1 copy.70
  5.8 0.9 maximum_bitcast_fusion
  6.7 8.9 %all-to-all-start = ((f32[16,1,72,128]{3,2,1,0:T(8,128)}), f32[16,1,72,128]{3,2,1,0:T(8,128)S(1)}, u32[]{:S(2)}, u32[]{:S(2)}) async-start(f32[16,1,72,128]{3,2,1,0:T(8,128)} %maximum_bitcast_fusion), calls=%async_computation | async-start | bytes 1179648 | tf_op jit(solution)/shard_map/all_to_all | solution.py:101
  15.6 15.7 %all-to-all-done = f32[16,1,72,128]{3,2,1,0:T(8,128)S(1)} async-done(((f32[16,1,72,128]{3,2,1,0:T(8,128)}), f32[16,1,72,128]{3,2,1,0:T(8,128)S(1)}, u32[]{:S(2)}, u32[]{:S(2)}) %all-to-all-start) | async-done | bytes 589856 | tf_op jit(solution)/shard_map/all_to_all | solution.py:101
  32.5 1.3 multiply_reduce_fusion
  35.2 12.4 %all-to-all-start.1 = ((f32[4,1,72,128]{3,2,1,0:T(8,128)}), f32[4,1,72,128]{3,2,1,0:T(8,128)S(1)}, u32[]{:S(2)}, u32[]{:S(2)}) async-start(f32[4,1,72,128]{3,2,1,0:T(8,128)} %broadcast_in_dim.134), calls=%async_computation.1 | async-start | bytes 294912 | tf_op jit(solution)/shard_map/all_to_all | solution.py:69
  47.6 15.1 %all-to-all-done.1 = f32[4,1,72,128]{3,2,1,0:T(8,128)S(1)} async-done(((f32[4,1,72,128]{3,2,1,0:T(8,128)}), f32[4,1,72,128]{3,2,1,0:T(8,128)S(1)}, u32[]{:S(2)}, u32[]{:S(2)}) %all-to-all-start.1) | async-done | bytes 147488 | tf_op jit(solution)/shard_map/all_to_all | solution.py:69
  63.0 0.9 fusion.16
  64.0 5.1 %all-to-all-start.2 = ((f32[16,1,64,128]{3,2,1,0:T(8,128)}), f32[16,1,64,128]{3,2,1,0:T(8,128)S(1)}, u32[]{:S(2)}, u32[]{:S(2)}) async-start(f32[16,1,64,128]{3,2,1,0:T(8,128)} %fusion.16), calls=%async_computation.2 | async-start | bytes 1048576 | tf_op jit(solution)/shard_map/all_to_all | solution.py:120
  69.2 2.9 %copy.69 = bf16[1024,1024]{1,0:T(8,128)(2,1)S(1)} copy(bf16[1024,1024]{0,1:T(8,128)(2,1)} %bitcast.98) | data formatting | bytes 4194304 | tf_op jit(solution)/shard_map/dot_general | solution.py:154
  72.1 0.8 fusion.44
  73.0 2.2 %convolution_bitcast_fusion.2 = f32[64,1,16,64]{3,0,2,1:T(8,128)} fusion(bf16[64,16,64]{0,2,1:T(8,128)(2,1)S(1)} %bitcast.101, f32[16,64]{1,0:T(8,128)} %get-tuple-element.5, f32[16,64]{1,0:T(8,128)} %bitcast.106, f32[64,64]{1,0:T(8,128)S(1)} %fusion.44, pred[64,64]{1,0:T(8,128)(4,1)S(1)} %iota_compare_fusion.1), kind=kOutput, calls=%fused_computation.13 | convolution fusion | flops 50593792 | bytes 421888 | tf_op jit(solution)/shard_map/gkts,sgkp->tgkp/dot_general | solution.py:29
  75.9 4.5 %all-to-all-done.2 = f32[16,1,64,128]{3,2,1,0:T(8,128)S(1)} async-done(((f32[16,1,64,128]{3,2,1,0:T(8,128)}), f32[16,1,64,128]{3,2,1,0:T(8,128)S(1)}, u32[]{:S(2)}, u32[]{:S(2)}) %all-to-all-start.2) | async-done | bytes 524320 | tf_op jit(solution)/shard_map/all_to_all | solution.py:120
  80.5 2.0 %fusion.9 = f32[64,1,16,64]{3,0,2,1:T(8,128)S(1)} fusion(f32[64,1,16,64]{3,0,2,1:T(8,128)} %convolution_bitcast_fusion.2, f32[16,1,64,128]{3,2,1,0:T(8,128)S(1)} %all-to-all-done.2, f32[64,1,16,64]{3,2,0,1:T(8,128)S(1)} %reshape.459, f32[16]{0:T(128)} %param.17, f32[64,16]{0,1:T(8,128)S(1)} %exponential_bitcast_fusion, bf16[64,128]{1,0:T(8,128)(2,1)} %param.14), kind=kOutput, calls=%fused_computation.16 | convolution fusion | flops 100925440 | bytes 1331264 | tf_op jit(solution)/shard_map/tgn,gkpn->tgkp/dot_general | solution.py:36
  83.3 0.8 convolution_bitcast_fusion.3
  84.1 11.8 %all_to_all.30 = f32[8,64,128]{2,1,0:T(8,128)S(1)} all-to-all(f32[8,64,128]{2,1,0:T(8,128)S(1)} %convolution_bitcast_fusion.3), channel_id=1, replica_groups=mesh['zh'=4,'zl'=4,'sx'=4,'tp'=8] {'tp'}, dimensions={0} | all-to-all | bytes 524288 | tf_op jit(solution)/shard_map/all_to_all | solution.py:158
  96.7 33.8 %all_to_all.31 = bf16[16,2,1,64,128]{4,3,1,2,0:T(8,128)(2,1)S(1)} all-to-all(bf16[16,2,1,64,128]{4,3,1,2,0:T(8,128)(2,1)S(1)} %broadcast_in_dim.140), channel_id=1, replica_groups=mesh['zh'=4,'zl'=4,'sx'=4,'tp'=8] {'zh','zl'}, dimensions={0} | all-to-all | bytes 1048576 | tf_op jit(solution)/shard_map/all_to_all | solution.py:69
  130.5 1.9 %broadcast_in_dim.142 = bf16[4,16,2,1,64,128]{5,4,1,3,2,0:T(8,128)(2,1)} broadcast(bf16[16,2,64,128]{3,2,0,1:T(8,128)(2,1)S(1)} %copy.64), dimensions={1,2,4,5} | broadcast | bytes 2621440 | tf_op jit(solution)/shard_map/broadcast_in_dim | solution.py:68
  132.4 3.6 %all-to-all-start.5 = ((bf16[4,16,2,1,64,128]{5,4,1,3,2,0:T(8,128)(2,1)}), bf16[4,16,2,1,64,128]{5,4,1,3,2,0:T(8,128)(2,1)S(1)}, u32[]{:S(2)}, u32[]{:S(2)}) async-start(bf16[4,16,2,1,64,128]{5,4,1,3,2,0:T(8,128)(2,1)} %broadcast_in_dim.142), calls=%async_computation.5 | async-start | bytes 4194304 | tf_op jit(solution)/shard_map/all_to_all | solution.py:69
  136.2 22.4 %all-to-all-done.5 = bf16[4,16,2,1,64,128]{5,4,1,3,2,0:T(8,128)(2,1)S(1)} async-done(((bf16[4,16,2,1,64,128]{5,4,1,3,2,0:T(8,128)(2,1)}), bf16[4,16,2,1,64,128]{5,4,1,3,2,0:T(8,128)(2,1)S(1)}, u32[]{:S(2)}, u32[]{:S(2)}) %all-to-all-start.5) | async-done | bytes 2097184 | tf_op jit(solution)/shard_map/all_to_all | solution.py:69
  159.1 0.9 fusion.43
  160.6 0.9 fusion.13
  (59 shorter events, 9.3 us)
Async XLA Ops:
  0.6 4.7 %copy-start = (bf16[64,128]{1,0:T(8,128)(2,1)S(1)}, bf16[64,128]{1,0:T(8,128)(2,1)}, u32[]{:S(2)}) copy-start(bf16[64,128]{1,0:T(8,128)(2,1)} %param.13) | copy-start | bytes 49156
  2.3 0.6 copy-start.4
  5.3 63.8 %copy-start.1 = (bf16[64,1024]{1,0:T(8,128)(2,1)S(1)}, bf16[64,1024]{1,0:T(8,128)(2,1)}, u32[]{:S(2)}) copy-start(bf16[64,1024]{1,0:T(8,128)(2,1)} %param.11) | copy-start | bytes 393220
  6.7 24.6 %all-to-all-start = ((f32[16,1,72,128]{3,2,1,0:T(8,128)}), f32[16,1,72,128]{3,2,1,0:T(8,128)S(1)}, u32[]{:S(2)}, u32[]{:S(2)}) async-start(f32[16,1,72,128]{3,2,1,0:T(8,128)} %maximum_bitcast_fusion), calls=%async_computation | async-start | bytes 1179648 | tf_op jit(solution)/shard_map/all_to_all | solution.py:101
  35.2 27.5 %all-to-all-start.1 = ((f32[4,1,72,128]{3,2,1,0:T(8,128)}), f32[4,1,72,128]{3,2,1,0:T(8,128)S(1)}, u32[]{:S(2)}, u32[]{:S(2)}) async-start(f32[4,1,72,128]{3,2,1,0:T(8,128)} %broadcast_in_dim.134), calls=%async_computation.1 | async-start | bytes 294912 | tf_op jit(solution)/shard_map/all_to_all | solution.py:69
  64.0 16.5 %all-to-all-start.2 = ((f32[16,1,64,128]{3,2,1,0:T(8,128)}), f32[16,1,64,128]{3,2,1,0:T(8,128)S(1)}, u32[]{:S(2)}, u32[]{:S(2)}) async-start(f32[16,1,64,128]{3,2,1,0:T(8,128)} %fusion.16), calls=%async_computation.2 | async-start | bytes 1048576 | tf_op jit(solution)/shard_map/all_to_all | solution.py:120
  69.2 13.8 %copy-start.3 = (bf16[64,1024]{1,0:T(8,128)(2,1)S(1)}, bf16[64,1024]{1,0:T(8,128)(2,1)}, u32[]{:S(2)}) copy-start(bf16[64,1024]{1,0:T(8,128)(2,1)} %param.12) | copy-start | bytes 393220
  75.2 8.0 %copy-start.6 = (f32[1024]{0:T(1024)S(1)}, f32[1024]{0:T(1024)}, u32[]{:S(2)}) copy-start(f32[1024]{0:T(1024)} %param.18) | copy-start | bytes 12292
  83.3 49.1 %copy-start.2 = (bf16[64,1024]{1,0:T(8,128)(2,1)}, bf16[64,1024]{1,0:T(8,128)(2,1)S(1)}, u32[]{:S(2)}) copy-start(bf16[64,1024]{1,0:T(8,128)(2,1)S(1)} %multiply_convert_fusion) | copy-start | bytes 393220
  130.5 5.7 %copy-start.5 = (bf16[64,512]{1,0:T(8,128)(2,1)S(1)}, bf16[64,512]{1,0:T(8,128)(2,1)}, u32[]{:S(2)}) copy-start(bf16[64,512]{1,0:T(8,128)(2,1)} %param.20) | copy-start | bytes 196612
  132.4 26.2 %all-to-all-start.5 = ((bf16[4,16,2,1,64,128]{5,4,1,3,2,0:T(8,128)(2,1)}), bf16[4,16,2,1,64,128]{5,4,1,3,2,0:T(8,128)(2,1)S(1)}, u32[]{:S(2)}, u32[]{:S(2)}) async-start(bf16[4,16,2,1,64,128]{5,4,1,3,2,0:T(8,128)(2,1)} %broadcast_in_dim.142), calls=%async_computation.5 | async-start | bytes 4194304 | tf_op jit(solution)/shard_map/all_to_all | solution.py:69

commit v10 on v9

--- a/solution.py
+++ b/solution.py
@@ -67,6 +67,17 @@
     count = lax.axis_size(axis)
     repeated = jnp.broadcast_to(block[None], (count,) + block.shape)
     return lax.all_to_all(repeated, axis, 0, 0, tiled=True)
+
+
+def gather_around(block, axis):
+    count = lax.axis_size(axis)
+    here = lax.axis_index(axis)
+    shifted = [block]
+    for shift in range(1, count):
+        pairs = [(source, (source + shift) % count) for source in range(count)]
+        shifted.append(lax.ppermute(block, axis, pairs))
+    stacked = jnp.stack(shifted)
+    return stacked[(here - jnp.arange(count)) % count]
 
 
 def masked_weights(decays, upto):
@@ -160,7 +171,7 @@
     values = jnp.transpose(values.reshape(tokens_here, kv_here, HEAD_DIM), (1, 0, 2))
     key_heads = jnp.transpose(keys.reshape(tokens_here, kv_here, HEAD_DIM), (1, 0, 2))
     pair = jnp.stack([key_heads, values])
-    pair = gather_by_exchange(gather_by_exchange(pair, ("zh", "zl")), "sx")
+    pair = gather_around(gather_by_exchange(pair, ("zh", "zl")), "sx")
     all_pairs = jnp.transpose(pair, (2, 3, 1, 0, 4, 5)).reshape(2, kv_here, -1, HEAD_DIM)
     key_portion = all_pairs[0]
     value_portion = all_pairs[1]

time: 163 us -> 166 us (1.018)
  starting transfers between devices: 30 us -> 35.2 us
  waiting for transfers between devices: 57.8 us -> 55.6 us
    all_to_all x2 -> x1, waiting for transfers between devices: 37.6 us -> 15.1 us  [gather_by_exchange(): return lax.all_to_all(repeated, axis, 0, 0, tiled=True)]
    ppermute x0 -> x3, waiting for transfers between devices: none -> 18 us  [gather_around(): shifted.append(lax.ppermute(block, axis, pairs))]
    ppermute x0 -> x3, starting transfers between devices: none -> 8.85 us  [gather_around(): shifted.append(lax.ppermute(block, axis, pairs))]
    all_to_all x2 -> x1, starting transfers between devices: 16 us -> 12.4 us  [gather_by_exchange(): return lax.all_to_all(repeated, axis, 0, 0, tiled=True)]
    all_to_all x1, waiting for transfers between devices: 4.52 us -> 6.73 us  [entering_state(): returned = lax.all_to_all(outgoing, axis, 0, 0, tiled=True)]
    gather x0 -> x1, local copies, waits for them, and re-layouts: none -> 2.17 us  [gather_around(): return stacked[(here - jnp.arange(count)) % count]]
    broadcast_in_dim x5 -> x3, local copies, waits for them, and re-layouts: 3.37 us -> 1.42 us  [gather_by_exchange(): repeated = jnp.broadcast_to(block[None], (count,) + block.shape)]
  transfers between devices with their start and end apart: 4 -> 6, of which waited for: 4 -> 6; matrix products, arithmetic and copies ran while one was open for 4% -> 3% of each run, Pallas kernels for 0% -> 0%
where the time goes in v10:
time: 166 us; the launch traced here: 165 us
  waiting for transfers between devices  55.6 us (33%)
  blocking collectives  45.6 us (27%)
  starting transfers between devices  35.2 us (21%)
  local copies, waits for them, and re-layouts  13.7 us (8%)
  other arithmetic  7.72 us (5%)
  matrix products  6.59 us (4%)
    all_to_all x1, blocking collectives, gather_by_exchange(): return lax.all_to_all(repeated, axis, 0, 0, tiled=True)  33.8 us
    ppermute x3, waiting for transfers between devices, gather_around(): shifted.append(lax.ppermute(block, axis, pairs))  18 us
    all_to_all x1, waiting for transfers between devices, entering_state(): received = lax.all_to_all(packed, axis, 0, 0, tiled=True)  15.7 us
    all_to_all x1, waiting for transfers between devices, gather_by_exchange(): return lax.all_to_all(repeated, axis, 0, 0, tiled=True)  15.1 us
    all_to_all x1, starting transfers between devices, gather_by_exchange(): return lax.all_to_all(repeated, axis, 0, 0, tiled=True)  12.4 us
    all_to_all x1, blocking collectives, per_device(): exchanged = lax.all_to_all(partials, 'tp', 0, 0, tiled=True)  11.8 us
    all_to_all x1, starting transfers between devices, entering_state(): received = lax.all_to_all(packed, axis, 0, 0, tiled=True)  8.87 us
    ppermute x3, starting transfers between devices, gather_around(): shifted.append(lax.ppermute(block, axis, pairs))  8.85 us
  transfers between devices with their start and end apart: 6, of which 6 were waited for; matrix products, arithmetic and copies ran while one was open for 3% of the time, Pallas kernels for 0%

profile of v10, /device:TPU:32, one launch (start us, length us, event | category | flops | bytes accessed | tf_op | source)
XLA Modules:
  0.0 165.4 jit_solution(7019441083040971791)
XLA Ops:
  3.3 1.1 copy.88
  5.7 8.9 %all-to-all-start = ((f32[16,1,72,128]{3,2,1,0:T(8,128)}), f32[16,1,72,128]{3,2,1,0:T(8,128)S(1)}, u32[]{:S(2)}, u32[]{:S(2)}) async-start(f32[16,1,72,128]{3,2,1,0:T(8,128)} %maximum_bitcast_fusion.1), calls=%async_computation | async-start | bytes 1179648 | tf_op jit(solution)/shard_map/all_to_all | solution.py:112
  14.6 15.7 %all-to-all-done = f32[16,1,72,128]{3,2,1,0:T(8,128)S(1)} async-done(((f32[16,1,72,128]{3,2,1,0:T(8,128)}), f32[16,1,72,128]{3,2,1,0:T(8,128)S(1)}, u32[]{:S(2)}, u32[]{:S(2)}) %all-to-all-start) | async-done | bytes 589856 | tf_op jit(solution)/shard_map/all_to_all | solution.py:112
  31.5 1.3 multiply_reduce_fusion
  34.1 12.4 %all-to-all-start.1 = ((f32[4,1,72,128]{3,2,1,0:T(8,128)}), f32[4,1,72,128]{3,2,1,0:T(8,128)S(1)}, u32[]{:S(2)}, u32[]{:S(2)}) async-start(f32[4,1,72,128]{3,2,1,0:T(8,128)} %broadcast_in_dim.127), calls=%async_computation.1 | async-start | bytes 294912 | tf_op jit(solution)/shard_map/all_to_all | solution.py:69
  46.5 15.1 %all-to-all-done.1 = f32[4,1,72,128]{3,2,1,0:T(8,128)S(1)} async-done(((f32[4,1,72,128]{3,2,1,0:T(8,128)}), f32[4,1,72,128]{3,2,1,0:T(8,128)S(1)}, u32[]{:S(2)}, u32[]{:S(2)}) %all-to-all-start.1) | async-done | bytes 147488 | tf_op jit(solution)/shard_map/all_to_all | solution.py:69
  62.0 0.9 fusion.16
  62.9 5.1 %all-to-all-start.2 = ((f32[16,1,64,128]{3,2,1,0:T(8,128)}), f32[16,1,64,128]{3,2,1,0:T(8,128)S(1)}, u32[]{:S(2)}, u32[]{:S(2)}) async-start(f32[16,1,64,128]{3,2,1,0:T(8,128)} %fusion.16), calls=%async_computation.2 | async-start | bytes 1048576 | tf_op jit(solution)/shard_map/all_to_all | solution.py:131
  68.2 2.9 %copy.87 = bf16[1024,1024]{1,0:T(8,128)(2,1)S(1)} copy(bf16[1024,1024]{0,1:T(8,128)(2,1)} %bitcast.108) | data formatting | bytes 4194304 | tf_op jit(solution)/shard_map/dot_general | solution.py:165
  71.2 1.5 convolution_bitcast_fusion.2
  72.7 6.7 %all-to-all-done.2 = f32[16,1,64,128]{3,2,1,0:T(8,128)S(1)} async-done(((f32[16,1,64,128]{3,2,1,0:T(8,128)}), f32[16,1,64,128]{3,2,1,0:T(8,128)S(1)}, u32[]{:S(2)}, u32[]{:S(2)}) %all-to-all-start.2) | async-done | bytes 524320 | tf_op jit(solution)/shard_map/all_to_all | solution.py:131
  79.4 2.0 %fusion.9 = f32[64,1,16,64]{3,0,2,1:T(8,128)S(1)} fusion(f32[64,1,16,64]{3,0,2,1:T(8,128)} %convolution_bitcast_fusion.2, f32[16,1,64,128]{3,2,1,0:T(8,128)S(1)} %all-to-all-done.2, f32[64,1,16,64]{3,2,0,1:T(8,128)S(1)} %reshape.505, f32[16]{0:T(128)S(1)} %copy-done.10, f32[64,16]{0,1:T(8,128)S(1)} %exponential_bitcast_fusion, bf16[64,128]{1,0:T(8,128)(2,1)S(1)} %copy-done.6), kind=kOutput, calls=%fused_computation.17 | convolution fusion | flops 100925440 | bytes 1331264 | tf_op jit(solution)/shard_map/tgn,gkpn->tgkp/dot_general | solution.py:36
  83.0 11.8 %all_to_all.25 = f32[8,64,128]{2,1,0:T(8,128)S(1)} all-to-all(f32[8,64,128]{2,1,0:T(8,128)S(1)} %convolution_bitcast_fusion.3), channel_id=1, replica_groups=mesh['zh'=4,'zl'=4,'sx'=4,'tp'=8] {'tp'}, dimensions={0} | all-to-all | bytes 524288 | tf_op jit(solution)/shard_map/all_to_all | solution.py:169
  95.0 33.8 %all_to_all.26 = bf16[16,2,1,64,128]{4,3,1,2,0:T(8,128)(2,1)S(1)} all-to-all(bf16[16,2,1,64,128]{4,3,1,2,0:T(8,128)(2,1)S(1)} %broadcast_in_dim.133), channel_id=1, replica_groups=mesh['zh'=4,'zl'=4,'sx'=4,'tp'=8] {'zh','zl'}, dimensions={0} | all-to-all | bytes 1048576 | tf_op jit(solution)/shard_map/all_to_all | solution.py:69
  128.8 3.0 %collective-permute-start.2 = (bf16[16,2,1,64,128]{4,3,1,0,2:T(8,128)(2,1)S(1)}, bf16[16,2,1,64,128]{4,3,1,0,2:T(8,128)(2,1)S(1)}, u32[]{:S(2)}, u32[]{:S(2)}) collective-permute-start(bf16[16,2,1,64,128]{4,3,1,0,2:T(8,128)(2,1)S(1)} %bitcast.109), channel_id=1, source_target_pairs={{0,24},{8,0},{16,8},{24,16},{1,25},{9,1},{17,9},{25,17},{2,26},{10... | collective-permute-start | bytes 1572872 | tf_op jit(solution)/shard_map/ppermute | solution.py:78
  131.8 3.4 %collective-permute-start.1 = (bf16[16,2,1,64,128]{4,3,1,0,2:T(8,128)(2,1)S(1)}, bf16[16,2,1,64,128]{4,3,1,0,2:T(8,128)(2,1)S(1)}, u32[]{:S(2)}, u32[]{:S(2)}) collective-permute-start(bf16[16,2,1,64,128]{4,3,1,0,2:T(8,128)(2,1)S(1)} %bitcast.110), channel_id=1, source_target_pairs={{0,16},{8,24},{16,0},{24,8},{1,17},{9,25},{17,1},{25,9},{2,18},{10... | collective-permute-start | bytes 1572872 | tf_op jit(solution)/shard_map/ppermute | solution.py:78
  135.2 2.4 %collective-permute-start = (bf16[16,2,1,64,128]{4,3,1,0,2:T(8,128)(2,1)S(1)}, bf16[16,2,1,64,128]{4,3,1,0,2:T(8,128)(2,1)S(1)}, u32[]{:S(2)}, u32[]{:S(2)}) collective-permute-start(bf16[16,2,1,64,128]{4,3,1,0,2:T(8,128)(2,1)S(1)} %bitcast.111), channel_id=1, source_target_pairs={{0,8},{8,16},{16,24},{24,0},{1,9},{9,17},{17,25},{25,1},{2,10},{10... | collective-permute-start | bytes 1572872 | tf_op jit(solution)/shard_map/ppermute | solution.py:78
  137.8 7.7 %collective-permute-done.2 = bf16[16,2,1,64,128]{4,3,1,0,2:T(8,128)(2,1)S(1)} collective-permute-done((bf16[16,2,1,64,128]{4,3,1,0,2:T(8,128)(2,1)S(1)}, bf16[16,2,1,64,128]{4,3,1,0,2:T(8,128)(2,1)S(1)}, u32[]{:S(2)}, u32[]{:S(2)}) %collective-permute-start.2) | collective-permute-done | bytes 524320 | tf_op jit(solution)/shard_map/ppermute | solution.py:78
  145.5 4.5 %collective-permute-done.1 = bf16[16,2,1,64,128]{4,3,1,0,2:T(8,128)(2,1)S(1)} collective-permute-done((bf16[16,2,1,64,128]{4,3,1,0,2:T(8,128)(2,1)S(1)}, bf16[16,2,1,64,128]{4,3,1,0,2:T(8,128)(2,1)S(1)}, u32[]{:S(2)}, u32[]{:S(2)}) %collective-permute-start.1) | collective-permute-done | bytes 524320 | tf_op jit(solution)/shard_map/ppermute | solution.py:78
  150.1 5.8 %collective-permute-done = bf16[16,2,1,64,128]{4,3,1,0,2:T(8,128)(2,1)S(1)} collective-permute-done((bf16[16,2,1,64,128]{4,3,1,0,2:T(8,128)(2,1)S(1)}, bf16[16,2,1,64,128]{4,3,1,0,2:T(8,128)(2,1)S(1)}, u32[]{:S(2)}, u32[]{:S(2)}) %collective-permute-start) | collective-permute-done | bytes 524320 | tf_op jit(solution)/shard_map/ppermute | solution.py:78
  156.6 1.5 maximum_bitcast_fusion
  158.1 2.2 %gather_fusion = bf16[4,16,2,64,128]{4,3,2,1,0:T(8,128)(2,1)} fusion(bf16[4,16,2,64,128]{4,3,2,1,0:T(8,128)(2,1)S(1)} %maximum_bitcast_fusion, s32[1024]{0:T(1024)S(1)} %pad_clamp_fusion), kind=kCustom, calls=%fused_computation | custom fusion | bytes 4194320 | tf_op jit(solution)/shard_map/gather | solution.py:80
  160.3 1.7 %fusion.44 = (bf16[1,1,16,4,64,128]{5,4,0,2,3,1:T(8,128)(2,1)S(1)}, bf16[1,1,16,4,64,128]{5,4,0,2,3,1:T(8,128)(2,1)S(1)}) fusion(bf16[2,1,16,4,64,128]{5,4,0,2,3,1:T(8,128)(2,1)} %bitcast.106), kind=kLoop, calls=%fused_computation.87 | loop fusion | bytes 4194304 | tf_op jit(solution)/shard_map/slice | solution.py:176
  162.2 0.9 fusion.45
  (74 shorter events, 12.1 us)
Async XLA Ops:
  0.6 3.7 %copy-start = (bf16[64,128]{1,0:T(8,128)(2,1)S(1)}, bf16[64,128]{1,0:T(8,128)(2,1)}, u32[]{:S(2)}) copy-start(bf16[64,128]{1,0:T(8,128)(2,1)} %param.13) | copy-start | bytes 49156
  5.7 24.6 %all-to-all-start = ((f32[16,1,72,128]{3,2,1,0:T(8,128)}), f32[16,1,72,128]{3,2,1,0:T(8,128)S(1)}, u32[]{:S(2)}, u32[]{:S(2)}) async-start(f32[16,1,72,128]{3,2,1,0:T(8,128)} %maximum_bitcast_fusion.1), calls=%async_computation | async-start | bytes 1179648 | tf_op jit(solution)/shard_map/all_to_all | solution.py:112
  31.5 36.5 %copy-start.1 = (bf16[64,1024]{1,0:T(8,128)(2,1)S(1)}, bf16[64,1024]{1,0:T(8,128)(2,1)}, u32[]{:S(2)}) copy-start(bf16[64,1024]{1,0:T(8,128)(2,1)} %param.11) | copy-start | bytes 393220
  34.1 27.5 %all-to-all-start.1 = ((f32[4,1,72,128]{3,2,1,0:T(8,128)}), f32[4,1,72,128]{3,2,1,0:T(8,128)S(1)}, u32[]{:S(2)}, u32[]{:S(2)}) async-start(f32[4,1,72,128]{3,2,1,0:T(8,128)} %broadcast_in_dim.127), calls=%async_computation.1 | async-start | bytes 294912 | tf_op jit(solution)/shard_map/all_to_all | solution.py:69
  62.9 16.5 %all-to-all-start.2 = ((f32[16,1,64,128]{3,2,1,0:T(8,128)}), f32[16,1,64,128]{3,2,1,0:T(8,128)S(1)}, u32[]{:S(2)}, u32[]{:S(2)}) async-start(f32[16,1,64,128]{3,2,1,0:T(8,128)} %fusion.16), calls=%async_computation.2 | async-start | bytes 1048576 | tf_op jit(solution)/shard_map/all_to_all | solution.py:131
  68.1 2.9 %copy-start.6 = (bf16[64,128]{1,0:T(8,128)(2,1)S(1)}, bf16[64,128]{1,0:T(8,128)(2,1)}, u32[]{:S(2)}) copy-start(bf16[64,128]{1,0:T(8,128)(2,1)} %param.14) | copy-start | bytes 49156
  68.2 11.3 %copy-start.10 = (f32[16]{0:T(128)S(1)}, f32[16]{0:T(128)}, u32[]{:S(2)}) copy-start(f32[16]{0:T(128)} %param.17) | copy-start | bytes 196
  72.7 9.2 %copy-start.3 = (bf16[64,1024]{1,0:T(8,128)(2,1)S(1)}, bf16[64,1024]{1,0:T(8,128)(2,1)}, u32[]{:S(2)}) copy-start(bf16[64,1024]{1,0:T(8,128)(2,1)} %param.12) | copy-start | bytes 393220
  72.7 9.4 %copy-start.9 = (f32[1024]{0:T(1024)S(1)}, f32[1024]{0:T(1024)}, u32[]{:S(2)}) copy-start(f32[1024]{0:T(1024)} %param.18) | copy-start | bytes 12292
  81.9 12.9 %copy-start.8 = (bf16[64,128]{1,0:T(8,128)(2,1)S(1)}, bf16[64,128]{1,0:T(8,128)(2,1)}, u32[]{:S(2)}) copy-start(bf16[64,128]{1,0:T(8,128)(2,1)} %param.21) | copy-start | bytes 49156
  82.2 46.5 %copy-start.2 = (bf16[64,1024]{1,0:T(8,128)(2,1)}, bf16[64,1024]{1,0:T(8,128)(2,1)S(1)}, u32[]{:S(2)}) copy-start(bf16[64,1024]{1,0:T(8,128)(2,1)S(1)} %multiply_convert_fusion) | copy-start | bytes 393220
  82.3 55.5 %copy-start.7 = (bf16[64,512]{1,0:T(8,128)(2,1)S(1)}, bf16[64,512]{1,0:T(8,128)(2,1)}, u32[]{:S(2)}) copy-start(bf16[64,512]{1,0:T(8,128)(2,1)} %param.20) | copy-start | bytes 196612
  128.8 16.7 %collective-permute-start.2 = (bf16[16,2,1,64,128]{4,3,1,0,2:T(8,128)(2,1)S(1)}, bf16[16,2,1,64,128]{4,3,1,0,2:T(8,128)(2,1)S(1)}, u32[]{:S(2)}, u32[]{:S(2)}) collective-permute-start(bf16[16,2,1,64,128]{4,3,1,0,2:T(8,128)(2,1)S(1)} %bitcast.109), channel_id=1, source_target_pairs={{0,24},{8,0},{16,8},{24,16},{1,25},{9,1},{17,9},{25,17},{2,26},{10... | collective-permute-start | bytes 1572872 | tf_op jit(solution)/shard_map/ppermute | solution.py:78
  131.8 18.3 %collective-permute-start.1 = (bf16[16,2,1,64,128]{4,3,1,0,2:T(8,128)(2,1)S(1)}, bf16[16,2,1,64,128]{4,3,1,0,2:T(8,128)(2,1)S(1)}, u32[]{:S(2)}, u32[]{:S(2)}) collective-permute-start(bf16[16,2,1,64,128]{4,3,1,0,2:T(8,128)(2,1)S(1)} %bitcast.110), channel_id=1, source_target_pairs={{0,16},{8,24},{16,0},{24,8},{1,17},{9,25},{17,1},{25,9},{2,18},{10... | collective-permute-start | bytes 1572872 | tf_op jit(solution)/shard_map/ppermute | solution.py:78
  135.2 20.6 %collective-permute-start = (bf16[16,2,1,64,128]{4,3,1,0,2:T(8,128)(2,1)S(1)}, bf16[16,2,1,64,128]{4,3,1,0,2:T(8,128)(2,1)S(1)}, u32[]{:S(2)}, u32[]{:S(2)}) collective-permute-start(bf16[16,2,1,64,128]{4,3,1,0,2:T(8,128)(2,1)S(1)} %bitcast.111), channel_id=1, source_target_pairs={{0,8},{8,16},{16,24},{24,0},{1,9},{9,17},{17,25},{25,1},{2,10},{10... | collective-permute-start | bytes 1572872 | tf_op jit(solution)/shard_map/ppermute | solution.py:78
  150.1 5.8 %copy-start.4 = (bf16[16,2,1,64,128]{4,3,1,0,2:T(8,128)(2,1)}, bf16[16,2,1,64,128]{4,3,1,0,2:T(8,128)(2,1)S(1)}, u32[]{:S(2)}) copy-start(bf16[16,2,1,64,128]{4,3,1,0,2:T(8,128)(2,1)S(1)} %collective-permute-done.1) | copy-start | bytes 1572868
  155.8 0.8 copy-start.5

commit v11 on v9

--- a/solution.py
+++ b/solution.py
@@ -160,7 +160,7 @@
     values = jnp.transpose(values.reshape(tokens_here, kv_here, HEAD_DIM), (1, 0, 2))
     key_heads = jnp.transpose(keys.reshape(tokens_here, kv_here, HEAD_DIM), (1, 0, 2))
     pair = jnp.stack([key_heads, values])
-    pair = gather_by_exchange(gather_by_exchange(pair, ("zh", "zl")), "sx")
+    pair = gather_by_exchange(lax.all_gather(pair, ("zh", "zl")), "sx")
     all_pairs = jnp.transpose(pair, (2, 3, 1, 0, 4, 5)).reshape(2, kv_here, -1, HEAD_DIM)
     key_portion = all_pairs[0]
     value_portion = all_pairs[1]

time: 163 us -> 158 us (0.969)
  blocking collectives: 45.6 us -> 41.7 us
  waiting for transfers between devices: 57.8 us -> 55.4 us
    all_to_all x1 -> x0, blocking collectives: 33.8 us -> none  [gather_by_exchange(): return lax.all_to_all(repeated, axis, 0, 0, tiled=True)]
    all_gather x0 -> x1, blocking collectives: none -> 29.9 us  [per_device(): pair = gather_by_exchange(lax.all_gather(pair, ('zh', 'zl')), 'sx')]
    all_to_all x2, waiting for transfers between devices: 37.6 us -> 35.1 us  [gather_by_exchange(): return lax.all_to_all(repeated, axis, 0, 0, tiled=True)]
    broadcast_in_dim x5 -> x4, local copies, waits for them, and re-layouts: 3.37 us -> 3.27 us  [gather_by_exchange(): repeated = jnp.broadcast_to(block[None], (count,) + block.shape)]
where the time goes in v11:
time: 158 us; the launch traced here: 156 us
  waiting for transfers between devices  55.4 us (35%)
  blocking collectives  41.7 us (26%)
  starting transfers between devices  30 us (19%)
  local copies, waits for them, and re-layouts  12.3 us (8%)
  other arithmetic  8.19 us (5%)
  matrix products  8.09 us (5%)
    all_to_all x2, waiting for transfers between devices, gather_by_exchange(): return lax.all_to_all(repeated, axis, 0, 0, tiled=True)  35.1 us
    all_gather x1, blocking collectives, per_device(): pair = gather_by_exchange(lax.all_gather(pair, ('zh', 'zl')), 'sx')  29.9 us
    all_to_all x2, starting transfers between devices, gather_by_exchange(): return lax.all_to_all(repeated, axis, 0, 0, tiled=True)  16 us
    all_to_all x1, waiting for transfers between devices, entering_state(): received = lax.all_to_all(packed, axis, 0, 0, tiled=True)  15.7 us
    all_to_all x1, blocking collectives, per_device(): exchanged = lax.all_to_all(partials, 'tp', 0, 0, tiled=True)  11.8 us
    all_to_all x1, starting transfers between devices, entering_state(): received = lax.all_to_all(packed, axis, 0, 0, tiled=True)  8.87 us
    all_to_all x1, starting transfers between devices, entering_state(): returned = lax.all_to_all(outgoing, axis, 0, 0, tiled=True)  5.09 us
    all_to_all x1, waiting for transfers between devices, entering_state(): returned = lax.all_to_all(outgoing, axis, 0, 0, tiled=True)  4.54 us
  transfers between devices with their start and end apart: 4, of which 4 were waited for; matrix products, arithmetic and copies ran while one was open for 4% of the time, Pallas kernels for 0%

profile of v11, /device:TPU:32, one launch (start us, length us, event | category | flops | bytes accessed | tf_op | source)
XLA Modules:
  0.0 156.5 jit_solution(5472760557059159958)
XLA Ops:
  1.3 0.8 multiply_bitcast_fusion.1
  2.9 1.3 multiply_bitcast_fusion
  4.2 1.1 copy.72
  5.8 0.9 maximum_bitcast_fusion
  6.7 8.9 %all-to-all-start = ((f32[16,1,72,128]{3,2,1,0:T(8,128)}), f32[16,1,72,128]{3,2,1,0:T(8,128)S(1)}, u32[]{:S(2)}, u32[]{:S(2)}) async-start(f32[16,1,72,128]{3,2,1,0:T(8,128)} %maximum_bitcast_fusion), calls=%async_computation | async-start | bytes 1179648 | tf_op jit(solution)/shard_map/all_to_all | solution.py:101
  15.6 15.7 %all-to-all-done = f32[16,1,72,128]{3,2,1,0:T(8,128)S(1)} async-done(((f32[16,1,72,128]{3,2,1,0:T(8,128)}), f32[16,1,72,128]{3,2,1,0:T(8,128)S(1)}, u32[]{:S(2)}, u32[]{:S(2)}) %all-to-all-start) | async-done | bytes 589856 | tf_op jit(solution)/shard_map/all_to_all | solution.py:101
  32.5 1.3 multiply_reduce_fusion
  35.2 12.4 %all-to-all-start.1 = ((f32[4,1,72,128]{3,2,1,0:T(8,128)}), f32[4,1,72,128]{3,2,1,0:T(8,128)S(1)}, u32[]{:S(2)}, u32[]{:S(2)}) async-start(f32[4,1,72,128]{3,2,1,0:T(8,128)} %broadcast_in_dim.126), calls=%async_computation.1 | async-start | bytes 294912 | tf_op jit(solution)/shard_map/all_to_all | solution.py:69
  47.6 15.1 %all-to-all-done.1 = f32[4,1,72,128]{3,2,1,0:T(8,128)S(1)} async-done(((f32[4,1,72,128]{3,2,1,0:T(8,128)}), f32[4,1,72,128]{3,2,1,0:T(8,128)S(1)}, u32[]{:S(2)}, u32[]{:S(2)}) %all-to-all-start.1) | async-done | bytes 147488 | tf_op jit(solution)/shard_map/all_to_all | solution.py:69
  63.0 0.9 fusion.16
  64.0 5.1 %all-to-all-start.2 = ((f32[16,1,64,128]{3,2,1,0:T(8,128)}), f32[16,1,64,128]{3,2,1,0:T(8,128)S(1)}, u32[]{:S(2)}, u32[]{:S(2)}) async-start(f32[16,1,64,128]{3,2,1,0:T(8,128)} %fusion.16), calls=%async_computation.2 | async-start | bytes 1048576 | tf_op jit(solution)/shard_map/all_to_all | solution.py:120
  69.2 2.9 %copy.71 = bf16[1024,1024]{1,0:T(8,128)(2,1)S(1)} copy(bf16[1024,1024]{0,1:T(8,128)(2,1)} %bitcast.96) | data formatting | bytes 4194304 | tf_op jit(solution)/shard_map/dot_general | solution.py:154
  72.1 0.8 fusion.44
  73.0 2.2 %convolution_bitcast_fusion.2 = f32[64,1,16,64]{3,0,2,1:T(8,128)} fusion(bf16[64,16,64]{0,2,1:T(8,128)(2,1)S(1)} %bitcast.99, f32[16,64]{1,0:T(8,128)} %get-tuple-element.5, f32[16,64]{1,0:T(8,128)} %bitcast.104, f32[64,64]{1,0:T(8,128)S(1)} %fusion.44, pred[64,64]{1,0:T(8,128)(4,1)S(1)} %iota_compare_fusion.1), kind=kOutput, calls=%fused_computation.13 | convolution fusion | flops 50593792 | bytes 421888 | tf_op jit(solution)/shard_map/gkts,sgkp->tgkp/dot_general | solution.py:29
  75.9 4.5 %all-to-all-done.2 = f32[16,1,64,128]{3,2,1,0:T(8,128)S(1)} async-done(((f32[16,1,64,128]{3,2,1,0:T(8,128)}), f32[16,1,64,128]{3,2,1,0:T(8,128)S(1)}, u32[]{:S(2)}, u32[]{:S(2)}) %all-to-all-start.2) | async-done | bytes 524320 | tf_op jit(solution)/shard_map/all_to_all | solution.py:120
  80.5 2.0 %fusion.9 = f32[64,1,16,64]{3,0,2,1:T(8,128)S(1)} fusion(f32[64,1,16,64]{3,0,2,1:T(8,128)} %convolution_bitcast_fusion.2, f32[16,1,64,128]{3,2,1,0:T(8,128)S(1)} %all-to-all-done.2, f32[64,1,16,64]{3,2,0,1:T(8,128)S(1)} %reshape.456, f32[16]{0:T(128)} %param.17, f32[64,16]{0,1:T(8,128)S(1)} %exponential_bitcast_fusion, bf16[64,128]{1,0:T(8,128)(2,1)} %param.14), kind=kOutput, calls=%fused_computation.16 | convolution fusion | flops 100925440 | bytes 1331264 | tf_op jit(solution)/shard_map/tgn,gkpn->tgkp/dot_general | solution.py:36
  83.2 0.8 multiply_convert_fusion
  84.7 11.8 %all_to_all.25 = f32[8,64,128]{2,1,0:T(8,128)S(1)} all-to-all(f32[8,64,128]{2,1,0:T(8,128)S(1)} %convolution_bitcast_fusion.3), channel_id=1, replica_groups=mesh['zh'=4,'zl'=4,'sx'=4,'tp'=8] {'tp'}, dimensions={0} | all-to-all | bytes 524288 | tf_op jit(solution)/shard_map/all_to_all | solution.py:158
  97.3 29.9 %all-gather = bf16[32,1,64,128]{3,2,1,0:T(8,128)(2,1)S(1)} all-gather(bf16[2,1,64,128]{3,2,1,0:T(8,128)(2,1)S(1)} %pad_maximum_fusion), channel_id=2, replica_groups=mesh['zh'=4,'zl'=4,'sx'=4,'tp'=8] {'zh','zl'}, dimensions={0}, use_global_device_ids=true | all-gather | bytes 557056 | tf_op jit(solution)/shard_map/all_gather | solution.py:163
  127.2 1.9 %broadcast_in_dim.132 = bf16[4,16,2,1,64,128]{5,4,1,3,2,0:T(8,128)(2,1)} broadcast(bf16[16,2,64,128]{3,2,0,1:T(8,128)(2,1)S(1)} %copy.66), dimensions={1,2,4,5} | broadcast | bytes 2621440 | tf_op jit(solution)/shard_map/broadcast_in_dim | solution.py:68
  129.1 3.6 %all-to-all-start.4 = ((bf16[4,16,2,1,64,128]{5,4,1,3,2,0:T(8,128)(2,1)}), bf16[4,16,2,1,64,128]{5,4,1,3,2,0:T(8,128)(2,1)S(1)}, u32[]{:S(2)}, u32[]{:S(2)}) async-start(bf16[4,16,2,1,64,128]{5,4,1,3,2,0:T(8,128)(2,1)} %broadcast_in_dim.132), calls=%async_computation.4 | async-start | bytes 4194304 | tf_op jit(solution)/shard_map/all_to_all | solution.py:69
  132.9 20.0 %all-to-all-done.4 = bf16[4,16,2,1,64,128]{5,4,1,3,2,0:T(8,128)(2,1)S(1)} async-done(((bf16[4,16,2,1,64,128]{5,4,1,3,2,0:T(8,128)(2,1)}), bf16[4,16,2,1,64,128]{5,4,1,3,2,0:T(8,128)(2,1)S(1)}, u32[]{:S(2)}, u32[]{:S(2)}) %all-to-all-start.4) | async-done | bytes 2097184 | tf_op jit(solution)/shard_map/all_to_all | solution.py:69
  153.3 0.9 fusion.43
  154.9 0.9 fusion.13
  (56 shorter events, 9.8 us)
Async XLA Ops:
  0.6 4.7 %copy-start = (bf16[64,128]{1,0:T(8,128)(2,1)S(1)}, bf16[64,128]{1,0:T(8,128)(2,1)}, u32[]{:S(2)}) copy-start(bf16[64,128]{1,0:T(8,128)(2,1)} %param.13) | copy-start | bytes 49156
  2.3 0.6 copy-start.4
  5.3 63.8 %copy-start.1 = (bf16[64,1024]{1,0:T(8,128)(2,1)S(1)}, bf16[64,1024]{1,0:T(8,128)(2,1)}, u32[]{:S(2)}) copy-start(bf16[64,1024]{1,0:T(8,128)(2,1)} %param.11) | copy-start | bytes 393220
  6.7 24.6 %all-to-all-start = ((f32[16,1,72,128]{3,2,1,0:T(8,128)}), f32[16,1,72,128]{3,2,1,0:T(8,128)S(1)}, u32[]{:S(2)}, u32[]{:S(2)}) async-start(f32[16,1,72,128]{3,2,1,0:T(8,128)} %maximum_bitcast_fusion), calls=%async_computation | async-start | bytes 1179648 | tf_op jit(solution)/shard_map/all_to_all | solution.py:101
  35.2 27.5 %all-to-all-start.1 = ((f32[4,1,72,128]{3,2,1,0:T(8,128)}), f32[4,1,72,128]{3,2,1,0:T(8,128)S(1)}, u32[]{:S(2)}, u32[]{:S(2)}) async-start(f32[4,1,72,128]{3,2,1,0:T(8,128)} %broadcast_in_dim.126), calls=%async_computation.1 | async-start | bytes 294912 | tf_op jit(solution)/shard_map/all_to_all | solution.py:69
  64.0 16.5 %all-to-all-start.2 = ((f32[16,1,64,128]{3,2,1,0:T(8,128)}), f32[16,1,64,128]{3,2,1,0:T(8,128)S(1)}, u32[]{:S(2)}, u32[]{:S(2)}) async-start(f32[16,1,64,128]{3,2,1,0:T(8,128)} %fusion.16), calls=%async_computation.2 | async-start | bytes 1048576 | tf_op jit(solution)/shard_map/all_to_all | solution.py:120
  69.2 13.8 %copy-start.3 = (bf16[64,1024]{1,0:T(8,128)(2,1)S(1)}, bf16[64,1024]{1,0:T(8,128)(2,1)}, u32[]{:S(2)}) copy-start(bf16[64,1024]{1,0:T(8,128)(2,1)} %param.12) | copy-start | bytes 393220
  84.0 45.1 %copy-start.2 = (bf16[64,1024]{1,0:T(8,128)(2,1)}, bf16[64,1024]{1,0:T(8,128)(2,1)S(1)}, u32[]{:S(2)}) copy-start(bf16[64,1024]{1,0:T(8,128)(2,1)S(1)} %multiply_convert_fusion) | copy-start | bytes 393220
  97.3 35.5 %copy-start.5 = (bf16[64,512]{1,0:T(8,128)(2,1)S(1)}, bf16[64,512]{1,0:T(8,128)(2,1)}, u32[]{:S(2)}) copy-start(bf16[64,512]{1,0:T(8,128)(2,1)} %param.20) | copy-start | bytes 196612
  129.1 23.8 %all-to-all-start.4 = ((bf16[4,16,2,1,64,128]{5,4,1,3,2,0:T(8,128)(2,1)}), bf16[4,16,2,1,64,128]{5,4,1,3,2,0:T(8,128)(2,1)S(1)}, u32[]{:S(2)}, u32[]{:S(2)}) async-start(bf16[4,16,2,1,64,128]{5,4,1,3,2,0:T(8,128)(2,1)} %broadcast_in_dim.132), calls=%async_computation.4 | async-start | bytes 4194304 | tf_op jit(solution)/shard_map/all_to_all | solution.py:69

commit v12 on v11

--- a/solution.py
+++ b/solution.py
@@ -85,7 +85,7 @@
 
 def entering_top(axis, decay, state):
     rows = state.shape[-2]
-    gathered = gather_by_exchange(pack_decay(state, decay), axis)
+    gathered = lax.all_gather(pack_decay(state, decay), axis)
     weights = masked_weights(gathered[:, :, rows, 0], lax.axis_index(axis))
     return jnp.sum(weights[:, :, None, None] * gathered[:, :, :rows], axis=0)
 

time: 158 us -> 152 us (0.962)
  blocking collectives: 41.7 us -> 66.6 us
  waiting for transfers between devices: 55.4 us -> 39.6 us
  starting transfers between devices: 30 us -> 16.4 us
    all_gather x0 -> x1, blocking collectives: none -> 24.8 us  [entering_top(): gathered = lax.all_gather(pack_decay(state, decay), axis)]
    all_to_all x2 -> x1, waiting for transfers between devices: 35.1 us -> 19.6 us  [gather_by_exchange(): return lax.all_to_all(repeated, axis, 0, 0, tiled=True)]
    all_to_all x2 -> x1, starting transfers between devices: 16 us -> 3.61 us  [gather_by_exchange(): return lax.all_to_all(repeated, axis, 0, 0, tiled=True)]
    broadcast_in_dim x4 -> x2, local copies, waits for them, and re-layouts: 3.27 us -> 1.91 us  [gather_by_exchange(): repeated = jnp.broadcast_to(block[None], (count,) + block.shape)]
  transfers between devices with their start and end apart: 4 -> 3, of which waited for: 4 -> 3; matrix products, arithmetic and copies ran while one was open for 4% -> 5% of each run, Pallas kernels for 0% -> 0%
where the time goes in v12:
time: 152 us; the launch traced here: 151 us
  blocking collectives  66.6 us (44%)
  waiting for transfers between devices  39.6 us (26%)
  starting transfers between devices  16.4 us (11%)
  local copies, waits for them, and re-layouts  11.7 us (8%)
  other arithmetic  8.19 us (5%)
  matrix products  8.09 us (5%)
    all_gather x1, blocking collectives, per_device(): pair = gather_by_exchange(lax.all_gather(pair, ('zh', 'zl')), 'sx')  30 us
    all_gather x1, blocking collectives, entering_top(): gathered = lax.all_gather(pack_decay(state, decay), axis)  24.8 us
    all_to_all x1, waiting for transfers between devices, gather_by_exchange(): return lax.all_to_all(repeated, axis, 0, 0, tiled=True)  19.6 us
    all_to_all x1, waiting for transfers between devices, entering_state(): received = lax.all_to_all(packed, axis, 0, 0, tiled=True)  15.7 us
    all_to_all x1, blocking collectives, per_device(): exchanged = lax.all_to_all(partials, 'tp', 0, 0, tiled=True)  11.8 us
    all_to_all x1, starting transfers between devices, entering_state(): received = lax.all_to_all(packed, axis, 0, 0, tiled=True)  8.87 us
    all_to_all x1, waiting for transfers between devices, entering_state(): returned = lax.all_to_all(outgoing, axis, 0, 0, tiled=True)  4.34 us
    all_to_all x1, starting transfers between devices, entering_state(): returned = lax.all_to_all(outgoing, axis, 0, 0, tiled=True)  3.9 us
  transfers between devices with their start and end apart: 3, of which 3 were waited for; matrix products, arithmetic and copies ran while one was open for 5% of the time, Pallas kernels for 0%

profile of v12, /device:TPU:32, one launch (start us, length us, event | category | flops | bytes accessed | tf_op | source)
XLA Modules:
  0.0 151.5 jit_solution(5346892447808357534)
XLA Ops:
  1.3 0.8 multiply_bitcast_fusion.1
  2.9 1.3 multiply_bitcast_fusion
  4.2 1.1 copy.62
  5.9 0.9 maximum_bitcast_fusion
  6.7 8.9 %all-to-all-start = ((f32[16,1,72,128]{3,2,1,0:T(8,128)}), f32[16,1,72,128]{3,2,1,0:T(8,128)S(1)}, u32[]{:S(2)}, u32[]{:S(2)}) async-start(f32[16,1,72,128]{3,2,1,0:T(8,128)} %maximum_bitcast_fusion), calls=%async_computation | async-start | bytes 1179648 | tf_op jit(solution)/shard_map/all_to_all | solution.py:101
  15.6 15.7 %all-to-all-done = f32[16,1,72,128]{3,2,1,0:T(8,128)S(1)} async-done(((f32[16,1,72,128]{3,2,1,0:T(8,128)}), f32[16,1,72,128]{3,2,1,0:T(8,128)S(1)}, u32[]{:S(2)}, u32[]{:S(2)}) %all-to-all-start) | async-done | bytes 589856 | tf_op jit(solution)/shard_map/all_to_all | solution.py:101
  32.6 1.3 multiply_reduce_fusion
  34.6 24.8 %all-gather = f32[4,72,128]{2,1,0:T(8,128)S(1)} all-gather(f32[1,72,128]{2,1,0:T(8,128)S(1)} %concatenate.7), channel_id=2, replica_groups=mesh['zh'=4,'zl'=4,'sx'=4,'tp'=8] {'zh'}, dimensions={0}, use_global_device_ids=true | all-gather | bytes 184320 | tf_op jit(solution)/shard_map/all_gather | solution.py:88
  59.8 0.9 fusion.16
  60.7 3.9 %all-to-all-start.1 = ((f32[16,1,64,128]{3,2,1,0:T(8,128)}), f32[16,1,64,128]{3,2,1,0:T(8,128)S(1)}, u32[]{:S(2)}, u32[]{:S(2)}) async-start(f32[16,1,64,128]{3,2,1,0:T(8,128)} %fusion.16), calls=%async_computation.1 | async-start | bytes 1048576 | tf_op jit(solution)/shard_map/all_to_all | solution.py:120
  64.8 2.9 %copy.61 = bf16[1024,1024]{1,0:T(8,128)(2,1)S(1)} copy(bf16[1024,1024]{0,1:T(8,128)(2,1)} %bitcast.95) | data formatting | bytes 4194304 | tf_op jit(solution)/shard_map/dot_general | solution.py:154
  67.7 0.8 fusion.44
  68.5 2.2 %convolution_bitcast_fusion.2 = f32[64,1,16,64]{3,0,2,1:T(8,128)} fusion(bf16[64,16,64]{0,2,1:T(8,128)(2,1)S(1)} %bitcast.98, f32[16,64]{1,0:T(8,128)} %get-tuple-element.5, f32[16,64]{1,0:T(8,128)} %bitcast.105, f32[64,64]{1,0:T(8,128)S(1)} %fusion.44, pred[64,64]{1,0:T(8,128)(4,1)S(1)} %iota_compare_fusion.1), kind=kOutput, calls=%fused_computation.13 | convolution fusion | flops 50593792 | bytes 421888 | tf_op jit(solution)/shard_map/gkts,sgkp->tgkp/dot_general | solution.py:29
  71.5 4.3 %all-to-all-done.1 = f32[16,1,64,128]{3,2,1,0:T(8,128)S(1)} async-done(((f32[16,1,64,128]{3,2,1,0:T(8,128)}), f32[16,1,64,128]{3,2,1,0:T(8,128)S(1)}, u32[]{:S(2)}, u32[]{:S(2)}) %all-to-all-start.1) | async-done | bytes 524320 | tf_op jit(solution)/shard_map/all_to_all | solution.py:120
  75.8 2.0 %fusion.9 = f32[64,1,16,64]{3,0,2,1:T(8,128)S(1)} fusion(f32[64,1,16,64]{3,0,2,1:T(8,128)} %convolution_bitcast_fusion.2, f32[16,1,64,128]{3,2,1,0:T(8,128)S(1)} %all-to-all-done.1, f32[64,1,16,64]{3,2,0,1:T(8,128)S(1)} %reshape.453, f32[16]{0:T(128)} %param.17, f32[64,16]{0,1:T(8,128)S(1)} %exponential_bitcast_fusion, bf16[64,128]{1,0:T(8,128)(2,1)} %param.14), kind=kOutput, calls=%fused_computation.16 | convolution fusion | flops 100925440 | bytes 1331264 | tf_op jit(solution)/shard_map/tgn,gkpn->tgkp/dot_general | solution.py:36
  78.5 0.8 multiply_convert_fusion
  79.3 0.8 convolution_bitcast_fusion.3
  80.1 11.8 %all_to_all.20 = f32[8,64,128]{2,1,0:T(8,128)S(1)} all-to-all(f32[8,64,128]{2,1,0:T(8,128)S(1)} %convolution_bitcast_fusion.3), channel_id=1, replica_groups=mesh['zh'=4,'zl'=4,'sx'=4,'tp'=8] {'tp'}, dimensions={0} | all-to-all | bytes 524288 | tf_op jit(solution)/shard_map/all_to_all | solution.py:158
  92.6 30.0 %all-gather.1 = bf16[32,1,64,128]{3,2,1,0:T(8,128)(2,1)S(1)} all-gather(bf16[2,1,64,128]{3,2,1,0:T(8,128)(2,1)S(1)} %pad_maximum_fusion), channel_id=3, replica_groups=mesh['zh'=4,'zl'=4,'sx'=4,'tp'=8] {'zh','zl'}, dimensions={0}, use_global_device_ids=true | all-gather | bytes 557056 | tf_op jit(solution)/shard_map/all_gather | solution.py:163
  122.7 1.9 %broadcast_in_dim.122 = bf16[4,16,2,1,64,128]{5,4,1,3,2,0:T(8,128)(2,1)} broadcast(bf16[16,2,64,128]{3,2,0,1:T(8,128)(2,1)S(1)} %copy.56), dimensions={1,2,4,5} | broadcast | bytes 2621440 | tf_op jit(solution)/shard_map/broadcast_in_dim | solution.py:68
  124.5 3.6 %all-to-all-start.3 = ((bf16[4,16,2,1,64,128]{5,4,1,3,2,0:T(8,128)(2,1)}), bf16[4,16,2,1,64,128]{5,4,1,3,2,0:T(8,128)(2,1)S(1)}, u32[]{:S(2)}, u32[]{:S(2)}) async-start(bf16[4,16,2,1,64,128]{5,4,1,3,2,0:T(8,128)(2,1)} %broadcast_in_dim.122), calls=%async_computation.3 | async-start | bytes 4194304 | tf_op jit(solution)/shard_map/all_to_all | solution.py:69
  128.3 19.6 %all-to-all-done.3 = bf16[4,16,2,1,64,128]{5,4,1,3,2,0:T(8,128)(2,1)S(1)} async-done(((bf16[4,16,2,1,64,128]{5,4,1,3,2,0:T(8,128)(2,1)}), bf16[4,16,2,1,64,128]{5,4,1,3,2,0:T(8,128)(2,1)S(1)}, u32[]{:S(2)}, u32[]{:S(2)}) %all-to-all-start.3) | async-done | bytes 2097184 | tf_op jit(solution)/shard_map/all_to_all | solution.py:69
  148.3 0.9 fusion.43
  149.9 0.9 fusion.13
  (54 shorter events, 8.4 us)
Async XLA Ops:
  0.6 4.7 %copy-start = (bf16[64,128]{1,0:T(8,128)(2,1)S(1)}, bf16[64,128]{1,0:T(8,128)(2,1)}, u32[]{:S(2)}) copy-start(bf16[64,128]{1,0:T(8,128)(2,1)} %param.13) | copy-start | bytes 49156
  2.3 0.6 copy-start.4
  4.2 60.4 %copy-start.1 = (bf16[64,1024]{1,0:T(8,128)(2,1)S(1)}, bf16[64,1024]{1,0:T(8,128)(2,1)}, u32[]{:S(2)}) copy-start(bf16[64,1024]{1,0:T(8,128)(2,1)} %param.11) | copy-start | bytes 393220
  6.7 24.6 %all-to-all-start = ((f32[16,1,72,128]{3,2,1,0:T(8,128)}), f32[16,1,72,128]{3,2,1,0:T(8,128)S(1)}, u32[]{:S(2)}, u32[]{:S(2)}) async-start(f32[16,1,72,128]{3,2,1,0:T(8,128)} %maximum_bitcast_fusion), calls=%async_computation | async-start | bytes 1179648 | tf_op jit(solution)/shard_map/all_to_all | solution.py:101
  60.7 15.1 %all-to-all-start.1 = ((f32[16,1,64,128]{3,2,1,0:T(8,128)}), f32[16,1,64,128]{3,2,1,0:T(8,128)S(1)}, u32[]{:S(2)}, u32[]{:S(2)}) async-start(f32[16,1,64,128]{3,2,1,0:T(8,128)} %fusion.16), calls=%async_computation.1 | async-start | bytes 1048576 | tf_op jit(solution)/shard_map/all_to_all | solution.py:120
  64.7 13.6 %copy-start.3 = (bf16[64,1024]{1,0:T(8,128)(2,1)S(1)}, bf16[64,1024]{1,0:T(8,128)(2,1)}, u32[]{:S(2)}) copy-start(bf16[64,1024]{1,0:T(8,128)(2,1)} %param.12) | copy-start | bytes 393220
  79.3 45.2 %copy-start.2 = (bf16[64,1024]{1,0:T(8,128)(2,1)}, bf16[64,1024]{1,0:T(8,128)(2,1)S(1)}, u32[]{:S(2)}) copy-start(bf16[64,1024]{1,0:T(8,128)(2,1)S(1)} %multiply_convert_fusion) | copy-start | bytes 393220
  92.6 35.6 %copy-start.5 = (bf16[64,512]{1,0:T(8,128)(2,1)S(1)}, bf16[64,512]{1,0:T(8,128)(2,1)}, u32[]{:S(2)}) copy-start(bf16[64,512]{1,0:T(8,128)(2,1)} %param.20) | copy-start | bytes 196612
  124.5 23.3 %all-to-all-start.3 = ((bf16[4,16,2,1,64,128]{5,4,1,3,2,0:T(8,128)(2,1)}), bf16[4,16,2,1,64,128]{5,4,1,3,2,0:T(8,128)(2,1)S(1)}, u32[]{:S(2)}, u32[]{:S(2)}) async-start(bf16[4,16,2,1,64,128]{5,4,1,3,2,0:T(8,128)(2,1)} %broadcast_in_dim.122), calls=%async_computation.3 | async-start | bytes 4194304 | tf_op jit(solution)/shard_map/all_to_all | solution.py:69

commit v13 on v12

--- a/solution.py
+++ b/solution.py
@@ -69,6 +69,16 @@
     return lax.all_to_all(repeated, axis, 0, 0, tiled=True)
 
 
+def gather_earlier(block, axis):
+    count = lax.axis_size(axis)
+    here = lax.axis_index(axis)
+    shifted = [block]
+    for shift in range(1, count):
+        pairs = [(source, source + shift) for source in range(count - shift)]
+        shifted.append(lax.ppermute(block, axis, pairs))
+    return jnp.stack(shifted)
+
+
 def masked_weights(decays, upto):
     count = decays.shape[0]
     earlier = jnp.arange(count)[:, None]
@@ -85,9 +95,15 @@
 
 def entering_top(axis, decay, state):
     rows = state.shape[-2]
-    gathered = lax.all_gather(pack_decay(state, decay), axis)
-    weights = masked_weights(gathered[:, :, rows, 0], lax.axis_index(axis))
-    return jnp.sum(weights[:, :, None, None] * gathered[:, :, :rows], axis=0)
+    shifted = gather_earlier(pack_decay(state, decay), axis)
+    here = lax.axis_index(axis)
+    count = shifted.shape[0]
+    decays = shifted[:, :, rows, 0]
+    present = (jnp.arange(count) >= 1) & (jnp.arange(count) <= here)
+    carried = jnp.where(present[:, None], decays, 1.0)
+    spans = jnp.cumprod(jnp.concatenate([jnp.ones_like(carried[:1]), carried[:-1]]), axis=0)
+    weights = jnp.where(present[:, None], spans, 0.0)
+    return jnp.sum(weights[:, :, None, None] * shifted[:, :, :rows], axis=0)
 
 
 def entering_state(axes, decay, state):

time: 152 us -> 153 us (level)
  the two profiles are of different devices: /device:TPU:32 before, /device:TPU:2 now
where the time goes in v13:
time: 153 us; the launch traced here: 152 us
  blocking collectives  45.1 us (29%)
  starting transfers between devices  39.3 us (26%)
  waiting for transfers between devices  38.9 us (25%)
  local copies, waits for them, and re-layouts  11.6 us (8%)
  other arithmetic  8.44 us (6%)
  matrix products  8.09 us (5%)
    all_gather x1, blocking collectives, per_device(): pair = gather_by_exchange(lax.all_gather(pair, ('zh', 'zl')), 'sx')  33.3 us
    ppermute x3, starting transfers between devices, gather_earlier(): shifted.append(lax.ppermute(block, axis, pairs))  18.6 us
    all_to_all x1, waiting for transfers between devices, gather_by_exchange(): return lax.all_to_all(repeated, axis, 0, 0, tiled=True)  17.4 us
    all_to_all x1, waiting for transfers between devices, entering_state(): received = lax.all_to_all(packed, axis, 0, 0, tiled=True)  14.7 us
    all_to_all x1, blocking collectives, per_device(): exchanged = lax.all_to_all(partials, 'tp', 0, 0, tiled=True)  11.8 us
    all_to_all x1, starting transfers between devices, entering_state(): received = lax.all_to_all(packed, axis, 0, 0, tiled=True)  9.28 us
    all_to_all x1, starting transfers between devices, entering_state(): returned = lax.all_to_all(outgoing, axis, 0, 0, tiled=True)  6.13 us
    all_to_all x1, starting transfers between devices, gather_by_exchange(): return lax.all_to_all(repeated, axis, 0, 0, tiled=True)  5.34 us
  transfers between devices with their start and end apart: 6, of which 5 were waited for; matrix products, arithmetic and copies ran while one was open for 5% of the time, Pallas kernels for 0%

profile of v13, /device:TPU:2, one launch (start us, length us, event | category | flops | bytes accessed | tf_op | source)
XLA Modules:
  0.0 152.4 jit_solution(17414960332296455776)
XLA Ops:
  2.9 1.3 multiply_bitcast_fusion
  4.2 1.1 copy.61
  5.9 0.9 maximum_bitcast_fusion
  6.7 9.3 %all-to-all-start = ((f32[16,1,72,128]{3,2,1,0:T(8,128)}), f32[16,1,72,128]{3,2,1,0:T(8,128)S(1)}, u32[]{:S(2)}, u32[]{:S(2)}) async-start(f32[16,1,72,128]{3,2,1,0:T(8,128)} %maximum_bitcast_fusion), calls=%async_computation | async-start | bytes 1179648 | tf_op jit(solution)/shard_map/all_to_all | solution.py:117
  16.0 14.7 %all-to-all-done = f32[16,1,72,128]{3,2,1,0:T(8,128)S(1)} async-done(((f32[16,1,72,128]{3,2,1,0:T(8,128)}), f32[16,1,72,128]{3,2,1,0:T(8,128)S(1)}, u32[]{:S(2)}, u32[]{:S(2)}) %all-to-all-start) | async-done | bytes 589856 | tf_op jit(solution)/shard_map/all_to_all | solution.py:117
  31.9 1.3 multiply_reduce_fusion
  33.9 13.0 %collective-permute-start.1 = (f32[1,72,128]{2,1,0:T(8,128)S(1)}, f32[1,72,128]{2,1,0:T(8,128)S(1)}, u32[]{:S(2)}, u32[]{:S(2)}) collective-permute-start(f32[1,72,128]{2,1,0:T(8,128)S(1)} %get-tuple-element.5), channel_id=1, source_target_pairs={{0,256},{128,384},{1,257},{129,385},{2,258},{130,386},{3,259},{131... | collective-permute-start | bytes 110600 | tf_op jit(solution)/shard_map/ppermute | solution.py:78
  46.9 4.3 %collective-permute-start = (f32[1,72,128]{2,1,0:T(8,128)S(1)}, f32[1,72,128]{2,1,0:T(8,128)S(1)}, u32[]{:S(2)}, u32[]{:S(2)}) collective-permute-start(f32[1,72,128]{2,1,0:T(8,128)S(1)} %get-tuple-element.5), channel_id=1, source_target_pairs={{0,128},{128,256},{256,384},{1,129},{129,257},{257,385},{2,130},{1... | collective-permute-start | bytes 110600 | tf_op jit(solution)/shard_map/ppermute | solution.py:78
  51.2 1.3 collective-permute-start.2
  52.8 1.4 collective-permute-done.2
  54.7 0.9 fusion.16
  55.6 6.1 %all-to-all-start.1 = ((f32[16,1,64,128]{3,2,1,0:T(8,128)}), f32[16,1,64,128]{3,2,1,0:T(8,128)S(1)}, u32[]{:S(2)}, u32[]{:S(2)}) async-start(f32[16,1,64,128]{3,2,1,0:T(8,128)} %fusion.16), calls=%async_computation.1 | async-start | bytes 1048576 | tf_op jit(solution)/shard_map/all_to_all | solution.py:136
  61.9 2.9 %copy.60 = bf16[1024,1024]{1,0:T(8,128)(2,1)S(1)} copy(bf16[1024,1024]{0,1:T(8,128)(2,1)} %bitcast.104) | data formatting | bytes 4194304 | tf_op jit(solution)/shard_map/dot_general | solution.py:170
  64.9 0.8 fusion.44
  65.7 2.2 %convolution_bitcast_fusion.2 = f32[64,1,16,64]{3,0,2,1:T(8,128)} fusion(bf16[64,16,64]{0,2,1:T(8,128)(2,1)S(1)} %bitcast.107, f32[16,64]{1,0:T(8,128)} %get-tuple-element.7, f32[16,64]{1,0:T(8,128)} %bitcast.118, f32[64,64]{1,0:T(8,128)S(1)} %fusion.44, pred[64,64]{1,0:T(8,128)(4,1)S(1)} %iota_compare_fusion.1), kind=kOutput, calls=%fused_computation.13 | convolution fusion | flops 50593792 | bytes 421888 | tf_op jit(solution)/shard_map/gkts,sgkp->tgkp/dot_general | solution.py:29
  68.6 5.1 %all-to-all-done.1 = f32[16,1,64,128]{3,2,1,0:T(8,128)S(1)} async-done(((f32[16,1,64,128]{3,2,1,0:T(8,128)}), f32[16,1,64,128]{3,2,1,0:T(8,128)S(1)}, u32[]{:S(2)}, u32[]{:S(2)}) %all-to-all-start.1) | async-done | bytes 524320 | tf_op jit(solution)/shard_map/all_to_all | solution.py:136
  73.8 2.0 %fusion.9 = f32[64,1,16,64]{3,0,2,1:T(8,128)S(1)} fusion(f32[64,1,16,64]{3,0,2,1:T(8,128)} %convolution_bitcast_fusion.2, f32[16,1,64,128]{3,2,1,0:T(8,128)S(1)} %all-to-all-done.1, f32[64,1,16,64]{3,2,0,1:T(8,128)S(1)} %reshape.426, f32[16]{0:T(128)} %param.17, f32[64,16]{0,1:T(8,128)S(1)} %exponential_bitcast_fusion, bf16[64,128]{1,0:T(8,128)(2,1)} %param.14), kind=kOutput, calls=%fused_computation.16 | convolution fusion | flops 100925440 | bytes 1331264 | tf_op jit(solution)/shard_map/tgn,gkpn->tgkp/dot_general | solution.py:36
  78.1 11.8 %all_to_all.20 = f32[8,64,128]{2,1,0:T(8,128)S(1)} all-to-all(f32[8,64,128]{2,1,0:T(8,128)S(1)} %convolution_bitcast_fusion.3), channel_id=1, replica_groups=mesh['zh'=4,'zl'=4,'sx'=4,'tp'=8] {'tp'}, dimensions={0} | all-to-all | bytes 524288 | tf_op jit(solution)/shard_map/all_to_all | solution.py:174
  90.6 33.3 %all-gather = bf16[32,1,64,128]{3,2,1,0:T(8,128)(2,1)S(1)} all-gather(bf16[2,1,64,128]{3,2,1,0:T(8,128)(2,1)S(1)} %pad_maximum_fusion.3), channel_id=2, replica_groups=mesh['zh'=4,'zl'=4,'sx'=4,'tp'=8] {'zh','zl'}, dimensions={0}, use_global_device_ids=true | all-gather | bytes 557056 | tf_op jit(solution)/shard_map/all_gather | solution.py:179
  124.0 1.9 %broadcast_in_dim.107 = bf16[4,16,2,1,64,128]{5,4,1,3,2,0:T(8,128)(2,1)} broadcast(bf16[16,2,64,128]{3,2,0,1:T(8,128)(2,1)S(1)} %copy.55), dimensions={1,2,4,5} | broadcast | bytes 2621440 | tf_op jit(solution)/shard_map/broadcast_in_dim | solution.py:68
  125.9 5.3 %all-to-all-start.3 = ((bf16[4,16,2,1,64,128]{5,4,1,3,2,0:T(8,128)(2,1)}), bf16[4,16,2,1,64,128]{5,4,1,3,2,0:T(8,128)(2,1)S(1)}, u32[]{:S(2)}, u32[]{:S(2)}) async-start(bf16[4,16,2,1,64,128]{5,4,1,3,2,0:T(8,128)(2,1)} %broadcast_in_dim.107), calls=%async_computation.3 | async-start | bytes 4194304 | tf_op jit(solution)/shard_map/all_to_all | solution.py:69
  131.3 17.4 %all-to-all-done.3 = bf16[4,16,2,1,64,128]{5,4,1,3,2,0:T(8,128)(2,1)S(1)} async-done(((bf16[4,16,2,1,64,128]{5,4,1,3,2,0:T(8,128)(2,1)}), bf16[4,16,2,1,64,128]{5,4,1,3,2,0:T(8,128)(2,1)S(1)}, u32[]{:S(2)}, u32[]{:S(2)}) %all-to-all-start.3) | async-done | bytes 2097184 | tf_op jit(solution)/shard_map/all_to_all | solution.py:69
  149.2 0.9 fusion.43
  150.7 0.9 fusion.13
  (60 shorter events, 11.2 us)
Async XLA Ops:
  0.6 4.7 %copy-start = (bf16[64,128]{1,0:T(8,128)(2,1)S(1)}, bf16[64,128]{1,0:T(8,128)(2,1)}, u32[]{:S(2)}) copy-start(bf16[64,128]{1,0:T(8,128)(2,1)} %param.13) | copy-start | bytes 49156
  2.3 0.6 copy-start.4
  4.2 57.5 %copy-start.1 = (bf16[64,1024]{1,0:T(8,128)(2,1)S(1)}, bf16[64,1024]{1,0:T(8,128)(2,1)}, u32[]{:S(2)}) copy-start(bf16[64,1024]{1,0:T(8,128)(2,1)} %param.11) | copy-start | bytes 393220
  6.7 24.0 %all-to-all-start = ((f32[16,1,72,128]{3,2,1,0:T(8,128)}), f32[16,1,72,128]{3,2,1,0:T(8,128)S(1)}, u32[]{:S(2)}, u32[]{:S(2)}) async-start(f32[16,1,72,128]{3,2,1,0:T(8,128)} %maximum_bitcast_fusion), calls=%async_computation | async-start | bytes 1179648 | tf_op jit(solution)/shard_map/all_to_all | solution.py:117
  33.9 18.6 %collective-permute-start.1 = (f32[1,72,128]{2,1,0:T(8,128)S(1)}, f32[1,72,128]{2,1,0:T(8,128)S(1)}, u32[]{:S(2)}, u32[]{:S(2)}) collective-permute-start(f32[1,72,128]{2,1,0:T(8,128)S(1)} %get-tuple-element.5), channel_id=1, source_target_pairs={{0,256},{128,384},{1,257},{129,385},{2,258},{130,386},{3,259},{131... | collective-permute-start | bytes 110600 | tf_op jit(solution)/shard_map/ppermute | solution.py:78
  46.9 5.9 %collective-permute-start = (f32[1,72,128]{2,1,0:T(8,128)S(1)}, f32[1,72,128]{2,1,0:T(8,128)S(1)}, u32[]{:S(2)}, u32[]{:S(2)}) collective-permute-start(f32[1,72,128]{2,1,0:T(8,128)S(1)} %get-tuple-element.5), channel_id=1, source_target_pairs={{0,128},{128,256},{256,384},{1,129},{129,257},{257,385},{2,130},{1... | collective-permute-start | bytes 110600 | tf_op jit(solution)/shard_map/ppermute | solution.py:78
  51.2 3.0 %collective-permute-start.2 = (f32[1,72,128]{2,1,0:T(8,128)S(1)}, f32[1,72,128]{2,1,0:T(8,128)S(1)}, u32[]{:S(2)}, u32[]{:S(2)}) collective-permute-start(f32[1,72,128]{2,1,0:T(8,128)S(1)} %get-tuple-element.5), channel_id=1, source_target_pairs={{0,384},{1,385},{2,386},{3,387},{4,388},{5,389},{6,390},{7,391},{8... | collective-permute-start | bytes 110600 | tf_op jit(solution)/shard_map/ppermute | solution.py:78
  55.6 18.2 %all-to-all-start.1 = ((f32[16,1,64,128]{3,2,1,0:T(8,128)}), f32[16,1,64,128]{3,2,1,0:T(8,128)S(1)}, u32[]{:S(2)}, u32[]{:S(2)}) async-start(f32[16,1,64,128]{3,2,1,0:T(8,128)} %fusion.16), calls=%async_computation.1 | async-start | bytes 1048576 | tf_op jit(solution)/shard_map/all_to_all | solution.py:136
  61.9 14.4 %copy-start.3 = (bf16[64,1024]{1,0:T(8,128)(2,1)S(1)}, bf16[64,1024]{1,0:T(8,128)(2,1)}, u32[]{:S(2)}) copy-start(bf16[64,1024]{1,0:T(8,128)(2,1)} %param.12) | copy-start | bytes 393220
  77.3 48.6 %copy-start.2 = (bf16[64,1024]{1,0:T(8,128)(2,1)}, bf16[64,1024]{1,0:T(8,128)(2,1)S(1)}, u32[]{:S(2)}) copy-start(bf16[64,1024]{1,0:T(8,128)(2,1)S(1)} %multiply_convert_fusion) | copy-start | bytes 393220
  90.6 40.7 %copy-start.5 = (bf16[64,512]{1,0:T(8,128)(2,1)S(1)}, bf16[64,512]{1,0:T(8,128)(2,1)}, u32[]{:S(2)}) copy-start(bf16[64,512]{1,0:T(8,128)(2,1)} %param.20) | copy-start | bytes 196612
  125.9 22.9 %all-to-all-start.3 = ((bf16[4,16,2,1,64,128]{5,4,1,3,2,0:T(8,128)(2,1)}), bf16[4,16,2,1,64,128]{5,4,1,3,2,0:T(8,128)(2,1)S(1)}, u32[]{:S(2)}, u32[]{:S(2)}) async-start(bf16[4,16,2,1,64,128]{5,4,1,3,2,0:T(8,128)(2,1)} %broadcast_in_dim.107), calls=%async_computation.3 | async-start | bytes 4194304 | tf_op jit(solution)/shard_map/all_to_all | solution.py:69

commit v14 on v12

--- a/solution.py
+++ b/solution.py
@@ -12,6 +12,7 @@
 HEAD_DIM = 128
 SEQ_AXES = (("zl", "sx"), "zh")
 ROWS = ("zh", "zl", "sx")
+TP = ("ty", "tc")
 
 
 highest = lax.Precision.HIGHEST
@@ -150,13 +151,15 @@
     mamba_out = gated_norm(ssm_out.reshape(tokens_here, -1), gate_z, norm_gain, group_count)
     kv_here = keys.shape[1] // HEAD_DIM
     per_kv = QHEADS // KVHEADS
-    tp_count = lax.axis_size("tp")
+    chips = lax.axis_size("ty")
+    cores = lax.axis_size("tc")
     product = jnp.dot(mamba_out, value_weight, preferred_element_type=jnp.float32)
     partials = jnp.transpose(
-        product.reshape(tokens_here, tp_count, kv_here * HEAD_DIM), (1, 0, 2)
-    )
-    exchanged = lax.all_to_all(partials, "tp", 0, 0, tiled=True)
-    values = jnp.sum(exchanged, axis=0).astype(jnp.bfloat16)
+        product.reshape(tokens_here, chips, cores, kv_here * HEAD_DIM), (2, 1, 0, 3)
+    )
+    on_chip = jnp.sum(lax.all_to_all(partials, "tc", 0, 0, tiled=True), axis=0)
+    values = jnp.sum(lax.all_to_all(on_chip, "ty", 0, 0, tiled=True), axis=0)
+    values = values.astype(jnp.bfloat16)
     values = jnp.transpose(values.reshape(tokens_here, kv_here, HEAD_DIM), (1, 0, 2))
     key_heads = jnp.transpose(keys.reshape(tokens_here, kv_here, HEAD_DIM), (1, 0, 2))
     pair = jnp.stack([key_heads, values])
@@ -186,27 +189,27 @@
 def solution(mesh):
     seq_count = mesh.shape["seq"]
     split = Mesh(
-        mesh.devices.reshape(seq_count // 16, 4, 4, mesh.shape["tp"]),
-        ROWS + ("tp",),
+        mesh.devices.reshape(seq_count // 16, 4, 4, mesh.shape["tp"] // 2, 2),
+        ROWS + TP,
     )
     rows = ROWS
     placed = (
-        P(rows, "tp"),
-        P(rows, "tp"),
-        P(rows, "tp"),
-        P(rows, "tp"),
-        P("tp", rows),
-        P("tp"),
-        P("tp"),
-        P("tp"),
-        P("tp", None),
-        P(rows, "tp"),
-        P(rows, "tp"),
+        P(rows, TP),
+        P(rows, TP),
+        P(rows, TP),
+        P(rows, TP),
+        P(TP, rows),
+        P(TP),
+        P(TP),
+        P(TP),
+        P(TP, None),
+        P(rows, TP),
+        P(rows, TP),
     )
     return jax.shard_map(
         per_device,
         mesh=split,
         in_specs=placed,
-        out_specs=(P(rows, "tp"), P(rows, "tp")),
+        out_specs=(P(rows, TP), P(rows, TP)),
         check_vma=False,
     )

time: 152 us -> 153 us (level)
  blocking collectives: 66.6 us -> 69 us
    all_to_all x1 -> x2, blocking collectives: 11.8 us -> 14.2 us  [the longest x1 10.2 us: per_device(): values = jnp.sum(lax.all_to_all(on_chip, 'ty', 0, 0, tiled=True), axis=0)]
where the time goes in v14:
time: 153 us; the launch traced here: 152 us
  blocking collectives  69 us (45%)
  waiting for transfers between devices  38.5 us (25%)
  starting transfers between devices  16.4 us (11%)
  local copies, waits for them, and re-layouts  11.7 us (8%)
  matrix products  8.08 us (5%)
  other arithmetic  7.51 us (5%)
    all_gather x1, blocking collectives, per_device(): pair = gather_by_exchange(lax.all_gather(pair, ('zh', 'zl')), 'sx')  30 us
    all_gather x1, blocking collectives, entering_top(): gathered = lax.all_gather(pack_decay(state, decay), axis)  24.8 us
    all_to_all x1, waiting for transfers between devices, gather_by_exchange(): return lax.all_to_all(repeated, axis, 0, 0, tiled=True)  18.5 us
    all_to_all x1, waiting for transfers between devices, entering_state(): received = lax.all_to_all(packed, axis, 0, 0, tiled=True)  15.7 us
    all_to_all x1, blocking collectives, per_device(): values = jnp.sum(lax.all_to_all(on_chip, 'ty', 0, 0, tiled=True), axis=0)  10.2 us
    all_to_all x1, starting transfers between devices, entering_state(): received = lax.all_to_all(packed, axis, 0, 0, tiled=True)  8.87 us
    all_to_all x1, waiting for transfers between devices, entering_state(): returned = lax.all_to_all(outgoing, axis, 0, 0, tiled=True)  4.32 us
    all_to_all x1, blocking collectives, per_device(): on_chip = jnp.sum(lax.all_to_all(partials, 'tc', 0, 0, tiled=True), axis=0)  3.94 us
  transfers between devices with their start and end apart: 3, of which 3 were waited for; matrix products, arithmetic and copies ran while one was open for 5% of the time, Pallas kernels for 0%

profile of v14, /device:TPU:32, one launch (start us, length us, event | category | flops | bytes accessed | tf_op | source)
XLA Modules:
  0.0 152.1 jit_solution(7908629390059539578)
XLA Ops:
  1.3 0.8 multiply_bitcast_fusion.1
  2.9 1.3 multiply_bitcast_fusion
  4.2 1.1 copy.65
  5.9 0.9 maximum_bitcast_fusion
  6.7 8.9 %all-to-all-start = ((f32[16,1,72,128]{3,2,1,0:T(8,128)}), f32[16,1,72,128]{3,2,1,0:T(8,128)S(1)}, u32[]{:S(2)}, u32[]{:S(2)}) async-start(f32[16,1,72,128]{3,2,1,0:T(8,128)} %maximum_bitcast_fusion), calls=%async_computation | async-start | bytes 1179648 | tf_op jit(solution)/shard_map/all_to_all | solution.py:102
  15.6 15.7 %all-to-all-done = f32[16,1,72,128]{3,2,1,0:T(8,128)S(1)} async-done(((f32[16,1,72,128]{3,2,1,0:T(8,128)}), f32[16,1,72,128]{3,2,1,0:T(8,128)S(1)}, u32[]{:S(2)}, u32[]{:S(2)}) %all-to-all-start) | async-done | bytes 589856 | tf_op jit(solution)/shard_map/all_to_all | solution.py:102
  32.6 1.3 multiply_reduce_fusion
  34.6 24.8 %all-gather = f32[4,72,128]{2,1,0:T(8,128)S(1)} all-gather(f32[1,72,128]{2,1,0:T(8,128)S(1)} %concatenate.7), channel_id=2, replica_groups=mesh['zh'=4,'zl'=4,'sx'=4,'ty'=4,'tc'=2] {'zh'}, dimensions={0}, use_global_device_ids=true | all-gather | bytes 184320 | tf_op jit(solution)/shard_map/all_gather | solution.py:89
  59.8 0.9 fusion.16
  60.7 3.9 %all-to-all-start.1 = ((f32[16,1,64,128]{3,2,1,0:T(8,128)}), f32[16,1,64,128]{3,2,1,0:T(8,128)S(1)}, u32[]{:S(2)}, u32[]{:S(2)}) async-start(f32[16,1,64,128]{3,2,1,0:T(8,128)} %fusion.16), calls=%async_computation.1 | async-start | bytes 1048576 | tf_op jit(solution)/shard_map/all_to_all | solution.py:121
  64.7 2.9 %copy.64 = bf16[1024,1024]{1,0:T(8,128)(2,1)S(1)} copy(bf16[1024,1024]{0,1:T(8,128)(2,1)} %bitcast.97) | data formatting | bytes 4194304 | tf_op jit(solution)/shard_map/dot_general | solution.py:156
  67.7 0.8 fusion.44
  68.5 2.2 %convolution_bitcast_fusion.2 = f32[64,1,16,64]{3,0,2,1:T(8,128)} fusion(bf16[64,16,64]{0,2,1:T(8,128)(2,1)S(1)} %bitcast.100, f32[16,64]{1,0:T(8,128)} %get-tuple-element.5, f32[16,64]{1,0:T(8,128)} %bitcast.107, f32[64,64]{1,0:T(8,128)S(1)} %fusion.44, pred[64,64]{1,0:T(8,128)(4,1)S(1)} %iota_compare_fusion.1), kind=kOutput, calls=%fused_computation.13 | convolution fusion | flops 50593792 | bytes 421888 | tf_op jit(solution)/shard_map/gkts,sgkp->tgkp/dot_general | solution.py:30
  71.5 4.3 %all-to-all-done.1 = f32[16,1,64,128]{3,2,1,0:T(8,128)S(1)} async-done(((f32[16,1,64,128]{3,2,1,0:T(8,128)}), f32[16,1,64,128]{3,2,1,0:T(8,128)S(1)}, u32[]{:S(2)}, u32[]{:S(2)}) %all-to-all-start.1) | async-done | bytes 524320 | tf_op jit(solution)/shard_map/all_to_all | solution.py:121
  75.8 2.0 %fusion.9 = f32[64,1,16,64]{3,0,2,1:T(8,128)S(1)} fusion(f32[64,1,16,64]{3,0,2,1:T(8,128)} %convolution_bitcast_fusion.2, f32[16,1,64,128]{3,2,1,0:T(8,128)S(1)} %all-to-all-done.1, f32[64,1,16,64]{3,2,0,1:T(8,128)S(1)} %reshape.453, f32[16]{0:T(128)} %param.17, f32[64,16]{0,1:T(8,128)S(1)} %exponential_bitcast_fusion, bf16[64,128]{1,0:T(8,128)(2,1)} %param.14), kind=kOutput, calls=%fused_computation.16 | convolution fusion | flops 100925440 | bytes 1331264 | tf_op jit(solution)/shard_map/tgn,gkpn->tgkp/dot_general | solution.py:37
  78.6 0.8 convolution_bitcast_fusion.3
  79.4 3.9 %all_to_all.25 = f32[2,4,64,128]{3,2,1,0:T(8,128)S(1)} all-to-all(f32[2,4,64,128]{3,2,1,0:T(8,128)S(1)} %copy.57), channel_id=1, replica_groups=mesh['zh'=4,'zl'=4,'sx'=4,'ty'=4,'tc'=2] {'tc'}, dimensions={0} | all-to-all | bytes 524288 | tf_op jit(solution)/shard_map/all_to_all | solution.py:160
  83.4 10.2 %all_to_all.26 = f32[4,64,128]{2,1,0:T(8,128)S(1)} all-to-all(f32[4,64,128]{2,1,0:T(8,128)S(1)} %reduce_sum.57), channel_id=1, replica_groups=mesh['zh'=4,'zl'=4,'sx'=4,'ty'=4,'tc'=2] {'ty'}, dimensions={0} | all-to-all | bytes 262144 | tf_op jit(solution)/shard_map/all_to_all | solution.py:161
  94.4 30.0 %all-gather.1 = bf16[32,1,64,128]{3,2,1,0:T(8,128)(2,1)S(1)} all-gather(bf16[2,1,64,128]{3,2,1,0:T(8,128)(2,1)S(1)} %pad_maximum_fusion), channel_id=3, replica_groups=mesh['zh'=4,'zl'=4,'sx'=4,'ty'=4,'tc'=2] {'zh','zl'}, dimensions={0}, use_global_device_ids=true | all-gather | bytes 557056 | tf_op jit(solution)/shard_map/all_gather | solution.py:166
  124.4 1.9 %broadcast_in_dim.122 = bf16[4,16,2,1,64,128]{5,4,1,3,2,0:T(8,128)(2,1)} broadcast(bf16[16,2,64,128]{3,2,0,1:T(8,128)(2,1)S(1)} %copy.58), dimensions={1,2,4,5} | broadcast | bytes 2621440 | tf_op jit(solution)/shard_map/broadcast_in_dim | solution.py:69
  126.3 3.6 %all-to-all-start.4 = ((bf16[4,16,2,1,64,128]{5,4,1,3,2,0:T(8,128)(2,1)}), bf16[4,16,2,1,64,128]{5,4,1,3,2,0:T(8,128)(2,1)S(1)}, u32[]{:S(2)}, u32[]{:S(2)}) async-start(bf16[4,16,2,1,64,128]{5,4,1,3,2,0:T(8,128)(2,1)} %broadcast_in_dim.122), calls=%async_computation.4 | async-start | bytes 4194304 | tf_op jit(solution)/shard_map/all_to_all | solution.py:70
  130.1 18.5 %all-to-all-done.4 = bf16[4,16,2,1,64,128]{5,4,1,3,2,0:T(8,128)(2,1)S(1)} async-done(((bf16[4,16,2,1,64,128]{5,4,1,3,2,0:T(8,128)(2,1)}), bf16[4,16,2,1,64,128]{5,4,1,3,2,0:T(8,128)(2,1)S(1)}, u32[]{:S(2)}, u32[]{:S(2)}) %all-to-all-start.4) | async-done | bytes 2097184 | tf_op jit(solution)/shard_map/all_to_all | solution.py:70
  148.9 0.9 fusion.43
  150.5 0.9 fusion.13
  (59 shorter events, 8.6 us)
Async XLA Ops:
  0.6 4.7 %copy-start = (bf16[64,128]{1,0:T(8,128)(2,1)S(1)}, bf16[64,128]{1,0:T(8,128)(2,1)}, u32[]{:S(2)}) copy-start(bf16[64,128]{1,0:T(8,128)(2,1)} %param.13) | copy-start | bytes 49156
  2.3 0.6 copy-start.4
  4.2 60.4 %copy-start.1 = (bf16[64,1024]{1,0:T(8,128)(2,1)S(1)}, bf16[64,1024]{1,0:T(8,128)(2,1)}, u32[]{:S(2)}) copy-start(bf16[64,1024]{1,0:T(8,128)(2,1)} %param.11) | copy-start | bytes 393220
  6.7 24.6 %all-to-all-start = ((f32[16,1,72,128]{3,2,1,0:T(8,128)}), f32[16,1,72,128]{3,2,1,0:T(8,128)S(1)}, u32[]{:S(2)}, u32[]{:S(2)}) async-start(f32[16,1,72,128]{3,2,1,0:T(8,128)} %maximum_bitcast_fusion), calls=%async_computation | async-start | bytes 1179648 | tf_op jit(solution)/shard_map/all_to_all | solution.py:102
  60.7 15.1 %all-to-all-start.1 = ((f32[16,1,64,128]{3,2,1,0:T(8,128)}), f32[16,1,64,128]{3,2,1,0:T(8,128)S(1)}, u32[]{:S(2)}, u32[]{:S(2)}) async-start(f32[16,1,64,128]{3,2,1,0:T(8,128)} %fusion.16), calls=%async_computation.1 | async-start | bytes 1048576 | tf_op jit(solution)/shard_map/all_to_all | solution.py:121
  64.7 13.6 %copy-start.3 = (bf16[64,1024]{1,0:T(8,128)(2,1)S(1)}, bf16[64,1024]{1,0:T(8,128)(2,1)}, u32[]{:S(2)}) copy-start(bf16[64,1024]{1,0:T(8,128)(2,1)} %param.12) | copy-start | bytes 393220
  70.8 7.7 %copy-start.6 = (f32[1024]{0:T(1024)S(1)}, f32[1024]{0:T(1024)}, u32[]{:S(2)}) copy-start(f32[1024]{0:T(1024)} %param.18) | copy-start | bytes 12292
  78.6 47.7 %copy-start.2 = (bf16[64,1024]{1,0:T(8,128)(2,1)}, bf16[64,1024]{1,0:T(8,128)(2,1)S(1)}, u32[]{:S(2)}) copy-start(bf16[64,1024]{1,0:T(8,128)(2,1)S(1)} %multiply_convert_fusion) | copy-start | bytes 393220
  94.4 35.6 %copy-start.5 = (bf16[64,512]{1,0:T(8,128)(2,1)S(1)}, bf16[64,512]{1,0:T(8,128)(2,1)}, u32[]{:S(2)}) copy-start(bf16[64,512]{1,0:T(8,128)(2,1)} %param.20) | copy-start | bytes 196612
  126.3 22.2 %all-to-all-start.4 = ((bf16[4,16,2,1,64,128]{5,4,1,3,2,0:T(8,128)(2,1)}), bf16[4,16,2,1,64,128]{5,4,1,3,2,0:T(8,128)(2,1)S(1)}, u32[]{:S(2)}, u32[]{:S(2)}) async-start(bf16[4,16,2,1,64,128]{5,4,1,3,2,0:T(8,128)(2,1)} %broadcast_in_dim.122), calls=%async_computation.4 | async-start | bytes 4194304 | tf_op jit(solution)/shard_map/all_to_all | solution.py:70

commit v15 on v12

--- a/solution.py
+++ b/solution.py
@@ -160,10 +160,13 @@
     values = jnp.transpose(values.reshape(tokens_here, kv_here, HEAD_DIM), (1, 0, 2))
     key_heads = jnp.transpose(keys.reshape(tokens_here, kv_here, HEAD_DIM), (1, 0, 2))
     pair = jnp.stack([key_heads, values])
-    pair = gather_by_exchange(lax.all_gather(pair, ("zh", "zl")), "sx")
-    all_pairs = jnp.transpose(pair, (2, 3, 1, 0, 4, 5)).reshape(2, kv_here, -1, HEAD_DIM)
-    key_portion = all_pairs[0]
-    value_portion = all_pairs[1]
+    pair = lax.all_gather(pair, ("zh", "zl"))
+    key_portion, value_portion = (
+        jnp.transpose(gather_by_exchange(pair[:, part], "sx"), (2, 1, 0, 3, 4)).reshape(
+            kv_here, -1, HEAD_DIM
+        )
+        for part in range(2)
+    )
     my_index = lax.axis_index(ROWS)
     query_block = query_layout(queries, kv_here, per_kv)
     query_pos = row_positions(my_index * tokens_here, tokens_here, per_kv)

time: 152 us -> 156 us (1.026)
  the two profiles are of different devices: /device:TPU:32 before, /device:TPU:2 now
where the time goes in v15:
time: 156 us; the launch traced here: 155 us
  blocking collectives  78.8 us (51%)
  waiting for transfers between devices  24.4 us (16%)
  starting transfers between devices  20.8 us (13%)
  local copies, waits for them, and re-layouts  12.6 us (8%)
  matrix products  10.3 us (7%)
  other arithmetic  7.51 us (5%)
    all_gather x1, blocking collectives, per_device(): pair = lax.all_gather(pair, ('zh', 'zl'))  29.7 us
    all_gather x1, blocking collectives, entering_top(): gathered = lax.all_gather(pack_decay(state, decay), axis)  23.3 us
    all_to_all x1, waiting for transfers between devices, entering_state(): received = lax.all_to_all(packed, axis, 0, 0, tiled=True)  14.7 us
    all_to_all x1, blocking collectives, gather_by_exchange(): return lax.all_to_all(repeated, axis, 0, 0, tiled=True)  14.1 us
    all_to_all x1, blocking collectives, per_device(): exchanged = lax.all_to_all(partials, 'tp', 0, 0, tiled=True)  11.8 us
    all_to_all x1, starting transfers between devices, entering_state(): received = lax.all_to_all(packed, axis, 0, 0, tiled=True)  9.28 us
    all_to_all x1, starting transfers between devices, entering_state(): returned = lax.all_to_all(outgoing, axis, 0, 0, tiled=True)  6.58 us
    all_to_all x1, waiting for transfers between devices, gather_by_exchange(): return lax.all_to_all(repeated, axis, 0, 0, tiled=True)  5.73 us
  transfers between devices with their start and end apart: 3, of which 3 were waited for; matrix products, arithmetic and copies ran while one was open for 6% of the time, Pallas kernels for 0%

profile of v15, /device:TPU:2, one launch (start us, length us, event | category | flops | bytes accessed | tf_op | source)
XLA Modules:
  0.0 155.2 jit_solution(393710209610993864)
XLA Ops:
  1.3 0.8 multiply_bitcast_fusion.1
  2.5 1.3 multiply_bitcast_fusion
  3.8 1.1 copy.64
  5.5 0.9 maximum_bitcast_fusion
  6.3 9.3 %all-to-all-start = ((f32[16,1,72,128]{3,2,1,0:T(8,128)}), f32[16,1,72,128]{3,2,1,0:T(8,128)S(1)}, u32[]{:S(2)}, u32[]{:S(2)}) async-start(f32[16,1,72,128]{3,2,1,0:T(8,128)} %maximum_bitcast_fusion), calls=%async_computation | async-start | bytes 1179648 | tf_op jit(solution)/shard_map/all_to_all | solution.py:101
  15.6 14.7 %all-to-all-done = f32[16,1,72,128]{3,2,1,0:T(8,128)S(1)} async-done(((f32[16,1,72,128]{3,2,1,0:T(8,128)}), f32[16,1,72,128]{3,2,1,0:T(8,128)S(1)}, u32[]{:S(2)}, u32[]{:S(2)}) %all-to-all-start) | async-done | bytes 589856 | tf_op jit(solution)/shard_map/all_to_all | solution.py:101
  30.9 1.3 multiply_reduce_fusion
  33.5 23.3 %all-gather = f32[4,72,128]{2,1,0:T(8,128)S(1)} all-gather(f32[1,72,128]{2,1,0:T(8,128)S(1)} %concatenate.7), channel_id=2, replica_groups=mesh['zh'=4,'zl'=4,'sx'=4,'tp'=8] {'zh'}, dimensions={0}, use_global_device_ids=true | all-gather | bytes 184320 | tf_op jit(solution)/shard_map/all_gather | solution.py:88
  57.1 0.9 fusion.16
  58.0 6.6 %all-to-all-start.1 = ((f32[16,1,64,128]{3,2,1,0:T(8,128)}), f32[16,1,64,128]{3,2,1,0:T(8,128)S(1)}, u32[]{:S(2)}, u32[]{:S(2)}) async-start(f32[16,1,64,128]{3,2,1,0:T(8,128)} %fusion.16), calls=%async_computation.1 | async-start | bytes 1048576 | tf_op jit(solution)/shard_map/all_to_all | solution.py:120
  64.8 2.9 %copy.63 = bf16[1024,1024]{1,0:T(8,128)(2,1)S(1)} copy(bf16[1024,1024]{0,1:T(8,128)(2,1)} %bitcast.99) | data formatting | bytes 4194304 | tf_op jit(solution)/shard_map/dot_general | solution.py:154
  67.7 0.8 fusion.43
  68.5 2.2 %convolution_bitcast_fusion.2 = f32[64,1,16,64]{3,0,2,1:T(8,128)} fusion(bf16[64,16,64]{0,2,1:T(8,128)(2,1)S(1)} %bitcast.102, f32[16,64]{1,0:T(8,128)} %get-tuple-element.5, f32[16,64]{1,0:T(8,128)} %bitcast.109, f32[64,64]{1,0:T(8,128)S(1)} %fusion.43, pred[64,64]{1,0:T(8,128)(4,1)S(1)} %iota_compare_fusion.1), kind=kOutput, calls=%fused_computation.12 | convolution fusion | flops 50593792 | bytes 421888 | tf_op jit(solution)/shard_map/gkts,sgkp->tgkp/dot_general | solution.py:29
  71.5 4.0 %all-to-all-done.1 = f32[16,1,64,128]{3,2,1,0:T(8,128)S(1)} async-done(((f32[16,1,64,128]{3,2,1,0:T(8,128)}), f32[16,1,64,128]{3,2,1,0:T(8,128)S(1)}, u32[]{:S(2)}, u32[]{:S(2)}) %all-to-all-start.1) | async-done | bytes 524320 | tf_op jit(solution)/shard_map/all_to_all | solution.py:120
  75.5 2.0 %fusion.9 = f32[64,1,16,64]{3,0,2,1:T(8,128)S(1)} fusion(f32[64,1,16,64]{3,0,2,1:T(8,128)} %convolution_bitcast_fusion.2, f32[16,1,64,128]{3,2,1,0:T(8,128)S(1)} %all-to-all-done.1, f32[64,1,16,64]{3,2,0,1:T(8,128)S(1)} %reshape.453, f32[16]{0:T(128)} %param.17, f32[64,16]{0,1:T(8,128)S(1)} %exponential_bitcast_fusion, bf16[64,128]{1,0:T(8,128)(2,1)} %param.14), kind=kOutput, calls=%fused_computation.15 | convolution fusion | flops 100925440 | bytes 1331264 | tf_op jit(solution)/shard_map/tgn,gkpn->tgkp/dot_general | solution.py:36
  79.1 11.8 %all_to_all.25 = f32[8,64,128]{2,1,0:T(8,128)S(1)} all-to-all(f32[8,64,128]{2,1,0:T(8,128)S(1)} %convolution_bitcast_fusion.3), channel_id=1, replica_groups=mesh['zh'=4,'zl'=4,'sx'=4,'tp'=8] {'tp'}, dimensions={0} | all-to-all | bytes 524288 | tf_op jit(solution)/shard_map/all_to_all | solution.py:158
  91.7 29.7 %all-gather.1 = bf16[32,1,64,128]{3,2,1,0:T(8,128)(2,1)S(1)} all-gather(bf16[2,1,64,128]{3,2,1,0:T(8,128)(2,1)S(1)} %pad_maximum_fusion), channel_id=3, replica_groups=mesh['zh'=4,'zl'=4,'sx'=4,'tp'=8] {'zh','zl'}, dimensions={0}, use_global_device_ids=true | all-gather | bytes 557056 | tf_op jit(solution)/shard_map/all_gather | solution.py:163
  121.7 14.1 %all_to_all.26 = bf16[4,16,1,64,128]{4,3,1,2,0:T(8,128)(2,1)S(1)} all-to-all(bf16[4,16,1,64,128]{4,3,1,2,0:T(8,128)(2,1)S(1)} %broadcast_in_dim.128), channel_id=1, replica_groups=mesh['zh'=4,'zl'=4,'sx'=4,'tp'=8] {'sx'}, dimensions={0} | all-to-all | bytes 2097152 | tf_op jit(solution)/shard_map/all_to_all | solution.py:69
  135.7 1.2 broadcast_in_dim.131
  137.0 4.9 %all-to-all-start.4 = ((bf16[4,16,1,64,128]{4,3,1,2,0:T(8,128)(2,1)}), bf16[4,16,1,64,128]{4,3,1,2,0:T(8,128)(2,1)S(1)}, u32[]{:S(2)}, u32[]{:S(2)}) async-start(bf16[4,16,1,64,128]{4,3,1,2,0:T(8,128)(2,1)} %broadcast_in_dim.131), calls=%async_computation.4 | async-start | bytes 2097152 | tf_op jit(solution)/shard_map/all_to_all | solution.py:69
  142.1 0.9 fusion.42
  143.1 1.9 %copy-done.1 = f32[256,4096]{0,1:T(8,128)} copy-done((f32[256,4096]{0,1:T(8,128)}, f32[256,4096]{0,1:T(8,128)S(1)}, u32[]{:S(2)}) %copy-start.1) | copy-done | bytes 4194328
  145.6 5.7 %all-to-all-done.4 = bf16[4,16,1,64,128]{4,3,1,2,0:T(8,128)(2,1)S(1)} async-done(((bf16[4,16,1,64,128]{4,3,1,2,0:T(8,128)(2,1)}), bf16[4,16,1,64,128]{4,3,1,2,0:T(8,128)(2,1)S(1)}, u32[]{:S(2)}, u32[]{:S(2)}) %all-to-all-start.4) | async-done | bytes 1048608 | tf_op jit(solution)/shard_map/all_to_all | solution.py:69
  151.4 3.1 %fusion.13 = bf16[256,128]{1,0:T(8,128)(2,1)S(1)} fusion(bf16[4096,128]{1,0:T(8,128)(2,1)S(1)} %bitcast.98, f32[256,4096]{0,1:T(8,128)} %copy-done.1, f32[256]{0:T(256)S(1)} %get-tuple-element.6, f32[256]{0:T(256)S(1)} %fusion.2), kind=kOutput, calls=%fused_computation.18 | convolution fusion | flops 270598144 | bytes 5310464 | tf_op jit(solution)/shard_map/hrc,hcd->hrd/dot_general | solution.py:182
  (60 shorter events, 8.9 us)
Async XLA Ops:
  0.6 4.3 %copy-start = (bf16[64,128]{1,0:T(8,128)(2,1)S(1)}, bf16[64,128]{1,0:T(8,128)(2,1)}, u32[]{:S(2)}) copy-start(bf16[64,128]{1,0:T(8,128)(2,1)} %param.13) | copy-start | bytes 49156
  2.3 1.5 copy-start.5
  3.8 60.8 %copy-start.2 = (bf16[64,1024]{1,0:T(8,128)(2,1)S(1)}, bf16[64,1024]{1,0:T(8,128)(2,1)}, u32[]{:S(2)}) copy-start(bf16[64,1024]{1,0:T(8,128)(2,1)} %param.11) | copy-start | bytes 393220
  6.3 24.0 %all-to-all-start = ((f32[16,1,72,128]{3,2,1,0:T(8,128)}), f32[16,1,72,128]{3,2,1,0:T(8,128)S(1)}, u32[]{:S(2)}, u32[]{:S(2)}) async-start(f32[16,1,72,128]{3,2,1,0:T(8,128)} %maximum_bitcast_fusion), calls=%async_computation | async-start | bytes 1179648 | tf_op jit(solution)/shard_map/all_to_all | solution.py:101
  58.0 17.5 %all-to-all-start.1 = ((f32[16,1,64,128]{3,2,1,0:T(8,128)}), f32[16,1,64,128]{3,2,1,0:T(8,128)S(1)}, u32[]{:S(2)}, u32[]{:S(2)}) async-start(f32[16,1,64,128]{3,2,1,0:T(8,128)} %fusion.16), calls=%async_computation.1 | async-start | bytes 1048576 | tf_op jit(solution)/shard_map/all_to_all | solution.py:120
  64.8 13.3 %copy-start.4 = (bf16[64,1024]{1,0:T(8,128)(2,1)S(1)}, bf16[64,1024]{1,0:T(8,128)(2,1)}, u32[]{:S(2)}) copy-start(bf16[64,1024]{1,0:T(8,128)(2,1)} %param.12) | copy-start | bytes 393220
  70.8 7.5 %copy-start.7 = (f32[1024]{0:T(1024)S(1)}, f32[1024]{0:T(1024)}, u32[]{:S(2)}) copy-start(f32[1024]{0:T(1024)} %param.18) | copy-start | bytes 12292
  78.3 58.6 %copy-start.3 = (bf16[64,1024]{1,0:T(8,128)(2,1)}, bf16[64,1024]{1,0:T(8,128)(2,1)S(1)}, u32[]{:S(2)}) copy-start(bf16[64,1024]{1,0:T(8,128)(2,1)S(1)} %multiply_convert_fusion) | copy-start | bytes 393220
  91.7 50.3 %copy-start.6 = (bf16[64,512]{1,0:T(8,128)(2,1)S(1)}, bf16[64,512]{1,0:T(8,128)(2,1)}, u32[]{:S(2)}) copy-start(bf16[64,512]{1,0:T(8,128)(2,1)} %param.20) | copy-start | bytes 196612
  137.0 14.4 %all-to-all-start.4 = ((bf16[4,16,1,64,128]{4,3,1,2,0:T(8,128)(2,1)}), bf16[4,16,1,64,128]{4,3,1,2,0:T(8,128)(2,1)S(1)}, u32[]{:S(2)}, u32[]{:S(2)}) async-start(bf16[4,16,1,64,128]{4,3,1,2,0:T(8,128)(2,1)} %broadcast_in_dim.131), calls=%async_computation.4 | async-start | bytes 2097152 | tf_op jit(solution)/shard_map/all_to_all | solution.py:69
  143.1 1.9 %copy-start.1 = (f32[256,4096]{0,1:T(8,128)}, f32[256,4096]{0,1:T(8,128)S(1)}, u32[]{:S(2)}) copy-start(f32[256,4096]{0,1:T(8,128)S(1)} %get-tuple-element.7) | copy-start | bytes 12582916
